TPU v7x, 512 devices: a whole 4x8x8 slice. The times are simulated.
512 devices in a mesh: island: 16 (over z, x_hi), fsdp: 32 (over y, x_lo, core).
Axes of the slice: x: 4 (x_hi: 2, x_lo: 2; x = x_hi * 2 + x_lo), y: 8, z: 8, core: 2. Of those that a mesh axis runs over, the one named last changes fastest.
Arguments:
- block_input: bfloat16 [65536, 8192], P(('island', 'fsdp')), may hold values from -170 to 170
- lang_ids: int32 [65536], P(('island', 'fsdp')), may hold values from 0 to 15
- queries: bfloat16 [65536, 4096], P(('island', 'fsdp')), may hold values from -52 to 52
- saved_keys: bfloat16 [65536, 512], P(('island', 'fsdp')), may hold values from -4 to 4
- out_grad: bfloat16 [65536, 4096], P(('island', 'fsdp')), may hold values from -70 to 70
- local_wv: bfloat16 [16, 8192, 512], P('island', 'fsdp'), may hold values from -8 to 8
- local_gain: bfloat16 [16, 16, 8192], P('island'), may hold values from -3 to 5
- outer_wv: float32 [8192, 512], P('fsdp', 'island'), may hold values from -4 to 4
- wv_momentum: float32 [8192, 512], P('fsdp', 'island'), may hold values from -1.8 to 1.8
- outer_gain: float32 [16, 8192], P('island', 'fsdp'), may hold values from 0.5 to 1.5
- gain_momentum: float32 [16, 8192], P('island', 'fsdp'), may hold values from -1.8 to 1.8
Outputs:
- new_outer_wv: float32 [8192, 512], P('fsdp', 'island')
- new_wv_momentum: float32 [8192, 512], P('fsdp', 'island')
- new_outer_gain: float32 [16, 8192], P('island', 'fsdp')
- new_gain_momentum: float32 [16, 8192], P('island', 'fsdp')
All inputs are finite; a program needn't handle non-finite values.
Results may differ from a plain program's by a relative error of at most 0.00045.
Values may be sent and summed in bfloat16 or wider, within the bound.
No kernel may reach another device: no remote copies, remote signals or barrier semaphores. Data moves between devices by JAX's collectives and lax.ppermute only.
A program may use at most 64 MiB of HBM per device.

v0:
```python
import jax
import jax.numpy as jnp
from jax import lax
from jax.sharding import PartitionSpec as P

HEADS = 32
KV_HEADS = 4
HEAD_DIM = 128


EPSILON = 1e-05
MOMENTUM = 0.9
OUTER_RATE = 0.7
CLIP_SHARE = 0.25


def normalize(input_rows):
    widened = input_rows.astype(jnp.float32)
    average = jnp.mean(widened, axis=-1, keepdims=True)
    centered = widened - average
    variance = jnp.mean(centered * centered, axis=-1, keepdims=True)
    return centered * lax.rsqrt(variance + EPSILON)


def value_grad(query_rows, key_block, grad_rows):
    length = query_rows.shape[0]
    group = HEADS // KV_HEADS
    query_four = query_rows.reshape(length, KV_HEADS, group, HEAD_DIM)
    key_three = key_block.reshape(length, KV_HEADS, HEAD_DIM)
    scores = jnp.einsum(
        "tkgd,skd->kgts", query_four, key_three, preferred_element_type=jnp.float32
    ) * HEAD_DIM ** (-0.5)
    position = jnp.arange(length, dtype=jnp.int32)
    causal = position[:, None] >= position[None, :]
    scores = jnp.where(causal, scores, -jnp.inf)
    row_top = jnp.max(scores, axis=-1, keepdims=True)
    exponent = jnp.exp(scores - row_top)
    weights_bf = (exponent / jnp.sum(exponent, axis=-1, keepdims=True)).astype(jnp.bfloat16)
    grad_four = grad_rows.reshape(length, KV_HEADS, group, HEAD_DIM)
    values = jnp.einsum("kgts,tkgd->skd", weights_bf, grad_four, preferred_element_type=jnp.float32)
    return values.reshape(length, KV_HEADS * HEAD_DIM).astype(jnp.bfloat16)


def body(
    block_input,
    lang_ids,
    queries,
    saved_keys,
    out_grad,
    local_wv,
    local_gain,
    outer_wv,
    wv_momentum,
    outer_gain,
    gain_momentum,
):
    width = block_input.shape[1]
    fsdp_count = lax.axis_size("fsdp")
    island_count = lax.axis_size("island")
    col_block = width // fsdp_count
    kv_width = local_wv.shape[2]
    lang_count = local_gain.shape[1]
    weight_scale = width ** (-0.5)
    col_begin = lax.axis_index("fsdp") * col_block
    standard = normalize(block_input)
    lang_table = lang_ids[None, :] == jnp.arange(lang_count, dtype=jnp.int32)[:, None]
    gain_rows = jnp.dot(
        lang_table.astype(jnp.bfloat16).T, local_gain[0], preferred_element_type=jnp.float32
    )
    normed = (standard * gain_rows).astype(jnp.bfloat16)
    values_grad = value_grad(queries, saved_keys, out_grad)
    weight_rows = local_wv[0]
    col_normed = lax.all_to_all(normed, "fsdp", split_axis=1, concat_axis=0, tiled=True)
    input_grad = (
        jnp.dot(
            values_grad,
            lax.all_gather(weight_rows, "fsdp", axis=0, tiled=True).T,
            preferred_element_type=jnp.float32,
        )
        * weight_scale
    )
    gain_part = jnp.dot(
        lang_table.astype(jnp.float32), standard * input_grad, precision=lax.Precision.HIGHEST
    )
    gain_grad = lax.psum(gain_part, "fsdp")
    wv_grad = (
        jnp.dot(
            col_normed.T,
            lax.all_gather(values_grad, "fsdp", axis=0, tiled=True),
            preferred_element_type=jnp.float32,
        )
        * weight_scale
    )
    wv_square = jnp.sum(wv_grad * wv_grad)
    weight_square = lax.psum(wv_square, "fsdp")
    gain_square = jnp.sum(gain_grad * gain_grad)
    own_grad = lax.dynamic_slice_in_dim(gain_grad, col_begin, col_block, 1)
    wv_clip = jnp.minimum(1.0, CLIP_SHARE * (width * kv_width) ** 0.5 / jnp.sqrt(weight_square))
    gain_clip = jnp.minimum(1.0, CLIP_SHARE * (lang_count * width) ** 0.5 / jnp.sqrt(gain_square))
    new_wv = weight_rows.astype(jnp.float32) - wv_clip * wv_grad
    own_gain = lax.dynamic_slice_in_dim(local_gain[0], col_begin, col_block, 1).astype(jnp.float32)
    new_gain = own_gain - gain_clip * own_grad
    wv_share = kv_width // island_count
    gain_share = lang_count // island_count
    total_wv, total_gain = lax.psum((new_wv, new_gain), "island")
    island_at = lax.axis_index("island")
    total_wv = lax.dynamic_slice_in_dim(total_wv, island_at * wv_share, wv_share, 1)
    total_gain = lax.dynamic_slice_in_dim(total_gain, island_at * gain_share, gain_share, 0)
    delta_wv = outer_wv - total_wv / island_count
    momentum_wv = MOMENTUM * wv_momentum + delta_wv
    result_wv = outer_wv - OUTER_RATE * (delta_wv + MOMENTUM * momentum_wv)
    delta_gain = outer_gain - total_gain / island_count
    momentum_gain = MOMENTUM * gain_momentum + delta_gain
    result_gain = outer_gain - OUTER_RATE * (delta_gain + MOMENTUM * momentum_gain)
    return (result_wv, momentum_wv, result_gain, momentum_gain)


def solution(mesh):
    in_specs = (
        P(("island", "fsdp"), None),
        P(("island", "fsdp")),
        P(("island", "fsdp"), None),
        P(("island", "fsdp"), None),
        P(("island", "fsdp"), None),
        P("island", "fsdp", None),
        P("island", None, None),
        P("fsdp", "island"),
        P("fsdp", "island"),
        P("island", "fsdp"),
        P("island", "fsdp"),
    )
    out_specs = (P("fsdp", "island"), P("fsdp", "island"), P("island", "fsdp"), P("island", "fsdp"))
    return jax.shard_map(body, mesh=mesh, in_specs=in_specs, out_specs=out_specs, check_vma=False)
```

profile of v0, /device:TPU:1, one launch (start us, length us, event | category | flops | bytes accessed | tf_op | source)
XLA Modules:
  0.0 677.7 jit_solution(18145128111917954765)
XLA Ops:
  7.2 0.0 all-gather.4.cloned.1.call-start
  7.2 1.4 copy.48
  8.7 0.9 reshape.40
  9.6 1.6 copy.46
  11.3 2.3 fusion.33
  13.6 2.8 fusion.8
  16.4 0.0 all-gather.6.cloned.1.call-start
  16.5 0.7 all-gather.6.cloned.1.call-update
  17.2 0.4 convert_reduce_fusion
  17.5 0.7 fusion.6
  18.3 0.8 fusion.2
  19.1 1.6 copy.70
  20.7 11.2 %all-to-all-start = ((bf16[128,32,256]{2,0,1:T(8,128)(2,1)}), bf16[128,32,256]{2,0,1:T(8,128)(2,1)}, u32[]{:S(2)}, u32[]{:S(2)}) async-start(bf16[128,32,256]{2,0,1:T(8,128)(2,1)} %bitcast.44), calls=%async_computation | async-start | bytes 4194304 | tf_op jit(solution)/shard_map/all_to_all | solution.py:73
  31.9 0.0 all-reduce.3.cloned.1.call-start
  31.9 0.1 copy.34
  32.1 61.0 %all-to-all-done = bf16[128,32,256]{2,0,1:T(8,128)(2,1)} async-done(((bf16[128,32,256]{2,0,1:T(8,128)(2,1)}), bf16[128,32,256]{2,0,1:T(8,128)(2,1)}, u32[]{:S(2)}, u32[]{:S(2)}) %all-to-all-start) | async-done | bytes 2097184 | tf_op jit(solution)/shard_map/all_to_all | solution.py:73
  93.0 31.1 %all-gather.4.cloned.1.call-done = bf16[4096,512]{0,1:T(8,128)(2,1)} async-done(((bf16[128,512]{0,1:T(8,128)(2,1)}), bf16[4096,512]{0,1:T(8,128)(2,1)}) %all-gather.4.cloned.1.call-update) | async-done | bytes 4194320 | tf_op jit(solution)/shard_map/all_gather | solution.py:89
  124.2 4.8 multiply_reduce_fusion.1
  129.0 54.4 %psum.28 = f32[]{:T(128)} all-reduce(f32[]{:T(128)} %get-tuple-element.18), channel_id=1, replica_groups=mesh['island'=16,'fsdp'=32] {'fsdp'}, use_global_device_ids=true, to_apply=%region_5.6 | all-reduce | flops 1 | bytes 8 | tf_op jit(solution)/shard_map/psum | solution.py:95
  183.4 0.2 copy.40
  184.3 0.9 convert_subtract_fusion.1
  185.2 0.0 all-reduce.5.cloned.1.call-start
  185.3 17.4 %all-gather.6.cloned.1.call-done = bf16[1,8192,512]{2,1,0:T(8,128)(2,1)} async-done(((bf16[1,256,512]{2,1,0:T(8,128)(2,1)}), bf16[1,8192,512]{2,1,0:T(8,128)(2,1)}) %all-gather.6.cloned.1.call-update) | async-done | bytes 8388624 | tf_op jit(solution)/shard_map/all_gather | solution.py:77
  202.6 6.6 fusion.1
  209.2 2.3 fusion.24
  211.6 148.1 %all-reduce.3.cloned.1.call-done = f32[256,512]{0,1:T(8,128)} async-done(((f32[256,512]{0,1:T(8,128)}), f32[256,512]{0,1:T(8,128)}) %all-reduce.3.cloned.1.call-update) | async-done | bytes 524304 | tf_op jit(solution)/shard_map/psum | solution.py:105
  359.7 1.4 multiply_subtract_fusion
  361.1 242.6 %all-reduce.5.cloned.1.call-done = f32[16,8192]{1,0:T(8,128)} async-done(((f32[16,8192]{1,0:T(8,128)}), f32[16,8192]{1,0:T(8,128)}) %all-reduce.5.cloned.1.call-update) | async-done | bytes 524304 | tf_op jit(solution)/shard_map/psum | solution.py:85
  603.7 1.8 multiply_reduce_fusion
  606.2 0.7 convert_subtract_fusion.2
  606.9 63.6 %psum.31 = f32[16,256]{1,0:T(8,128)S(1)} all-reduce(f32[16,256]{1,0:T(8,128)S(1)} %convert_subtract_fusion.2), channel_id=1, replica_groups=mesh['island'=16,'fsdp'=32] {'island'}, use_global_device_ids=true, to_apply=%region_9.10 | all-reduce | flops 4096 | bytes 32768 | tf_op jit(solution)/shard_map/psum | solution.py:105
  670.5 0.6 multiply_subtract_fusion.2
  (24 shorter events, 0.1 us)
Async XLA Ops:
  7.2 117.0 %all-gather.4.cloned.1.call-start = ((), (), s32[]{:S(2)}) async-start(), calls=%async_computation.1 | async-start | bytes 4325376 | tf_op jit(solution)/shard_map/all_gather | solution.py:89
  13.6 3.6 copy-start
  16.4 1.9 copy-start.7
  16.4 1.9 copy-start.8
  16.4 186.2 %all-gather.6.cloned.1.call-start = ((), (), s32[]{:S(2)}) async-start(), calls=%async_computation.4 | async-start | bytes 8650752 | tf_op jit(solution)/shard_map/all_gather | solution.py:77
  19.1 12.8 %copy-start.1 = (bf16[1,256,512]{2,1,0:T(8,128)(2,1)S(1)}, bf16[1,256,512]{2,1,0:T(8,128)(2,1)}, u32[]{:S(2)}) copy-start(bf16[1,256,512]{2,1,0:T(8,128)(2,1)} %param.16) | copy-start | bytes 786436
  20.7 72.3 %all-to-all-start = ((bf16[128,32,256]{2,0,1:T(8,128)(2,1)}), bf16[128,32,256]{2,0,1:T(8,128)(2,1)}, u32[]{:S(2)}, u32[]{:S(2)}) async-start(bf16[128,32,256]{2,0,1:T(8,128)(2,1)} %bitcast.44), calls=%async_computation | async-start | bytes 4194304 | tf_op jit(solution)/shard_map/all_to_all | solution.py:73
  31.9 327.8 %all-reduce.3.cloned.1.call-start = ((), (), s32[]{:S(2)}) async-start(), calls=%async_computation.2 | async-start | bytes 1048576 | tf_op jit(solution)/shard_map/psum | solution.py:105
  124.2 78.4 %copy-start.2 = (bf16[4,128,128]{1,2,0:T(8,128)(2,1)S(1)}, bf16[4,128,128]{1,2,0:T(8,128)(2,1)}, u32[]{:S(2)}) copy-start(bf16[4,128,128]{1,2,0:T(8,128)(2,1)} %fusion.8) | copy-start | bytes 393220
  185.2 418.5 %all-reduce.5.cloned.1.call-start = ((), (), s32[]{:S(2)}) async-start(), calls=%async_computation.3 | async-start | bytes 1048576 | tf_op jit(solution)/shard_map/psum | solution.py:85
  209.2 150.5 %copy-start.3 = (f32[256,32]{0,1:T(8,128)S(1)}, f32[256,32]{0,1:T(8,128)}, u32[]{:S(2)}) copy-start(f32[256,32]{0,1:T(8,128)} %param.18) | copy-start | bytes 98308
  209.2 150.5 %copy-start.4 = (f32[256,32]{0,1:T(8,128)S(1)}, f32[256,32]{0,1:T(8,128)}, u32[]{:S(2)}) copy-start(f32[256,32]{0,1:T(8,128)} %param.19) | copy-start | bytes 98308
  209.2 461.3 %copy-start.5 = (f32[1,256]{1,0:T(1,128)S(1)}, f32[1,256]{1,0:T(1,128)}, u32[]{:S(2)}) copy-start(f32[1,256]{1,0:T(1,128)} %param.20) | copy-start | bytes 3076
  209.2 461.3 %copy-start.6 = (f32[1,256]{1,0:T(1,128)S(1)}, f32[1,256]{1,0:T(1,128)}, u32[]{:S(2)}) copy-start(f32[1,256]{1,0:T(1,128)} %param.21) | copy-start | bytes 3076
Sparse Core Ops, SparseCore 0:
  16.5 107.6 all-gather.3
  126.3 76.2 all-gather.5
  205.5 154.1 all-reduce.2
  362.5 241.2 all-reduce.4
where the time goes:
time: 691 us; the launch traced here: 678 us
  waiting for transfers between devices  501 us (73%)
  blocking collectives  118 us (17%)
  matrix products  19.6 us (3%)
  between operations  15.3 us (2%)
  starting transfers between devices  11.3 us (2%)
    psum x1, waiting for transfers between devices, body(): gain_grad = lax.psum(gain_part, 'fsdp')  243 us
    psum x1, waiting for transfers between devices, body(): total_wv, total_gain = lax.psum((new_wv, new_gain), 'island')  148 us
    psum x1, blocking collectives, body(): total_wv, total_gain = lax.psum((new_wv, new_gain), 'island')  63.6 us
    all_to_all x1, waiting for transfers between devices, body(): lax.all_to_all(normed, 'fsdp', split_axis=1, concat_axis=0, tiled=True)  61 us
    psum x1, blocking collectives, body(): weight_square = lax.psum(wv_square, 'fsdp')  54.4 us
    all_gather x1, waiting for transfers between devices, body(): lax.all_gather(values_grad, 'fsdp', axis=0, tiled=True)  31.1 us
    all_gather x1, waiting for transfers between devices, body(): lax.all_gather(weight_rows, 'fsdp', axis=0, tiled=True)  17.4 us
  transfers between devices with their start and end apart: 5, of which 5 were waited for; matrix products, arithmetic and copies ran while one was open for 3% of the time, Pallas kernels for 0%

commit v1 on v0

--- a/solution.py
+++ b/solution.py
@@ -14,12 +14,12 @@
 CLIP_SHARE = 0.25
 
 
-def normalize(input_rows):
+def row_stats(input_rows):
     widened = input_rows.astype(jnp.float32)
-    average = jnp.mean(widened, axis=-1, keepdims=True)
-    centered = widened - average
-    variance = jnp.mean(centered * centered, axis=-1, keepdims=True)
-    return centered * lax.rsqrt(variance + EPSILON)
+    average = jnp.mean(widened, axis=-1)
+    centered = widened - average[:, None]
+    variance = jnp.mean(centered * centered, axis=-1)
+    return average, lax.rsqrt(variance + EPSILON)
 
 
 def value_grad(query_rows, key_block, grad_rows):
@@ -62,50 +62,47 @@
     lang_count = local_gain.shape[1]
     weight_scale = width ** (-0.5)
     col_begin = lax.axis_index("fsdp") * col_block
-    standard = normalize(block_input)
-    lang_table = lang_ids[None, :] == jnp.arange(lang_count, dtype=jnp.int32)[:, None]
+
+    average, inv_std = row_stats(block_input)
+    stats = jnp.stack([average, inv_std, lang_ids.astype(jnp.float32)])
+    all_stats = lax.all_gather(stats, "fsdp", axis=1, tiled=True)
+    col_input = lax.all_to_all(block_input, "fsdp", split_axis=1, concat_axis=0, tiled=True)
+
+    values_grad = value_grad(queries, saved_keys, out_grad)
+    all_values = lax.all_gather(values_grad, "fsdp", axis=0, tiled=True)
+
+    standard = (col_input.astype(jnp.float32) - all_stats[0][:, None]) * all_stats[1][:, None]
+    all_lang = all_stats[2].astype(jnp.int32)
+    lang_table = all_lang[None, :] == jnp.arange(lang_count, dtype=jnp.int32)[:, None]
+    own_gain = lax.dynamic_slice_in_dim(local_gain[0], col_begin, col_block, 1)
     gain_rows = jnp.dot(
-        lang_table.astype(jnp.bfloat16).T, local_gain[0], preferred_element_type=jnp.float32
+        lang_table.astype(jnp.bfloat16).T, own_gain, preferred_element_type=jnp.float32
     )
     normed = (standard * gain_rows).astype(jnp.bfloat16)
-    values_grad = value_grad(queries, saved_keys, out_grad)
     weight_rows = local_wv[0]
-    col_normed = lax.all_to_all(normed, "fsdp", split_axis=1, concat_axis=0, tiled=True)
     input_grad = (
-        jnp.dot(
-            values_grad,
-            lax.all_gather(weight_rows, "fsdp", axis=0, tiled=True).T,
-            preferred_element_type=jnp.float32,
-        )
-        * weight_scale
+        jnp.dot(all_values, weight_rows.T, preferred_element_type=jnp.float32) * weight_scale
     )
-    gain_part = jnp.dot(
+    gain_grad = jnp.dot(
         lang_table.astype(jnp.float32), standard * input_grad, precision=lax.Precision.HIGHEST
     )
-    gain_grad = lax.psum(gain_part, "fsdp")
-    wv_grad = (
-        jnp.dot(
-            col_normed.T,
-            lax.all_gather(values_grad, "fsdp", axis=0, tiled=True),
-            preferred_element_type=jnp.float32,
-        )
-        * weight_scale
-    )
-    wv_square = jnp.sum(wv_grad * wv_grad)
-    weight_square = lax.psum(wv_square, "fsdp")
-    gain_square = jnp.sum(gain_grad * gain_grad)
-    own_grad = lax.dynamic_slice_in_dim(gain_grad, col_begin, col_block, 1)
-    wv_clip = jnp.minimum(1.0, CLIP_SHARE * (width * kv_width) ** 0.5 / jnp.sqrt(weight_square))
-    gain_clip = jnp.minimum(1.0, CLIP_SHARE * (lang_count * width) ** 0.5 / jnp.sqrt(gain_square))
+    wv_grad = jnp.dot(normed.T, all_values, preferred_element_type=jnp.float32) * weight_scale
+    squares = lax.psum(jnp.stack([jnp.sum(wv_grad * wv_grad), jnp.sum(gain_grad * gain_grad)]), "fsdp")
+    wv_clip = jnp.minimum(1.0, CLIP_SHARE * (width * kv_width) ** 0.5 / jnp.sqrt(squares[0]))
+    gain_clip = jnp.minimum(1.0, CLIP_SHARE * (lang_count * width) ** 0.5 / jnp.sqrt(squares[1]))
     new_wv = weight_rows.astype(jnp.float32) - wv_clip * wv_grad
-    own_gain = lax.dynamic_slice_in_dim(local_gain[0], col_begin, col_block, 1).astype(jnp.float32)
-    new_gain = own_gain - gain_clip * own_grad
+    new_gain = own_gain.astype(jnp.float32) - gain_clip * gain_grad
+
     wv_share = kv_width // island_count
     gain_share = lang_count // island_count
-    total_wv, total_gain = lax.psum((new_wv, new_gain), "island")
-    island_at = lax.axis_index("island")
-    total_wv = lax.dynamic_slice_in_dim(total_wv, island_at * wv_share, wv_share, 1)
-    total_gain = lax.dynamic_slice_in_dim(total_gain, island_at * gain_share, gain_share, 0)
+    wv_part = new_wv.reshape(col_block, island_count, wv_share).transpose(1, 0, 2)
+    wv_part = wv_part.reshape(island_count, col_block * wv_share)
+    gain_part = new_gain.reshape(island_count, gain_share * col_block)
+    packed = jnp.concatenate([wv_part, gain_part], axis=1)
+    total = lax.psum_scatter(packed, "island", scatter_dimension=0, tiled=True)
+    total_wv = total[0, : col_block * wv_share].reshape(col_block, wv_share)
+    total_gain = total[0, col_block * wv_share :].reshape(gain_share, col_block)
+
     delta_wv = outer_wv - total_wv / island_count
     momentum_wv = MOMENTUM * wv_momentum + delta_wv
     result_wv = outer_wv - OUTER_RATE * (delta_wv + MOMENTUM * momentum_wv)

time: 691 us -> 381 us (0.55)
  the two profiles are of different devices: /device:TPU:1 before, /device:TPU:8 now
where the time goes in v1:
time: 381 us; the launch traced here: 380 us
  waiting for transfers between devices  175 us (46%)
  blocking collectives  129 us (34%)
  matrix products  18 us (5%)
  other arithmetic  16.7 us (4%)
  local copies, waits for them, and re-layouts  15.9 us (4%)
  between operations  15.6 us (4%)
  starting transfers between devices  10.4 us (3%)
    unnamed x3, waiting for transfers between devices  175 us
    all_gather x1, blocking collectives, body(): all_stats = lax.all_gather(stats, 'fsdp', axis=1, tiled=True)  79.9 us
    psum x1, blocking collectives, body(): lax.psum(jnp.stack([jnp.sum(wv_grad * wv_grad), jnp.sum(gain_grad * gain_...  48.9 us
    all_to_all x1, starting transfers between devices, body(): lax.all_to_all(block_input, 'fsdp', split_axis=1, concat_axis=0, tiled=True)  10.3 us
  transfers between devices with their start and end apart: 3, of which 1 were waited for; matrix products, arithmetic and copies ran while one was open for 5% of the time, Pallas kernels for 0%

profile of v1, /device:TPU:8, one launch (start us, length us, event | category | flops | bytes accessed | tf_op | source)
XLA Modules:
  0.0 380.3 jit_solution(11737211862245932639)
XLA Ops:
  7.2 1.4 copy.73
  8.7 0.9 reshape.79
  9.6 1.6 copy.72
  11.3 2.3 fusion.44
  13.5 2.8 fusion.8
  16.4 2.5 copy.58
  18.9 10.3 %all-to-all-start = ((bf16[128,32,256]{0,2,1:T(8,128)(2,1)}), bf16[128,32,256]{0,2,1:T(8,128)(2,1)}, u32[]{:S(2)}, u32[]{:S(2)}) async-start(bf16[128,32,256]{0,2,1:T(8,128)(2,1)} %bitcast.59), calls=%async_computation | async-start | bytes 4194304 | tf_op jit(solution)/shard_map/all_to_all | solution.py:69
  29.3 0.4 convert_reduce_fusion
  29.6 0.7 fusion.4
  30.4 79.9 %all_gather.6 = f32[3,4096]{1,0:T(4,128)S(1)} all-gather(f32[3,128]{1,0:T(4,128)S(1)} %pad_maximum_fusion.1), channel_id=1, replica_groups=mesh['island'=16,'fsdp'=32] {'fsdp'}, dimensions={1}, use_global_device_ids=true | all-gather | bytes 50688 | tf_op jit(solution)/shard_map/all_gather | solution.py:68
  110.3 4.1 %convert_bitcast_fusion = f32[32,128,256]{1,2,0:T(8,128)} fusion(bf16[128,32,256]{0,2,1:T(8,128)(2,1)} %all-to-all-done), kind=kLoop, calls=%fused_computation.11 | loop fusion | flops 1048576 | bytes 6291456 | tf_op jit(solution)/shard_map/convert_element_type | solution.py:74
  114.4 5.6 %copy.59 = f32[32,128,256]{2,1,0:T(8,128)} copy(f32[32,128,256]{1,2,0:T(8,128)} %convert_bitcast_fusion) | data formatting | bytes 8388608 | tf_op jit(solution)/shard_map/convert_element_type | solution.py:74
  120.0 4.2 %fusion.5 = f32[4096,256]{1,0:T(8,128)} fusion(f32[32,128,256]{2,1,0:T(8,128)} %copy.59, f32[4096]{0:T(1024)S(1)} %bitcast.68, f32[4096]{0:T(1024)S(1)} %bitcast.69), kind=kLoop, calls=%fused_computation.10 | loop fusion | flops 2097152 | bytes 8421376 | tf_op jit(solution)/shard_map/mul | solution.py:74
  124.2 4.8 %fusion.1 = f32[4096,256]{1,0:T(8,128)S(1)} fusion(f32[4096,256]{1,0:T(8,128)} %fusion.5, bf16[4096,512]{0,1:T(8,128)(2,1)} %all-gather.2.cloned.1.call-done, bf16[1,256,512]{2,1,0:T(8,128)(2,1)S(1)} %copy-done.1), kind=kOutput, calls=%fused_computation.2 | convolution fusion | flops 1075838976 | bytes 12845056 | tf_op jit(solution)/shard_map/dot_general | solution.py:84
  129.0 2.1 multiply_reduce_fusion.1
  131.1 6.0 %multiply_reduce_fusion = (f32[]{:T(128)}, f32[256,512]{1,0:T(8,128)S(1)}) fusion(bf16[4096,512]{0,1:T(8,128)(2,1)} %all-gather.2.cloned.1.call-done, f32[4096,256]{1,0:T(8,128)} %fusion.5, s32[4096]{0:T(1024)S(1)} %bitcast.65, bf16[1,16,8192]{2,1,0:T(8,128)(2,1)} %param.17, s32[]{:T(128)S(6)} %select_n.7), kind=kOutput, calls=%fused_computation.26 | convolution fusion | flops 1109852160 | bytes 8937480 | tf_op jit(solution)/shard_map/dot_general | solution.py:89
  137.0 1.4 pad_maximum_fusion.2
  138.4 48.9 %psum.7 = f32[2]{0:T(128)S(1)} all-reduce(f32[2]{0:T(128)S(1)} %pad_maximum_fusion.2), channel_id=1, replica_groups=mesh['island'=16,'fsdp'=32] {'fsdp'}, use_global_device_ids=true, to_apply=%region_6.7 | all-reduce | flops 2 | bytes 16 | tf_op jit(solution)/shard_map/psum | solution.py:90
  187.3 0.6 fusion.43
  188.5 0.1 multiply_subtract_fusion
  188.7 0.2 copy.64
  188.9 0.6 copy.65
  189.5 1.0 reshape.83
  191.1 0.7 multiply_subtract_fusion.2
  191.8 0.8 pad_maximum_fusion
  192.7 1.3 dynamic-slice.1
  194.0 175.0 %all-reduce.3.cloned.1.call-done = f32[16,8448]{1,0:T(8,128)} async-done(((f32[16,8448]{1,0:T(8,128)}), f32[16,8448]{1,0:T(8,128)}) %all-reduce.3.cloned.1.call-update) | async-done | bytes 540688
  369.0 1.7 fusion.28
  370.7 0.1 div.45
  370.8 0.1 copy.66
  370.9 0.6 multiply_subtract_fusion.1
  371.5 2.0 multiply_subtract_fusion.3
  (26 shorter events, 0.2 us)
Async XLA Ops:
  7.2 117.0 %all-gather.2.cloned.1.call-start = ((), (), s32[]{:S(2)}) async-start(), calls=%async_computation.1 | async-start | bytes 4325376 | tf_op jit(solution)/shard_map/all_gather | solution.py:72
  13.5 2.9 copy-start
  18.9 11.5 %copy-start.6 = (s32[128]{0:T(128)S(1)}, s32[128]{0:T(128)}, u32[]{:S(2)}) copy-start(s32[128]{0:T(128)} %param.12) | copy-start | bytes 1540
  18.9 91.4 %all-to-all-start = ((bf16[128,32,256]{0,2,1:T(8,128)(2,1)}), bf16[128,32,256]{0,2,1:T(8,128)(2,1)}, u32[]{:S(2)}, u32[]{:S(2)}) async-start(bf16[128,32,256]{0,2,1:T(8,128)(2,1)} %bitcast.59), calls=%async_computation | async-start | bytes 4194304 | tf_op jit(solution)/shard_map/all_to_all | solution.py:69
  29.2 339.8 %all-reduce.3.cloned.1.call-start = ((), (), s32[]{:S(2)}) async-start(), calls=%async_computation.2 | async-start | bytes 1081344
  120.0 4.2 %copy-start.1 = (bf16[1,256,512]{2,1,0:T(8,128)(2,1)S(1)}, bf16[1,256,512]{2,1,0:T(8,128)(2,1)}, u32[]{:S(2)}) copy-start(bf16[1,256,512]{2,1,0:T(8,128)(2,1)} %param.16) | copy-start | bytes 786436
  188.6 182.2 %copy-start.2 = (f32[256,32]{0,1:T(8,128)S(1)}, f32[256,32]{0,1:T(8,128)}, u32[]{:S(2)}) copy-start(f32[256,32]{0,1:T(8,128)} %param.18) | copy-start | bytes 98308
  188.6 182.2 %copy-start.3 = (f32[256,32]{0,1:T(8,128)S(1)}, f32[256,32]{0,1:T(8,128)}, u32[]{:S(2)}) copy-start(f32[256,32]{0,1:T(8,128)} %param.19) | copy-start | bytes 98308
  188.6 182.9 %copy-start.4 = (f32[1,256]{1,0:T(1,128)S(1)}, f32[1,256]{1,0:T(1,128)}, u32[]{:S(2)}) copy-start(f32[1,256]{1,0:T(1,128)} %param.20) | copy-start | bytes 3076
  188.7 182.9 %copy-start.5 = (f32[1,256]{1,0:T(1,128)S(1)}, f32[1,256]{1,0:T(1,128)}, u32[]{:S(2)}) copy-start(f32[1,256]{1,0:T(1,128)} %param.21) | copy-start | bytes 3076
Sparse Core Ops, SparseCore 0:
  16.5 104.6 all-gather.1
  192.8 176.1 all-reduce.2

commit v2 on v1

--- a/solution.py
+++ b/solution.py
@@ -39,6 +39,39 @@
     grad_four = grad_rows.reshape(length, KV_HEADS, group, HEAD_DIM)
     values = jnp.einsum("kgts,tkgd->skd", weights_bf, grad_four, preferred_element_type=jnp.float32)
     return values.reshape(length, KV_HEADS * HEAD_DIM).astype(jnp.bfloat16)
+
+
+def exchange_sum(part, axis, mask):
+    count = lax.axis_size(axis)
+    pairs = [(rank, rank ^ mask) for rank in range(count)]
+    return part + lax.ppermute(part, axis, pairs)
+
+
+def doubling_sum(value, axis):
+    count = lax.axis_size(axis)
+    mask = 1
+    while mask < count:
+        value = exchange_sum(value, axis, mask)
+        mask *= 2
+    return value
+
+
+def halving_scatter(rows, axis, bit_order):
+    count = lax.axis_size(axis)
+    bits = len(bit_order)
+    rank = lax.axis_index(axis)
+    grid = rows.reshape((2,) * bits + rows.shape[1:])
+    place = list(range(bits))
+    for bit in bit_order:
+        axis_at = place.index(bit)
+        mine = (rank >> (bits - 1 - bit)) & 1
+        keep = lax.dynamic_index_in_dim(grid, mine, axis=axis_at, keepdims=False)
+        send = lax.dynamic_index_in_dim(grid, 1 - mine, axis=axis_at, keepdims=False)
+        mask = 1 << (bits - 1 - bit)
+        pairs = [(member, member ^ mask) for member in range(count)]
+        grid = keep + lax.ppermute(send, axis, pairs)
+        place.pop(axis_at)
+    return grid
 
 
 def body(
@@ -87,7 +120,9 @@
         lang_table.astype(jnp.float32), standard * input_grad, precision=lax.Precision.HIGHEST
     )
     wv_grad = jnp.dot(normed.T, all_values, preferred_element_type=jnp.float32) * weight_scale
-    squares = lax.psum(jnp.stack([jnp.sum(wv_grad * wv_grad), jnp.sum(gain_grad * gain_grad)]), "fsdp")
+    squares = doubling_sum(
+        jnp.stack([jnp.sum(wv_grad * wv_grad), jnp.sum(gain_grad * gain_grad)]), "fsdp"
+    )
     wv_clip = jnp.minimum(1.0, CLIP_SHARE * (width * kv_width) ** 0.5 / jnp.sqrt(squares[0]))
     gain_clip = jnp.minimum(1.0, CLIP_SHARE * (lang_count * width) ** 0.5 / jnp.sqrt(squares[1]))
     new_wv = weight_rows.astype(jnp.float32) - wv_clip * wv_grad
@@ -99,7 +134,7 @@
     wv_part = wv_part.reshape(island_count, col_block * wv_share)
     gain_part = new_gain.reshape(island_count, gain_share * col_block)
     packed = jnp.concatenate([wv_part, gain_part], axis=1)
-    total = lax.psum_scatter(packed, "island", scatter_dimension=0, tiled=True)
+    total = halving_scatter(packed, "island", (2, 1, 3, 0))[None, :]
     total_wv = total[0, : col_block * wv_share].reshape(col_block, wv_share)
     total_gain = total[0, col_block * wv_share :].reshape(gain_share, col_block)
 

time: 381 us -> 226 us (0.59)
  the two profiles are of different devices: /device:TPU:8 before, /device:TPU:32 now
where the time goes in v2:
time: 226 us; the launch traced here: 225 us
  blocking collectives  83.1 us (37%)
  starting transfers between devices  41.5 us (18%)
  waiting for transfers between devices  35.5 us (16%)
  matrix products  17.9 us (8%)
  other arithmetic  15.9 us (7%)
  between operations  15.8 us (7%)
  local copies, waits for them, and re-layouts  15.3 us (7%)
    all_gather x1, blocking collectives, body(): all_stats = lax.all_gather(stats, 'fsdp', axis=1, tiled=True)  83.1 us
    ppermute x4, starting transfers between devices, halving_scatter(): grid = keep + lax.ppermute(send, axis, pairs)  21.3 us
    ppermute x5, waiting for transfers between devices, exchange_sum(): return part + lax.ppermute(part, axis, pairs)  19.6 us
    ppermute x4, waiting for transfers between devices, halving_scatter(): grid = keep + lax.ppermute(send, axis, pairs)  15.9 us
    ppermute x5, starting transfers between devices, exchange_sum(): return part + lax.ppermute(part, axis, pairs)  10.1 us
    all_to_all x1, starting transfers between devices, body(): lax.all_to_all(block_input, 'fsdp', split_axis=1, concat_axis=0, tiled=True)  10 us
    dot_general x1, matrix products, body(): jnp.dot(normed.T, all_values, preferred_element_type=jnp.float32)  5.98 us
    convert_element_type x1, local copies, waits for them, and re-layouts, body(): col_input.astype(jnp.float32) - all_stats[0][:, None]  5.6 us
  transfers between devices with their start and end apart: 11, of which 9 were waited for; matrix products, arithmetic and copies ran while one was open for 8% of the time, Pallas kernels for 0%

profile of v2, /device:TPU:32, one launch (start us, length us, event | category | flops | bytes accessed | tf_op | source)
XLA Modules:
  0.0 224.9 jit_solution(2373262035398129725)
XLA Ops:
  7.2 1.4 copy.61
  9.6 1.6 copy.58
  11.3 2.3 %fusion.44 = (f32[4,8,128]{2,1,0:T(8,128)S(1)}, f32[4,8,128,128]{2,3,1,0:T(8,128)}) fusion(pred[128,128]{0,1:T(8,128)(4,1)S(1)} %iota_compare_fusion.4, bf16[128,4,8,128]{3,2,1,0:T(8,128)(2,1)S(1)} %bitcast.75, bf16[128,4,128,1]{2,1,0,3:T(4,128)(2,1)S(1)} %bitcast.79), kind=kOutput, calls=%fused_computation.68 | convolution fusion | flops 136315008 | bytes 3309568 | tf_op jit(solution)/shard_map/sub | solution.py:37
  13.5 2.8 %fusion.8 = bf16[4,128,128]{1,2,0:T(8,128)(2,1)} fusion(bf16[128,4,8,128]{0,3,2,1:T(8,128)(2,1)S(1)} %bitcast.74, f32[4,8,128,128]{2,3,1,0:T(8,128)} %get-tuple-element.28, f32[4,8,128]{2,1,0:T(8,128)S(1)} %get-tuple-element.27), kind=kOutput, calls=%fused_computation.18 | convolution fusion | flops 135331840 | bytes 3293184 | tf_op jit(solution)/shard_map/kgts,tkgd->skd/dot_general | solution.py:40
  16.4 2.5 %copy.44 = bf16[128,8192]{0,1:T(8,128)(2,1)} copy(bf16[128,8192]{1,0:T(8,128)(2,1)S(1)} %copy-done) | data formatting | bytes 4194304 | tf_op args[0]
  18.9 10.0 %all-to-all-start = ((bf16[128,32,256]{0,2,1:T(8,128)(2,1)}), bf16[128,32,256]{0,2,1:T(8,128)(2,1)}, u32[]{:S(2)}, u32[]{:S(2)}) async-start(bf16[128,32,256]{0,2,1:T(8,128)(2,1)} %bitcast.71), calls=%async_computation | async-start | bytes 4194304 | tf_op jit(solution)/shard_map/all_to_all | solution.py:102
  30.1 83.1 %all_gather.6 = f32[3,4096]{1,0:T(4,128)S(1)} all-gather(f32[3,128]{1,0:T(4,128)S(1)} %pad_maximum_fusion), channel_id=1, replica_groups=mesh['island'=16,'fsdp'=32] {'fsdp'}, dimensions={1}, use_global_device_ids=true | all-gather | bytes 50688 | tf_op jit(solution)/shard_map/all_gather | solution.py:101
  113.2 4.1 %convert_bitcast_fusion = f32[32,128,256]{1,2,0:T(8,128)} fusion(bf16[128,32,256]{0,2,1:T(8,128)(2,1)} %all-to-all-done), kind=kLoop, calls=%fused_computation.11 | loop fusion | flops 1048576 | bytes 6291456 | tf_op jit(solution)/shard_map/convert_element_type | solution.py:107
  117.3 5.6 %copy.45 = f32[32,128,256]{2,1,0:T(8,128)} copy(f32[32,128,256]{1,2,0:T(8,128)} %convert_bitcast_fusion) | data formatting | bytes 8388608 | tf_op jit(solution)/shard_map/convert_element_type | solution.py:107
  122.9 4.2 %fusion.5 = f32[4096,256]{1,0:T(8,128)} fusion(f32[32,128,256]{2,1,0:T(8,128)} %copy.45, f32[4096]{0:T(1024)S(1)} %bitcast.81, f32[4096]{0:T(1024)S(1)} %bitcast.82), kind=kLoop, calls=%fused_computation.10 | loop fusion | flops 2097152 | bytes 8421376 | tf_op jit(solution)/shard_map/mul | solution.py:107
  127.1 4.8 %fusion.1 = f32[4096,256]{1,0:T(8,128)S(1)} fusion(f32[4096,256]{1,0:T(8,128)} %fusion.5, bf16[4096,512]{0,1:T(8,128)(2,1)} %all-gather.2.cloned.1.call-done, bf16[1,256,512]{2,1,0:T(8,128)(2,1)S(1)} %copy-done.1), kind=kOutput, calls=%fused_computation.2 | convolution fusion | flops 1075838976 | bytes 12845056 | tf_op jit(solution)/shard_map/dot_general | solution.py:117
  131.9 2.1 multiply_reduce_fusion.1
  134.0 6.0 %multiply_reduce_fusion = (f32[]{:T(128)}, f32[256,512]{1,0:T(8,128)S(1)}) fusion(bf16[4096,512]{0,1:T(8,128)(2,1)} %all-gather.2.cloned.1.call-done, f32[4096,256]{1,0:T(8,128)} %fusion.5, s32[4096]{0:T(1024)S(1)} %bitcast.77, bf16[1,16,8192]{2,1,0:T(8,128)(2,1)} %param.17, s32[]{:T(128)S(6)} %select_n.35), kind=kOutput, calls=%fused_computation.25 | convolution fusion | flops 1109852160 | bytes 8937480 | tf_op jit(solution)/shard_map/dot_general | solution.py:122
  141.3 2.2 collective-permute-start
  144.4 1.4 fusion.55
  145.7 1.9 collective-permute-start.1
  147.6 3.5 %collective-permute-done.1 = f32[2]{0:T(128)S(1)} collective-permute-done((f32[2]{0:T(128)S(1)}, f32[2]{0:T(128)S(1)}, u32[]{:S(2)}, u32[]{:S(2)}) %collective-permute-start.1) | collective-permute-done | bytes 40 | tf_op jit(solution)/shard_map/ppermute | solution.py:47
  151.2 1.4 fusion.56
  152.5 1.9 collective-permute-start.2
  154.5 3.5 %collective-permute-done.2 = f32[2]{0:T(128)S(1)} collective-permute-done((f32[2]{0:T(128)S(1)}, f32[2]{0:T(128)S(1)}, u32[]{:S(2)}, u32[]{:S(2)}) %collective-permute-start.2) | collective-permute-done | bytes 40 | tf_op jit(solution)/shard_map/ppermute | solution.py:47
  158.0 1.9 collective-permute-start.3
  159.9 4.4 %collective-permute-done.3 = f32[2]{0:T(128)S(1)} collective-permute-done((f32[2]{0:T(128)S(1)}, f32[2]{0:T(128)S(1)}, u32[]{:S(2)}, u32[]{:S(2)}) %collective-permute-start.3) | collective-permute-done | bytes 40 | tf_op jit(solution)/shard_map/ppermute | solution.py:47
  164.3 2.1 collective-permute-start.4
  166.4 7.3 %collective-permute-done.4 = f32[2]{0:T(128)S(1)} collective-permute-done((f32[2]{0:T(128)S(1)}, f32[2]{0:T(128)S(1)}, u32[]{:S(2)}, u32[]{:S(2)}) %collective-permute-start.4) | collective-permute-done | bytes 40 | tf_op jit(solution)/shard_map/ppermute | solution.py:47
  178.6 1.9 collective-permute-start.5
  180.5 6.4 %collective-permute-done.5 = f32[2,2,2,8448]{3,2,1,0:T(2,128)S(1)} collective-permute-done((f32[2,2,2,8448]{3,2,1,0:T(2,128)S(1)}, f32[2,2,2,8448]{3,2,1,0:T(2,128)S(1)}, u32[]{:S(2)}, u32[]{:S(2)}) %collective-permute-start.5) | collective-permute-done | bytes 270368 | tf_op jit(solution)/shard_map/ppermute | solution.py:72
  187.1 5.4 %collective-permute-start.6 = (f32[2,2,8448]{2,1,0:T(2,128)S(1)}, f32[2,2,8448]{2,1,0:T(2,128)S(1)}, u32[]{:S(2)}, u32[]{:S(2)}) collective-permute-start(f32[2,2,8448]{2,1,0:T(2,128)S(1)} %dynamic-slice_bitcast_fusion.1), channel_id=1, source_target_pairs={{0,128},{32,160},{64,192},{96,224},{128,0},{160,32},{192,64},{224,... | collective-permute-start | bytes 405512 | tf_op jit(solution)/shard_map/ppermute | solution.py:72
  192.5 4.4 %collective-permute-done.6 = f32[2,2,8448]{2,1,0:T(2,128)S(1)} collective-permute-done((f32[2,2,8448]{2,1,0:T(2,128)S(1)}, f32[2,2,8448]{2,1,0:T(2,128)S(1)}, u32[]{:S(2)}, u32[]{:S(2)}) %collective-permute-start.6) | collective-permute-done | bytes 135200 | tf_op jit(solution)/shard_map/ppermute | solution.py:72
  197.1 4.5 %collective-permute-start.7 = (f32[2,8448]{1,0:T(2,128)S(1)}, f32[2,8448]{1,0:T(2,128)S(1)}, u32[]{:S(2)}, u32[]{:S(2)}) collective-permute-start(f32[2,8448]{1,0:T(2,128)S(1)} %bitcast.80), channel_id=1, source_target_pairs={{0,32},{32,0},{64,96},{96,64},{128,160},{160,128},{192,224},{224,1... | collective-permute-start | bytes 202760 | tf_op jit(solution)/shard_map/ppermute | solution.py:72
  201.7 3.1 %collective-permute-done.7 = f32[2,8448]{1,0:T(2,128)S(1)} collective-permute-done((f32[2,8448]{1,0:T(2,128)S(1)}, f32[2,8448]{1,0:T(2,128)S(1)}, u32[]{:S(2)}, u32[]{:S(2)}) %collective-permute-start.7) | collective-permute-done | bytes 67616 | tf_op jit(solution)/shard_map/ppermute | solution.py:72
  205.1 9.5 %collective-permute-start.8 = (f32[8448]{0:T(1024)S(1)}, f32[8448]{0:T(1024)S(1)}, u32[]{:S(2)}, u32[]{:S(2)}) collective-permute-start(f32[8448]{0:T(1024)S(1)} %get-tuple-element.12), channel_id=1, source_target_pairs={{0,256},{32,288},{64,320},{96,352},{128,384},{160,416},{192,448},{... | collective-permute-start | bytes 101384 | tf_op jit(solution)/shard_map/ppermute | solution.py:72
  214.6 1.9 collective-permute-done.8
  (56 shorter events, 9.9 us)
Async XLA Ops:
  7.2 119.9 %all-gather.2.cloned.1.call-start = ((), (), s32[]{:S(2)}) async-start(), calls=%async_computation.1 | async-start | bytes 4325376 | tf_op jit(solution)/shard_map/all_gather | solution.py:105
  13.5 2.9 %copy-start = (bf16[128,8192]{1,0:T(8,128)(2,1)S(1)}, bf16[128,8192]{1,0:T(8,128)(2,1)}, u32[]{:S(2)}) copy-start(bf16[128,8192]{1,0:T(8,128)(2,1)} %param.11) | copy-start | bytes 6291460
  18.9 11.2 %copy-start.6 = (s32[128]{0:T(128)S(1)}, s32[128]{0:T(128)}, u32[]{:S(2)}) copy-start(s32[128]{0:T(128)} %param.12) | copy-start | bytes 1540
  18.9 94.3 %all-to-all-start = ((bf16[128,32,256]{0,2,1:T(8,128)(2,1)}), bf16[128,32,256]{0,2,1:T(8,128)(2,1)}, u32[]{:S(2)}, u32[]{:S(2)}) async-start(bf16[128,32,256]{0,2,1:T(8,128)(2,1)} %bitcast.71), calls=%async_computation | async-start | bytes 4194304 | tf_op jit(solution)/shard_map/all_to_all | solution.py:102
  122.9 4.2 %copy-start.1 = (bf16[1,256,512]{2,1,0:T(8,128)(2,1)S(1)}, bf16[1,256,512]{2,1,0:T(8,128)(2,1)}, u32[]{:S(2)}) copy-start(bf16[1,256,512]{2,1,0:T(8,128)(2,1)} %param.16) | copy-start | bytes 786436
  141.3 3.0 %collective-permute-start = (f32[2]{0:T(128)S(1)}, f32[2]{0:T(128)S(1)}, u32[]{:S(2)}, u32[]{:S(2)}) collective-permute-start(f32[2]{0:T(128)S(1)} %pad_maximum_fusion.1), channel_id=1, source_target_pairs={{0,1},{1,0},{2,3},{3,2},{4,5},{5,4},{6,7},{7,6},{8,9},{9,8},{10,11... | collective-permute-start | bytes 32 | tf_op jit(solution)/shard_map/ppermute | solution.py:47
  145.7 5.5 %collective-permute-start.1 = (f32[2]{0:T(128)S(1)}, f32[2]{0:T(128)S(1)}, u32[]{:S(2)}, u32[]{:S(2)}) collective-permute-start(f32[2]{0:T(128)S(1)} %fusion.55), channel_id=1, source_target_pairs={{0,2},{1,3},{2,0},{3,1},{4,6},{5,7},{6,4},{7,5},{8,10},{9,11},{10,... | collective-permute-start | bytes 32 | tf_op jit(solution)/shard_map/ppermute | solution.py:47
  152.5 5.5 %collective-permute-start.2 = (f32[2]{0:T(128)S(1)}, f32[2]{0:T(128)S(1)}, u32[]{:S(2)}, u32[]{:S(2)}) collective-permute-start(f32[2]{0:T(128)S(1)} %fusion.56), channel_id=1, source_target_pairs={{0,4},{1,5},{2,6},{3,7},{4,0},{5,1},{6,2},{7,3},{8,12},{9,13},{10,... | collective-permute-start | bytes 32 | tf_op jit(solution)/shard_map/ppermute | solution.py:47
  158.0 6.3 %collective-permute-start.3 = (f32[2]{0:T(128)S(1)}, f32[2]{0:T(128)S(1)}, u32[]{:S(2)}, u32[]{:S(2)}) collective-permute-start(f32[2]{0:T(128)S(1)} %add.93), channel_id=1, source_target_pairs={{0,8},{1,9},{2,10},{3,11},{4,12},{5,13},{6,14},{7,15},{8,0},{9,1},... | collective-permute-start | bytes 32 | tf_op jit(solution)/shard_map/ppermute | solution.py:47
  164.3 9.4 %collective-permute-start.4 = (f32[2]{0:T(128)S(1)}, f32[2]{0:T(128)S(1)}, u32[]{:S(2)}, u32[]{:S(2)}) collective-permute-start(f32[2]{0:T(128)S(1)} %add.94), channel_id=1, source_target_pairs={{0,16},{1,17},{2,18},{3,19},{4,20},{5,21},{6,22},{7,23},{8,24},{9,... | collective-permute-start | bytes 32 | tf_op jit(solution)/shard_map/ppermute | solution.py:47
  177.3 39.5 %copy-start.4 = (f32[1,256]{1,0:T(1,128)S(1)}, f32[1,256]{1,0:T(1,128)}, u32[]{:S(2)}) copy-start(f32[1,256]{1,0:T(1,128)} %param.20) | copy-start | bytes 3076
  177.3 39.5 %copy-start.5 = (f32[1,256]{1,0:T(1,128)S(1)}, f32[1,256]{1,0:T(1,128)}, u32[]{:S(2)}) copy-start(f32[1,256]{1,0:T(1,128)} %param.21) | copy-start | bytes 3076
  177.3 40.1 %copy-start.2 = (f32[256,32]{0,1:T(8,128)S(1)}, f32[256,32]{0,1:T(8,128)}, u32[]{:S(2)}) copy-start(f32[256,32]{0,1:T(8,128)} %param.18) | copy-start | bytes 98308
  177.3 40.1 %copy-start.3 = (f32[256,32]{0,1:T(8,128)S(1)}, f32[256,32]{0,1:T(8,128)}, u32[]{:S(2)}) copy-start(f32[256,32]{0,1:T(8,128)} %param.19) | copy-start | bytes 98308
  178.6 8.4 %collective-permute-start.5 = (f32[2,2,2,8448]{3,2,1,0:T(2,128)S(1)}, f32[2,2,2,8448]{3,2,1,0:T(2,128)S(1)}, u32[]{:S(2)}, u32[]{:S(2)}) collective-permute-start(f32[2,2,2,8448]{3,2,1,0:T(2,128)S(1)} %dynamic-slice_bitcast_fusion), channel_id=1, source_target_pairs={{0,64},{32,96},{64,0},{96,32},{128,192},{160,224},{192,128},{224,1... | collective-permute-start | bytes 811016 | tf_op jit(solution)/shard_map/ppermute | solution.py:72
  187.1 9.8 %collective-permute-start.6 = (f32[2,2,8448]{2,1,0:T(2,128)S(1)}, f32[2,2,8448]{2,1,0:T(2,128)S(1)}, u32[]{:S(2)}, u32[]{:S(2)}) collective-permute-start(f32[2,2,8448]{2,1,0:T(2,128)S(1)} %dynamic-slice_bitcast_fusion.1), channel_id=1, source_target_pairs={{0,128},{32,160},{64,192},{96,224},{128,0},{160,32},{192,64},{224,... | collective-permute-start | bytes 405512 | tf_op jit(solution)/shard_map/ppermute | solution.py:72
  197.1 7.7 %collective-permute-start.7 = (f32[2,8448]{1,0:T(2,128)S(1)}, f32[2,8448]{1,0:T(2,128)S(1)}, u32[]{:S(2)}, u32[]{:S(2)}) collective-permute-start(f32[2,8448]{1,0:T(2,128)S(1)} %bitcast.80), channel_id=1, source_target_pairs={{0,32},{32,0},{64,96},{96,64},{128,160},{160,128},{192,224},{224,1... | collective-permute-start | bytes 202760 | tf_op jit(solution)/shard_map/ppermute | solution.py:72
  205.1 11.4 %collective-permute-start.8 = (f32[8448]{0:T(1024)S(1)}, f32[8448]{0:T(1024)S(1)}, u32[]{:S(2)}, u32[]{:S(2)}) collective-permute-start(f32[8448]{0:T(1024)S(1)} %get-tuple-element.12), channel_id=1, source_target_pairs={{0,256},{32,288},{64,320},{96,352},{128,384},{160,416},{192,448},{... | collective-permute-start | bytes 101384 | tf_op jit(solution)/shard_map/ppermute | solution.py:72
Sparse Core Ops, SparseCore 0:
  16.5 103.5 all-gather.1

commit v3 on v2

--- a/solution.py
+++ b/solution.py
@@ -74,6 +74,14 @@
     return grid
 
 
+def split_three(value):
+    high = lax.reduce_precision(value, exponent_bits=8, mantissa_bits=7)
+    rest = value - high
+    middle = lax.reduce_precision(rest, exponent_bits=8, mantissa_bits=7)
+    low = rest - middle
+    return [part.astype(jnp.bfloat16) for part in (high, middle, low)]
+
+
 def body(
     block_input,
     lang_ids,
@@ -96,16 +104,27 @@
     weight_scale = width ** (-0.5)
     col_begin = lax.axis_index("fsdp") * col_block
 
+    rows = block_input.shape[0]
     average, inv_std = row_stats(block_input)
-    stats = jnp.stack([average, inv_std, lang_ids.astype(jnp.float32)])
-    all_stats = lax.all_gather(stats, "fsdp", axis=1, tiled=True)
-    col_input = lax.all_to_all(block_input, "fsdp", split_axis=1, concat_axis=0, tiled=True)
+    parts = split_three(average) + split_three(inv_std) + [lang_ids.astype(jnp.bfloat16)]
+    stat_rows = -(-len(parts) * rows // col_block)
+    flat = jnp.concatenate(parts)
+    flat = jnp.pad(flat, (0, stat_rows * col_block - flat.shape[0]))
+    extra = jnp.broadcast_to(flat.reshape(stat_rows, 1, col_block), (stat_rows, fsdp_count, col_block))
+    outgoing = jnp.concatenate([block_input.reshape(rows, fsdp_count, col_block), extra], axis=0)
+    arrived = lax.all_to_all(outgoing, "fsdp", split_axis=1, concat_axis=0, tiled=True)
+    arrived = arrived.reshape(fsdp_count, rows + stat_rows, col_block)
+    col_input = arrived[:, :rows, :].reshape(fsdp_count * rows, col_block)
+    got = arrived[:, rows:, :].reshape(fsdp_count, stat_rows * col_block)[:, : len(parts) * rows]
+    got = got.reshape(fsdp_count, len(parts), rows).astype(jnp.float32)
+    all_average = ((got[:, 0] + got[:, 1]) + got[:, 2]).reshape(-1)
+    all_inv_std = ((got[:, 3] + got[:, 4]) + got[:, 5]).reshape(-1)
+    all_lang = got[:, 6].reshape(-1).astype(jnp.int32)
 
     values_grad = value_grad(queries, saved_keys, out_grad)
     all_values = lax.all_gather(values_grad, "fsdp", axis=0, tiled=True)
 
-    standard = (col_input.astype(jnp.float32) - all_stats[0][:, None]) * all_stats[1][:, None]
-    all_lang = all_stats[2].astype(jnp.int32)
+    standard = (col_input.astype(jnp.float32) - all_average[:, None]) * all_inv_std[:, None]
     lang_table = all_lang[None, :] == jnp.arange(lang_count, dtype=jnp.int32)[:, None]
     own_gain = lax.dynamic_slice_in_dim(local_gain[0], col_begin, col_block, 1)
     gain_rows = jnp.dot(

time: 226 us -> 223 us (0.987)
  the two profiles are of different devices: /device:TPU:32 before, /device:TPU:64 now
where the time goes in v3:
time: 223 us; the launch traced here: 222 us
  waiting for transfers between devices  112 us (50%)
  starting transfers between devices  45.6 us (20%)
  local copies, waits for them, and re-layouts  19 us (9%)
  matrix products  17.3 us (8%)
  between operations  15.8 us (7%)
  other arithmetic  12.2 us (5%)
    all_to_all x1, waiting for transfers between devices, body(): lax.all_to_all(outgoing, 'fsdp', split_axis=1, concat_axis=0, tiled=True)  66.2 us
    ppermute x4, starting transfers between devices, halving_scatter(): grid = keep + lax.ppermute(send, axis, pairs)  20.4 us
    ppermute x5, starting transfers between devices, exchange_sum(): return part + lax.ppermute(part, axis, pairs)  16.4 us
    all_gather x1, waiting for transfers between devices, body(): all_values = lax.all_gather(values_grad, 'fsdp', axis=0, tiled=True)  16.4 us
    ppermute x4, waiting for transfers between devices, halving_scatter(): grid = keep + lax.ppermute(send, axis, pairs)  16.2 us
    ppermute x5, waiting for transfers between devices, exchange_sum(): return part + lax.ppermute(part, axis, pairs)  13.2 us
    all_to_all x1, starting transfers between devices, body(): lax.all_to_all(outgoing, 'fsdp', split_axis=1, concat_axis=0, tiled=True)  8.73 us
    dot_general x1, matrix products, body(): jnp.dot(normed.T, all_values, preferred_element_type=jnp.float32)  5.83 us
  transfers between devices with their start and end apart: 11, of which 11 were waited for; matrix products, arithmetic and copies ran while one was open for 8% of the time, Pallas kernels for 0%

profile of v3, /device:TPU:64, one launch (start us, length us, event | category | flops | bytes accessed | tf_op | source)
XLA Modules:
  0.0 221.9 jit_solution(2749305408318719075)
XLA Ops:
  7.2 1.4 copy.93
  9.6 1.6 copy.89
  11.3 2.3 %fusion.45 = (f32[4,8,128]{2,1,0:T(8,128)S(1)}, f32[4,8,128,128]{2,3,1,0:T(8,128)}) fusion(pred[128,128]{0,1:T(8,128)(4,1)S(1)} %iota_compare_fusion.4, bf16[128,4,8,128]{3,2,1,0:T(8,128)(2,1)S(1)} %bitcast.76, bf16[128,4,128,1]{2,1,0,3:T(4,128)(2,1)S(1)} %bitcast.80), kind=kOutput, calls=%fused_computation.80 | convolution fusion | flops 136315008 | bytes 3309568 | tf_op jit(solution)/shard_map/sub | solution.py:37
  13.6 2.8 %fusion.8 = bf16[4,128,128]{1,2,0:T(8,128)(2,1)} fusion(bf16[128,4,8,128]{0,3,2,1:T(8,128)(2,1)S(1)} %bitcast.75, f32[4,8,128,128]{2,3,1,0:T(8,128)} %get-tuple-element.41, f32[4,8,128]{2,1,0:T(8,128)S(1)} %get-tuple-element.40), kind=kOutput, calls=%fused_computation.18 | convolution fusion | flops 135331840 | bytes 3293184 | tf_op jit(solution)/shard_map/kgts,tkgd->skd/dot_general | solution.py:40
  16.5 2.5 %copy.74 = bf16[128,8192]{0,1:T(8,128)(2,1)} copy(bf16[128,8192]{1,0:T(8,128)(2,1)S(1)} %copy-done) | data formatting | bytes 4194304 | tf_op args[0]
  22.1 4.5 %pad_maximum_fusion = bf16[132,32,256]{0,2,1:T(8,128)(2,1)} fusion(bf16[4,32,256]{0,2,1:T(8,128)(2,1)S(1)} %broadcast_in_dim.26, bf16[128,32,256]{0,2,1:T(8,128)(2,1)} %bitcast.70), kind=kLoop, calls=%fused_computation.9 | loop fusion | flops 4325376 | bytes 4325376 | tf_op jit(solution)/shard_map/concatenate | solution.py:114
  26.6 5.6 %copy.76 = bf16[132,32,256]{2,0,1:T(8,128)(2,1)} copy(bf16[132,32,256]{0,2,1:T(8,128)(2,1)} %pad_maximum_fusion) | data formatting | bytes 4325376 | tf_op jit(solution)/shard_map/concatenate | solution.py:114
  32.3 8.7 %all-to-all-start = ((bf16[132,32,256]{2,0,1:T(8,128)(2,1)}), bf16[132,32,256]{2,0,1:T(8,128)(2,1)S(1)}, u32[]{:S(2)}, u32[]{:S(2)}) async-start(bf16[132,32,256]{2,0,1:T(8,128)(2,1)} %copy.76), calls=%async_computation | async-start | bytes 4456448 | tf_op jit(solution)/shard_map/all_to_all | solution.py:115
  41.0 66.2 %all-to-all-done = bf16[132,32,256]{2,0,1:T(8,128)(2,1)S(1)} async-done(((bf16[132,32,256]{2,0,1:T(8,128)(2,1)}), bf16[132,32,256]{2,0,1:T(8,128)(2,1)S(1)}, u32[]{:S(2)}, u32[]{:S(2)}) %all-to-all-start) | async-done | bytes 2162720 | tf_op jit(solution)/shard_map/all_to_all | solution.py:115
  107.3 1.6 slice.56
  109.0 16.4 %all-gather.2.cloned.1.call-done = bf16[4096,512]{0,1:T(8,128)(2,1)} async-done(((bf16[128,512]{0,1:T(8,128)(2,1)}), bf16[4096,512]{0,1:T(8,128)(2,1)}) %all-gather.2.cloned.1.call-update) | async-done | bytes 4194320 | tf_op jit(solution)/shard_map/all_gather | solution.py:125
  125.4 4.3 %fusion.1 = f32[4096,256]{1,0:T(8,128)S(1)} fusion(bf16[4096,512]{0,1:T(8,128)(2,1)} %all-gather.2.cloned.1.call-done, bf16[4096,256]{1,0:T(8,128)(2,1)} %bitcast.72, f32[4096]{0:T(1024)S(1)} %bitcast.86, f32[4096]{0:T(1024)S(1)} %bitcast.84, bf16[1,256,512]{2,1,0:T(8,128)(2,1)S(1)} %copy-done.2), kind=kOutput, calls=%fused_computation.2 | convolution fusion | flops 1078984704 | bytes 10780672 | tf_op jit(solution)/shard_map/dot_general | solution.py:136
  129.6 2.1 multiply_reduce_fusion.1
  131.7 5.8 %multiply_reduce_fusion = (f32[]{:T(128)}, f32[256,512]{1,0:T(8,128)S(1)}) fusion(bf16[4096,512]{0,1:T(8,128)(2,1)} %all-gather.2.cloned.1.call-done, bf16[4096,256]{1,0:T(8,128)(2,1)S(1)} %bitcast.73, f32[4096]{0:T(1024)S(1)} %bitcast.87, f32[4096]{0:T(1024)S(1)} %bitcast.85, s32[4096]{0:T(1024)S(1)} %bitcast.83, bf16[1,16,8192]{2,1,0:T(8,128)(2,1)} %param.17, ...), kind=kOutput, calls=%fused_computation.25 | convolution fusion | flops 1112997888 | bytes 6873096 | tf_op jit(solution)/shard_map/dot_general | solution.py:141
  138.9 2.1 collective-permute-start
  143.3 2.1 collective-permute-start.1
  145.5 3.3 %collective-permute-done.1 = f32[2]{0:T(128)S(1)} collective-permute-done((f32[2]{0:T(128)S(1)}, f32[2]{0:T(128)S(1)}, u32[]{:S(2)}, u32[]{:S(2)}) %collective-permute-start.1) | collective-permute-done | bytes 40 | tf_op jit(solution)/shard_map/ppermute | solution.py:47
  148.8 1.4 fusion.57
  150.2 3.3 %collective-permute-start.2 = (f32[2]{0:T(128)S(1)}, f32[2]{0:T(128)S(1)}, u32[]{:S(2)}, u32[]{:S(2)}) collective-permute-start(f32[2]{0:T(128)S(1)} %fusion.57), channel_id=1, source_target_pairs={{0,4},{1,5},{2,6},{3,7},{4,0},{5,1},{6,2},{7,3},{8,12},{9,13},{10,... | collective-permute-start | bytes 32 | tf_op jit(solution)/shard_map/ppermute | solution.py:47
  153.5 2.1 collective-permute-done.2
  155.6 3.3 %collective-permute-start.3 = (f32[2]{0:T(128)S(1)}, f32[2]{0:T(128)S(1)}, u32[]{:S(2)}, u32[]{:S(2)}) collective-permute-start(f32[2]{0:T(128)S(1)} %add.129), channel_id=1, source_target_pairs={{0,8},{1,9},{2,10},{3,11},{4,12},{5,13},{6,14},{7,15},{8,0},{9,1},... | collective-permute-start | bytes 32 | tf_op jit(solution)/shard_map/ppermute | solution.py:47
  159.0 3.0 %collective-permute-done.3 = f32[2]{0:T(128)S(1)} collective-permute-done((f32[2]{0:T(128)S(1)}, f32[2]{0:T(128)S(1)}, u32[]{:S(2)}, u32[]{:S(2)}) %collective-permute-start.3) | collective-permute-done | bytes 40 | tf_op jit(solution)/shard_map/ppermute | solution.py:47
  162.0 5.5 %collective-permute-start.4 = (f32[2]{0:T(128)S(1)}, f32[2]{0:T(128)S(1)}, u32[]{:S(2)}, u32[]{:S(2)}) collective-permute-start(f32[2]{0:T(128)S(1)} %add.130), channel_id=1, source_target_pairs={{0,16},{1,17},{2,18},{3,19},{4,20},{5,21},{6,22},{7,23},{8,24},{9,... | collective-permute-start | bytes 32 | tf_op jit(solution)/shard_map/ppermute | solution.py:47
  167.5 3.9 %collective-permute-done.4 = f32[2]{0:T(128)S(1)} collective-permute-done((f32[2]{0:T(128)S(1)}, f32[2]{0:T(128)S(1)}, u32[]{:S(2)}, u32[]{:S(2)}) %collective-permute-start.4) | collective-permute-done | bytes 40 | tf_op jit(solution)/shard_map/ppermute | solution.py:47
  176.2 1.9 collective-permute-start.5
  178.1 6.4 %collective-permute-done.5 = f32[2,2,2,8448]{3,2,1,0:T(2,128)S(1)} collective-permute-done((f32[2,2,2,8448]{3,2,1,0:T(2,128)S(1)}, f32[2,2,2,8448]{3,2,1,0:T(2,128)S(1)}, u32[]{:S(2)}, u32[]{:S(2)}) %collective-permute-start.5) | collective-permute-done | bytes 270368 | tf_op jit(solution)/shard_map/ppermute | solution.py:72
  184.7 3.8 %collective-permute-start.6 = (f32[2,2,8448]{2,1,0:T(2,128)S(1)}, f32[2,2,8448]{2,1,0:T(2,128)S(1)}, u32[]{:S(2)}, u32[]{:S(2)}) collective-permute-start(f32[2,2,8448]{2,1,0:T(2,128)S(1)} %dynamic-slice_bitcast_fusion.1), channel_id=1, source_target_pairs={{0,128},{32,160},{64,192},{96,224},{128,0},{160,32},{192,64},{224,... | collective-permute-start | bytes 405512 | tf_op jit(solution)/shard_map/ppermute | solution.py:72
  188.5 4.1 %collective-permute-done.6 = f32[2,2,8448]{2,1,0:T(2,128)S(1)} collective-permute-done((f32[2,2,8448]{2,1,0:T(2,128)S(1)}, f32[2,2,8448]{2,1,0:T(2,128)S(1)}, u32[]{:S(2)}, u32[]{:S(2)}) %collective-permute-start.6) | collective-permute-done | bytes 135200 | tf_op jit(solution)/shard_map/ppermute | solution.py:72
  192.9 4.2 %collective-permute-start.7 = (f32[2,8448]{1,0:T(2,128)S(1)}, f32[2,8448]{1,0:T(2,128)S(1)}, u32[]{:S(2)}, u32[]{:S(2)}) collective-permute-start(f32[2,8448]{1,0:T(2,128)S(1)} %bitcast.81), channel_id=1, source_target_pairs={{0,32},{32,0},{64,96},{96,64},{128,160},{160,128},{192,224},{224,1... | collective-permute-start | bytes 202760 | tf_op jit(solution)/shard_map/ppermute | solution.py:72
  197.1 3.5 %collective-permute-done.7 = f32[2,8448]{1,0:T(2,128)S(1)} collective-permute-done((f32[2,8448]{1,0:T(2,128)S(1)}, f32[2,8448]{1,0:T(2,128)S(1)}, u32[]{:S(2)}, u32[]{:S(2)}) %collective-permute-start.7) | collective-permute-done | bytes 67616 | tf_op jit(solution)/shard_map/ppermute | solution.py:72
  200.8 10.5 %collective-permute-start.8 = (f32[8448]{0:T(1024)S(1)}, f32[8448]{0:T(1024)S(1)}, u32[]{:S(2)}, u32[]{:S(2)}) collective-permute-start(f32[8448]{0:T(1024)S(1)} %get-tuple-element.20), channel_id=1, source_target_pairs={{0,256},{32,288},{64,320},{96,352},{128,384},{160,416},{192,448},{... | collective-permute-start | bytes 101384 | tf_op jit(solution)/shard_map/ppermute | solution.py:72
  211.3 2.2 collective-permute-done.8
  (72 shorter events, 13.5 us)
Async XLA Ops:
  7.2 118.2 %all-gather.2.cloned.1.call-start = ((), (), s32[]{:S(2)}) async-start(), calls=%async_computation.1 | async-start | bytes 4325376 | tf_op jit(solution)/shard_map/all_gather | solution.py:125
  13.6 2.9 %copy-start.7 = (s32[128]{0:T(128)S(1)}, s32[128]{0:T(128)}, u32[]{:S(2)}) copy-start(s32[128]{0:T(128)} %param.12) | copy-start | bytes 1540
  13.6 2.9 %copy-start = (bf16[128,8192]{1,0:T(8,128)(2,1)S(1)}, bf16[128,8192]{1,0:T(8,128)(2,1)}, u32[]{:S(2)}) copy-start(bf16[128,8192]{1,0:T(8,128)(2,1)} %param.11) | copy-start | bytes 6291460
  32.3 93.1 %copy-start.2 = (bf16[1,256,512]{2,1,0:T(8,128)(2,1)S(1)}, bf16[1,256,512]{2,1,0:T(8,128)(2,1)}, u32[]{:S(2)}) copy-start(bf16[1,256,512]{2,1,0:T(8,128)(2,1)} %param.16) | copy-start | bytes 786436
  32.3 75.0 %all-to-all-start = ((bf16[132,32,256]{2,0,1:T(8,128)(2,1)}), bf16[132,32,256]{2,0,1:T(8,128)(2,1)S(1)}, u32[]{:S(2)}, u32[]{:S(2)}) async-start(bf16[132,32,256]{2,0,1:T(8,128)(2,1)} %copy.76), calls=%async_computation | async-start | bytes 4456448 | tf_op jit(solution)/shard_map/all_to_all | solution.py:115
  129.6 2.1 copy-start.1
  138.9 3.0 %collective-permute-start = (f32[2]{0:T(128)S(1)}, f32[2]{0:T(128)S(1)}, u32[]{:S(2)}, u32[]{:S(2)}) collective-permute-start(f32[2]{0:T(128)S(1)} %pad_maximum_fusion.1), channel_id=1, source_target_pairs={{0,1},{1,0},{2,3},{3,2},{4,5},{5,4},{6,7},{7,6},{8,9},{9,8},{10,11... | collective-permute-start | bytes 32 | tf_op jit(solution)/shard_map/ppermute | solution.py:47
  143.3 5.5 %collective-permute-start.1 = (f32[2]{0:T(128)S(1)}, f32[2]{0:T(128)S(1)}, u32[]{:S(2)}, u32[]{:S(2)}) collective-permute-start(f32[2]{0:T(128)S(1)} %fusion.56), channel_id=1, source_target_pairs={{0,2},{1,3},{2,0},{3,1},{4,6},{5,7},{6,4},{7,5},{8,10},{9,11},{10,... | collective-permute-start | bytes 32 | tf_op jit(solution)/shard_map/ppermute | solution.py:47
  150.2 5.5 %collective-permute-start.2 = (f32[2]{0:T(128)S(1)}, f32[2]{0:T(128)S(1)}, u32[]{:S(2)}, u32[]{:S(2)}) collective-permute-start(f32[2]{0:T(128)S(1)} %fusion.57), channel_id=1, source_target_pairs={{0,4},{1,5},{2,6},{3,7},{4,0},{5,1},{6,2},{7,3},{8,12},{9,13},{10,... | collective-permute-start | bytes 32 | tf_op jit(solution)/shard_map/ppermute | solution.py:47
  155.6 6.3 %collective-permute-start.3 = (f32[2]{0:T(128)S(1)}, f32[2]{0:T(128)S(1)}, u32[]{:S(2)}, u32[]{:S(2)}) collective-permute-start(f32[2]{0:T(128)S(1)} %add.129), channel_id=1, source_target_pairs={{0,8},{1,9},{2,10},{3,11},{4,12},{5,13},{6,14},{7,15},{8,0},{9,1},... | collective-permute-start | bytes 32 | tf_op jit(solution)/shard_map/ppermute | solution.py:47
  162.0 9.4 %collective-permute-start.4 = (f32[2]{0:T(128)S(1)}, f32[2]{0:T(128)S(1)}, u32[]{:S(2)}, u32[]{:S(2)}) collective-permute-start(f32[2]{0:T(128)S(1)} %add.130), channel_id=1, source_target_pairs={{0,16},{1,17},{2,18},{3,19},{4,20},{5,21},{6,22},{7,23},{8,24},{9,... | collective-permute-start | bytes 32 | tf_op jit(solution)/shard_map/ppermute | solution.py:47
  174.9 38.9 %copy-start.5 = (f32[1,256]{1,0:T(1,128)S(1)}, f32[1,256]{1,0:T(1,128)}, u32[]{:S(2)}) copy-start(f32[1,256]{1,0:T(1,128)} %param.20) | copy-start | bytes 3076
  174.9 38.9 %copy-start.6 = (f32[1,256]{1,0:T(1,128)S(1)}, f32[1,256]{1,0:T(1,128)}, u32[]{:S(2)}) copy-start(f32[1,256]{1,0:T(1,128)} %param.21) | copy-start | bytes 3076
  174.9 39.5 %copy-start.3 = (f32[256,32]{0,1:T(8,128)S(1)}, f32[256,32]{0,1:T(8,128)}, u32[]{:S(2)}) copy-start(f32[256,32]{0,1:T(8,128)} %param.18) | copy-start | bytes 98308
  175.0 39.5 %copy-start.4 = (f32[256,32]{0,1:T(8,128)S(1)}, f32[256,32]{0,1:T(8,128)}, u32[]{:S(2)}) copy-start(f32[256,32]{0,1:T(8,128)} %param.19) | copy-start | bytes 98308
  176.2 8.4 %collective-permute-start.5 = (f32[2,2,2,8448]{3,2,1,0:T(2,128)S(1)}, f32[2,2,2,8448]{3,2,1,0:T(2,128)S(1)}, u32[]{:S(2)}, u32[]{:S(2)}) collective-permute-start(f32[2,2,2,8448]{3,2,1,0:T(2,128)S(1)} %dynamic-slice_bitcast_fusion), channel_id=1, source_target_pairs={{0,64},{32,96},{64,0},{96,32},{128,192},{160,224},{192,128},{224,1... | collective-permute-start | bytes 811016 | tf_op jit(solution)/shard_map/ppermute | solution.py:72
  184.7 7.9 %collective-permute-start.6 = (f32[2,2,8448]{2,1,0:T(2,128)S(1)}, f32[2,2,8448]{2,1,0:T(2,128)S(1)}, u32[]{:S(2)}, u32[]{:S(2)}) collective-permute-start(f32[2,2,8448]{2,1,0:T(2,128)S(1)} %dynamic-slice_bitcast_fusion.1), channel_id=1, source_target_pairs={{0,128},{32,160},{64,192},{96,224},{128,0},{160,32},{192,64},{224,... | collective-permute-start | bytes 405512 | tf_op jit(solution)/shard_map/ppermute | solution.py:72
  192.9 7.7 %collective-permute-start.7 = (f32[2,8448]{1,0:T(2,128)S(1)}, f32[2,8448]{1,0:T(2,128)S(1)}, u32[]{:S(2)}, u32[]{:S(2)}) collective-permute-start(f32[2,8448]{1,0:T(2,128)S(1)} %bitcast.81), channel_id=1, source_target_pairs={{0,32},{32,0},{64,96},{96,64},{128,160},{160,128},{192,224},{224,1... | collective-permute-start | bytes 202760 | tf_op jit(solution)/shard_map/ppermute | solution.py:72
  200.8 12.7 %collective-permute-start.8 = (f32[8448]{0:T(1024)S(1)}, f32[8448]{0:T(1024)S(1)}, u32[]{:S(2)}, u32[]{:S(2)}) collective-permute-start(f32[8448]{0:T(1024)S(1)} %get-tuple-element.20), channel_id=1, source_target_pairs={{0,256},{32,288},{64,320},{96,352},{128,384},{160,416},{192,448},{... | collective-permute-start | bytes 101384 | tf_op jit(solution)/shard_map/ppermute | solution.py:72
Sparse Core Ops, SparseCore 0:
  16.6 108.7 all-gather.1

commit v4 on v3

--- a/solution.py
+++ b/solution.py
@@ -1,7 +1,7 @@
 import jax
 import jax.numpy as jnp
 from jax import lax
-from jax.sharding import PartitionSpec as P
+from jax.sharding import Mesh, PartitionSpec as P
 
 HEADS = 32
 KV_HEADS = 4
@@ -96,13 +96,15 @@
     gain_momentum,
 ):
     width = block_input.shape[1]
-    fsdp_count = lax.axis_size("fsdp")
+    fsdp_count = lax.axis_size("chip") * lax.axis_size("core")
+    core = lax.axis_index("core")
+    fsdp_at = lax.axis_index("chip") * lax.axis_size("core") + core
     island_count = lax.axis_size("island")
     col_block = width // fsdp_count
     kv_width = local_wv.shape[2]
     lang_count = local_gain.shape[1]
     weight_scale = width ** (-0.5)
-    col_begin = lax.axis_index("fsdp") * col_block
+    col_begin = fsdp_at * col_block
 
     rows = block_input.shape[0]
     average, inv_std = row_stats(block_input)
@@ -112,7 +114,7 @@
     flat = jnp.pad(flat, (0, stat_rows * col_block - flat.shape[0]))
     extra = jnp.broadcast_to(flat.reshape(stat_rows, 1, col_block), (stat_rows, fsdp_count, col_block))
     outgoing = jnp.concatenate([block_input.reshape(rows, fsdp_count, col_block), extra], axis=0)
-    arrived = lax.all_to_all(outgoing, "fsdp", split_axis=1, concat_axis=0, tiled=True)
+    arrived = lax.all_to_all(outgoing, FSDP, split_axis=1, concat_axis=0, tiled=True)
     arrived = arrived.reshape(fsdp_count, rows + stat_rows, col_block)
     col_input = arrived[:, :rows, :].reshape(fsdp_count * rows, col_block)
     got = arrived[:, rows:, :].reshape(fsdp_count, stat_rows * col_block)[:, : len(parts) * rows]
@@ -122,7 +124,14 @@
     all_lang = got[:, 6].reshape(-1).astype(jnp.int32)
 
     values_grad = value_grad(queries, saved_keys, out_grad)
-    all_values = lax.all_gather(values_grad, "fsdp", axis=0, tiled=True)
+    own_half = lax.all_gather(values_grad, "chip", axis=0, tiled=True)
+    other_half = lax.ppermute(own_half, "core", [(0, 1), (1, 0)])
+    first = lax.select(core == 0, own_half, other_half)
+    second = lax.select(core == 0, other_half, own_half)
+    chips = lax.axis_size("chip")
+    all_values = jnp.stack(
+        [first.reshape(chips, rows, kv_width), second.reshape(chips, rows, kv_width)], axis=1
+    ).reshape(fsdp_count * rows, kv_width)
 
     standard = (col_input.astype(jnp.float32) - all_average[:, None]) * all_inv_std[:, None]
     lang_table = all_lang[None, :] == jnp.arange(lang_count, dtype=jnp.int32)[:, None]
@@ -140,7 +149,8 @@
     )
     wv_grad = jnp.dot(normed.T, all_values, preferred_element_type=jnp.float32) * weight_scale
     squares = doubling_sum(
-        jnp.stack([jnp.sum(wv_grad * wv_grad), jnp.sum(gain_grad * gain_grad)]), "fsdp"
+        doubling_sum(jnp.stack([jnp.sum(wv_grad * wv_grad), jnp.sum(gain_grad * gain_grad)]), "core"),
+        "chip",
     )
     wv_clip = jnp.minimum(1.0, CLIP_SHARE * (width * kv_width) ** 0.5 / jnp.sqrt(squares[0]))
     gain_clip = jnp.minimum(1.0, CLIP_SHARE * (lang_count * width) ** 0.5 / jnp.sqrt(squares[1]))
@@ -166,19 +176,24 @@
     return (result_wv, momentum_wv, result_gain, momentum_gain)
 
 
+FSDP = ("chip", "core")
+
+
 def solution(mesh):
+    island_count, fsdp_count = mesh.devices.shape
+    split = Mesh(mesh.devices.reshape(island_count, fsdp_count // 2, 2), ("island", "chip", "core"))
     in_specs = (
-        P(("island", "fsdp"), None),
-        P(("island", "fsdp")),
-        P(("island", "fsdp"), None),
-        P(("island", "fsdp"), None),
-        P(("island", "fsdp"), None),
-        P("island", "fsdp", None),
+        P(("island",) + FSDP, None),
+        P(("island",) + FSDP),
+        P(("island",) + FSDP, None),
+        P(("island",) + FSDP, None),
+        P(("island",) + FSDP, None),
+        P("island", FSDP, None),
         P("island", None, None),
-        P("fsdp", "island"),
-        P("fsdp", "island"),
-        P("island", "fsdp"),
-        P("island", "fsdp"),
+        P(FSDP, "island"),
+        P(FSDP, "island"),
+        P("island", FSDP),
+        P("island", FSDP),
     )
-    out_specs = (P("fsdp", "island"), P("fsdp", "island"), P("island", "fsdp"), P("island", "fsdp"))
-    return jax.shard_map(body, mesh=mesh, in_specs=in_specs, out_specs=out_specs, check_vma=False)
+    out_specs = (P(FSDP, "island"), P(FSDP, "island"), P("island", FSDP), P("island", FSDP))
+    return jax.shard_map(body, mesh=split, in_specs=in_specs, out_specs=out_specs, check_vma=False)

time: 223 us -> 248 us (1.11)
  the two profiles are of different devices: /device:TPU:64 before, /device:TPU:4 now
where the time goes in v4:
time: 248 us; the launch traced here: 247 us
  waiting for transfers between devices  123 us (50%)
  starting transfers between devices  49 us (20%)
  local copies, waits for them, and re-layouts  26 us (10%)
  other arithmetic  18.7 us (8%)
  between operations  15.8 us (6%)
  matrix products  14.4 us (6%)
    all_gather x1, waiting for transfers between devices, body(): own_half = lax.all_gather(values_grad, 'chip', axis=0, tiled=True)  88.4 us
    ppermute x4, starting transfers between devices, halving_scatter(): grid = keep + lax.ppermute(send, axis, pairs)  19.4 us
    ppermute x5, starting transfers between devices, exchange_sum(): return part + lax.ppermute(part, axis, pairs)  19.3 us
    ppermute x4, waiting for transfers between devices, halving_scatter(): grid = keep + lax.ppermute(send, axis, pairs)  19.3 us
    ppermute x5, waiting for transfers between devices, exchange_sum(): return part + lax.ppermute(part, axis, pairs)  12.8 us
    all_to_all x1, starting transfers between devices, body(): lax.all_to_all(outgoing, FSDP, split_axis=1, concat_axis=0, tiled=True)  8.13 us
    dot_general x1, matrix products, body(): jnp.dot(normed.T, all_values, preferred_element_type=jnp.float32)  5.95 us
    unnamed x29, local copies, waits for them, and re-layouts  5.88 us
  transfers between devices with their start and end apart: 12, of which 11 were waited for; matrix products, arithmetic and copies ran while one was open for 7% of the time, Pallas kernels for 0%

profile of v4, /device:TPU:4, one launch (start us, length us, event | category | flops | bytes accessed | tf_op | source)
XLA Modules:
  0.0 247.0 jit_solution(5157393792812463110)
XLA Ops:
  9.6 1.6 copy.99
  11.3 2.3 fusion.45
  13.5 2.8 %fusion.8 = bf16[4,128,128]{1,2,0:T(8,128)(2,1)} fusion(bf16[128,4,8,128]{0,3,2,1:T(8,128)(2,1)S(1)} %bitcast.82, f32[4,8,128,128]{2,3,1,0:T(8,128)} %get-tuple-element.43, f32[4,8,128]{2,1,0:T(8,128)S(1)} %get-tuple-element.42), kind=kOutput, calls=%fused_computation.21 | convolution fusion | flops 135331840 | bytes 3293184 | tf_op jit(solution)/shard_map/kgts,tkgd->skd/dot_general | solution.py:40
  16.5 2.5 copy.82
  22.0 4.5 %pad_maximum_fusion = bf16[132,32,256]{0,2,1:T(8,128)(2,1)} fusion(bf16[4,32,256]{0,2,1:T(8,128)(2,1)S(1)} %broadcast_in_dim.26, bf16[128,32,256]{0,2,1:T(8,128)(2,1)} %bitcast.73), kind=kLoop, calls=%fused_computation.9 | loop fusion | flops 4325376 | bytes 4325376 | tf_op jit(solution)/shard_map/concatenate | solution.py:116
  26.5 5.6 %copy.84 = bf16[132,32,256]{2,0,1:T(8,128)(2,1)} copy(bf16[132,32,256]{0,2,1:T(8,128)(2,1)} %pad_maximum_fusion) | data formatting | bytes 4325376 | tf_op jit(solution)/shard_map/concatenate | solution.py:116
  32.2 8.1 %all-to-all-start = ((bf16[132,32,256]{2,0,1:T(8,128)(2,1)}), bf16[132,32,256]{2,0,1:T(8,128)(2,1)S(1)}, u32[]{:S(2)}, u32[]{:S(2)}) async-start(bf16[132,32,256]{2,0,1:T(8,128)(2,1)} %copy.84), calls=%async_computation | async-start | bytes 4456448 | tf_op jit(solution)/shard_map/all_to_all | solution.py:117
  40.3 88.4 %all-gather.2.cloned.1.call-done = bf16[2048,512]{0,1:T(8,128)(2,1)} async-done(((bf16[128,512]{0,1:T(8,128)(2,1)}), bf16[2048,512]{0,1:T(8,128)(2,1)}) %all-gather.2.cloned.1.call-update) | async-done | bytes 2097168 | tf_op jit(solution)/shard_map/all_gather | solution.py:127
  128.8 2.1 collective-permute-start
  130.9 1.6 slice.56
  132.6 2.5 %collective-permute-done = bf16[2048,512]{0,1:T(8,128)(2,1)} collective-permute-done((bf16[2048,512]{0,1:T(8,128)(2,1)}, bf16[2048,512]{0,1:T(8,128)(2,1)}, u32[]{:S(2)}, u32[]{:S(2)}) %collective-permute-start) | collective-permute-done | bytes 2097184 | tf_op jit(solution)/shard_map/ppermute | solution.py:128
  135.1 3.8 %broadcast_select_fusion.1 = (bf16[2048,512]{0,1:T(8,128)(2,1)}, bf16[2048,512]{0,1:T(8,128)(2,1)S(1)}) fusion(bf16[2048,512]{0,1:T(8,128)(2,1)} %all-gather.2.cloned.1.call-done, bf16[2048,512]{0,1:T(8,128)(2,1)} %collective-permute-done, pred[]{:T(512)S(6)} %eq.20), kind=kLoop, calls=%fused_computation.17 | loop fusion | flops 2097152 | bytes 8388609 | tf_op jit(solution)/shard_map/select_n | solution.py:129
  139.0 3.9 %copy.89 = bf16[2048,512]{1,0:T(8,128)(2,1)} copy(bf16[2048,512]{0,1:T(8,128)(2,1)} %get-tuple-element.26) | data formatting | bytes 4194304 | tf_op jit(solution)/shard_map/select_n | solution.py:129
  142.9 2.5 %copy.90 = bf16[2048,512]{1,0:T(8,128)(2,1)} copy(bf16[2048,512]{0,1:T(8,128)(2,1)S(1)} %get-tuple-element.27) | data formatting | bytes 4194304 | tf_op jit(solution)/shard_map/select_n | solution.py:130
  145.4 2.8 %pad_maximum_fusion.1 = bf16[16,2,128,512]{3,2,1,0:T(8,128)(2,1)S(1)} fusion(bf16[16,1,128,512]{3,2,1,0:T(8,128)(2,1)} %bitcast.75, bf16[16,1,128,512]{3,2,1,0:T(8,128)(2,1)} %bitcast.74), kind=kLoop, calls=%fused_computation.10 | loop fusion | flops 2097152 | bytes 8388608 | tf_op jit(solution)/shard_map/stack | solution.py:132
  150.1 2.1 multiply_reduce_fusion.1
  152.1 5.9 %multiply_reduce_fusion = (f32[]{:T(128)}, f32[256,512]{1,0:T(8,128)S(1)}) fusion(bf16[4096,512]{1,0:T(8,128)(2,1)} %bitcast.77, bf16[4096,256]{1,0:T(8,128)(2,1)S(1)} %bitcast.80, f32[4096]{0:T(1024)S(1)} %bitcast.94, f32[4096]{0:T(1024)S(1)} %bitcast.92, s32[4096]{0:T(1024)S(1)} %bitcast.90, bf16[1,16,8192]{2,1,0:T(8,128)(2,1)} %param.17, s32[]{:T(128)S(6)} %select_n.45), kind=kOutput, calls=%fused_computation.28 | convolution fusion | flops 1112997888 | bytes 6873096 | tf_op jit(solution)/shard_map/dot_general | solution.py:150
  159.5 2.0 collective-permute-start.1
  163.9 4.8 %collective-permute-start.2 = (f32[2]{0:T(128)S(1)}, f32[2]{0:T(128)S(1)}, u32[]{:S(2)}, u32[]{:S(2)}) collective-permute-start(f32[2]{0:T(128)S(1)} %fusion.56), channel_id=1, source_target_pairs={{0,2},{2,0},{4,6},{6,4},{8,10},{10,8},{12,14},{14,12},{16,18},{18,... | collective-permute-start | bytes 32 | tf_op jit(solution)/shard_map/ppermute | solution.py:47
  171.6 4.5 %collective-permute-start.3 = (f32[2]{0:T(128)S(1)}, f32[2]{0:T(128)S(1)}, u32[]{:S(2)}, u32[]{:S(2)}) collective-permute-start(f32[2]{0:T(128)S(1)} %fusion.57), channel_id=1, source_target_pairs={{0,4},{2,6},{4,0},{6,2},{8,12},{10,14},{12,8},{14,10},{16,20},{18,... | collective-permute-start | bytes 32 | tf_op jit(solution)/shard_map/ppermute | solution.py:47
  176.1 1.5 collective-permute-done.3
  177.6 5.8 %collective-permute-start.4 = (f32[2]{0:T(128)S(1)}, f32[2]{0:T(128)S(1)}, u32[]{:S(2)}, u32[]{:S(2)}) collective-permute-start(f32[2]{0:T(128)S(1)} %add.133), channel_id=1, source_target_pairs={{0,8},{2,10},{4,12},{6,14},{8,0},{10,2},{12,4},{14,6},{16,24},{18,... | collective-permute-start | bytes 32 | tf_op jit(solution)/shard_map/ppermute | solution.py:47
  185.0 2.2 collective-permute-start.5
  187.1 7.2 %collective-permute-done.5 = f32[2]{0:T(128)S(1)} collective-permute-done((f32[2]{0:T(128)S(1)}, f32[2]{0:T(128)S(1)}, u32[]{:S(2)}, u32[]{:S(2)}) %collective-permute-start.5) | collective-permute-done | bytes 40 | tf_op jit(solution)/shard_map/ppermute | solution.py:47
  199.2 3.0 %collective-permute-start.6 = (f32[2,2,2,8448]{3,2,1,0:T(2,128)S(1)}, f32[2,2,2,8448]{3,2,1,0:T(2,128)S(1)}, u32[]{:S(2)}, u32[]{:S(2)}) collective-permute-start(f32[2,2,2,8448]{3,2,1,0:T(2,128)S(1)} %dynamic-slice_bitcast_fusion), channel_id=1, source_target_pairs={{0,64},{32,96},{64,0},{96,32},{128,192},{160,224},{192,128},{224,1... | collective-permute-start | bytes 811016 | tf_op jit(solution)/shard_map/ppermute | solution.py:72
  202.2 5.4 %collective-permute-done.6 = f32[2,2,2,8448]{3,2,1,0:T(2,128)S(1)} collective-permute-done((f32[2,2,2,8448]{3,2,1,0:T(2,128)S(1)}, f32[2,2,2,8448]{3,2,1,0:T(2,128)S(1)}, u32[]{:S(2)}, u32[]{:S(2)}) %collective-permute-start.6) | collective-permute-done | bytes 270368 | tf_op jit(solution)/shard_map/ppermute | solution.py:72
  207.7 8.5 %collective-permute-start.7 = (f32[2,2,8448]{2,1,0:T(2,128)S(1)}, f32[2,2,8448]{2,1,0:T(2,128)S(1)}, u32[]{:S(2)}, u32[]{:S(2)}) collective-permute-start(f32[2,2,8448]{2,1,0:T(2,128)S(1)} %dynamic-slice_bitcast_fusion.1), channel_id=1, source_target_pairs={{0,128},{32,160},{64,192},{96,224},{128,0},{160,32},{192,64},{224,... | collective-permute-start | bytes 405512 | tf_op jit(solution)/shard_map/ppermute | solution.py:72
  216.2 4.4 %collective-permute-done.7 = f32[2,2,8448]{2,1,0:T(2,128)S(1)} collective-permute-done((f32[2,2,8448]{2,1,0:T(2,128)S(1)}, f32[2,2,8448]{2,1,0:T(2,128)S(1)}, u32[]{:S(2)}, u32[]{:S(2)}) %collective-permute-start.7) | collective-permute-done | bytes 135200 | tf_op jit(solution)/shard_map/ppermute | solution.py:72
  220.9 1.9 collective-permute-start.8
  222.8 5.8 %collective-permute-done.8 = f32[2,8448]{1,0:T(2,128)S(1)} collective-permute-done((f32[2,8448]{1,0:T(2,128)S(1)}, f32[2,8448]{1,0:T(2,128)S(1)}, u32[]{:S(2)}, u32[]{:S(2)}) %collective-permute-start.8) | collective-permute-done | bytes 67616 | tf_op jit(solution)/shard_map/ppermute | solution.py:72
  228.9 6.0 %collective-permute-start.9 = (f32[8448]{0:T(1024)S(1)}, f32[8448]{0:T(1024)S(1)}, u32[]{:S(2)}, u32[]{:S(2)}) collective-permute-start(f32[8448]{0:T(1024)S(1)} %get-tuple-element.20), channel_id=1, source_target_pairs={{0,256},{32,288},{64,320},{96,352},{128,384},{160,416},{192,448},{... | collective-permute-start | bytes 101384 | tf_op jit(solution)/shard_map/ppermute | solution.py:72
  234.9 3.7 %collective-permute-done.9 = f32[8448]{0:T(1024)S(1)} collective-permute-done((f32[8448]{0:T(1024)S(1)}, f32[8448]{0:T(1024)S(1)}, u32[]{:S(2)}, u32[]{:S(2)}) %collective-permute-start.9) | collective-permute-done | bytes 33824 | tf_op jit(solution)/shard_map/ppermute | solution.py:72
  (80 shorter events, 21.4 us)
Async XLA Ops:
  7.2 121.6 %all-gather.2.cloned.1.call-start = ((), (), s32[]{:S(2)}) async-start(), calls=%async_computation.1 | async-start | bytes 2228224 | tf_op jit(solution)/shard_map/all_gather | solution.py:127
  13.5 2.9 %copy-start.8 = (s32[128]{0:T(128)S(1)}, s32[128]{0:T(128)}, u32[]{:S(2)}) copy-start(s32[128]{0:T(128)} %param.12) | copy-start | bytes 1540
  13.5 2.9 %copy-start = (bf16[128,8192]{1,0:T(8,128)(2,1)S(1)}, bf16[128,8192]{1,0:T(8,128)(2,1)}, u32[]{:S(2)}) copy-start(bf16[128,8192]{1,0:T(8,128)(2,1)} %param.11) | copy-start | bytes 6291460
  32.2 98.7 %all-to-all-start = ((bf16[132,32,256]{2,0,1:T(8,128)(2,1)}), bf16[132,32,256]{2,0,1:T(8,128)(2,1)S(1)}, u32[]{:S(2)}, u32[]{:S(2)}) async-start(bf16[132,32,256]{2,0,1:T(8,128)(2,1)} %copy.84), calls=%async_computation | async-start | bytes 4456448 | tf_op jit(solution)/shard_map/all_to_all | solution.py:117
  128.8 6.4 %collective-permute-start = (bf16[2048,512]{0,1:T(8,128)(2,1)}, bf16[2048,512]{0,1:T(8,128)(2,1)}, u32[]{:S(2)}, u32[]{:S(2)}) collective-permute-start(bf16[2048,512]{0,1:T(8,128)(2,1)} %all-gather.2.cloned.1.call-done), channel_id=1, source_target_pairs={{0,1},{1,0},{2,3},{3,2},{4,5},{5,4},{6,7},{7,6},{8,9},{9,8},{10,11... | collective-permute-start | bytes 6291464 | tf_op jit(solution)/shard_map/ppermute | solution.py:128
  145.4 2.9 %copy-start.2 = (bf16[32,128,256]{2,1,0:T(8,128)(2,1)S(1)}, bf16[32,128,256]{2,1,0:T(8,128)(2,1)}, u32[]{:S(2)}) copy-start(bf16[32,128,256]{2,1,0:T(8,128)(2,1)} %slice.56) | copy-start | bytes 6291460
  145.4 2.9 %copy-start.3 = (bf16[1,256,512]{2,1,0:T(8,128)(2,1)S(1)}, bf16[1,256,512]{2,1,0:T(8,128)(2,1)}, u32[]{:S(2)}) copy-start(bf16[1,256,512]{2,1,0:T(8,128)(2,1)} %param.16) | copy-start | bytes 786436
  148.1 1.9 copy-start.1
  159.5 3.0 %collective-permute-start.1 = (f32[2]{0:T(128)S(1)}, f32[2]{0:T(128)S(1)}, u32[]{:S(2)}, u32[]{:S(2)}) collective-permute-start(f32[2]{0:T(128)S(1)} %pad_maximum_fusion.2), channel_id=1, source_target_pairs={{0,1},{1,0},{2,3},{3,2},{4,5},{5,4},{6,7},{7,6},{8,9},{9,8},{10,11... | collective-permute-start | bytes 32 | tf_op jit(solution)/shard_map/ppermute | solution.py:47
  163.9 6.3 %collective-permute-start.2 = (f32[2]{0:T(128)S(1)}, f32[2]{0:T(128)S(1)}, u32[]{:S(2)}, u32[]{:S(2)}) collective-permute-start(f32[2]{0:T(128)S(1)} %fusion.56), channel_id=1, source_target_pairs={{0,2},{2,0},{4,6},{6,4},{8,10},{10,8},{12,14},{14,12},{16,18},{18,... | collective-permute-start | bytes 32 | tf_op jit(solution)/shard_map/ppermute | solution.py:47
  171.6 6.1 %collective-permute-start.3 = (f32[2]{0:T(128)S(1)}, f32[2]{0:T(128)S(1)}, u32[]{:S(2)}, u32[]{:S(2)}) collective-permute-start(f32[2]{0:T(128)S(1)} %fusion.57), channel_id=1, source_target_pairs={{0,4},{2,6},{4,0},{6,2},{8,12},{10,14},{12,8},{14,10},{16,20},{18,... | collective-permute-start | bytes 32 | tf_op jit(solution)/shard_map/ppermute | solution.py:47
  177.6 7.3 %collective-permute-start.4 = (f32[2]{0:T(128)S(1)}, f32[2]{0:T(128)S(1)}, u32[]{:S(2)}, u32[]{:S(2)}) collective-permute-start(f32[2]{0:T(128)S(1)} %add.133), channel_id=1, source_target_pairs={{0,8},{2,10},{4,12},{6,14},{8,0},{10,2},{12,4},{14,6},{16,24},{18,... | collective-permute-start | bytes 32 | tf_op jit(solution)/shard_map/ppermute | solution.py:47
  185.0 9.4 %collective-permute-start.5 = (f32[2]{0:T(128)S(1)}, f32[2]{0:T(128)S(1)}, u32[]{:S(2)}, u32[]{:S(2)}) collective-permute-start(f32[2]{0:T(128)S(1)} %add.134), channel_id=1, source_target_pairs={{0,16},{2,18},{4,20},{6,22},{8,24},{10,26},{12,28},{14,30},{16,0},... | collective-permute-start | bytes 32 | tf_op jit(solution)/shard_map/ppermute | solution.py:47
  197.9 41.0 %copy-start.6 = (f32[1,256]{1,0:T(1,128)S(1)}, f32[1,256]{1,0:T(1,128)}, u32[]{:S(2)}) copy-start(f32[1,256]{1,0:T(1,128)} %param.20) | copy-start | bytes 3076
  197.9 41.0 %copy-start.7 = (f32[1,256]{1,0:T(1,128)S(1)}, f32[1,256]{1,0:T(1,128)}, u32[]{:S(2)}) copy-start(f32[1,256]{1,0:T(1,128)} %param.21) | copy-start | bytes 3076
  198.0 41.5 %copy-start.4 = (f32[256,32]{0,1:T(8,128)S(1)}, f32[256,32]{0,1:T(8,128)}, u32[]{:S(2)}) copy-start(f32[256,32]{0,1:T(8,128)} %param.18) | copy-start | bytes 98308
  198.0 41.5 %copy-start.5 = (f32[256,32]{0,1:T(8,128)S(1)}, f32[256,32]{0,1:T(8,128)}, u32[]{:S(2)}) copy-start(f32[256,32]{0,1:T(8,128)} %param.19) | copy-start | bytes 98308
  199.2 8.4 %collective-permute-start.6 = (f32[2,2,2,8448]{3,2,1,0:T(2,128)S(1)}, f32[2,2,2,8448]{3,2,1,0:T(2,128)S(1)}, u32[]{:S(2)}, u32[]{:S(2)}) collective-permute-start(f32[2,2,2,8448]{3,2,1,0:T(2,128)S(1)} %dynamic-slice_bitcast_fusion), channel_id=1, source_target_pairs={{0,64},{32,96},{64,0},{96,32},{128,192},{160,224},{192,128},{224,1... | collective-permute-start | bytes 811016 | tf_op jit(solution)/shard_map/ppermute | solution.py:72
  207.7 12.9 %collective-permute-start.7 = (f32[2,2,8448]{2,1,0:T(2,128)S(1)}, f32[2,2,8448]{2,1,0:T(2,128)S(1)}, u32[]{:S(2)}, u32[]{:S(2)}) collective-permute-start(f32[2,2,8448]{2,1,0:T(2,128)S(1)} %dynamic-slice_bitcast_fusion.1), channel_id=1, source_target_pairs={{0,128},{32,160},{64,192},{96,224},{128,0},{160,32},{192,64},{224,... | collective-permute-start | bytes 405512 | tf_op jit(solution)/shard_map/ppermute | solution.py:72
  220.9 7.7 %collective-permute-start.8 = (f32[2,8448]{1,0:T(2,128)S(1)}, f32[2,8448]{1,0:T(2,128)S(1)}, u32[]{:S(2)}, u32[]{:S(2)}) collective-permute-start(f32[2,8448]{1,0:T(2,128)S(1)} %bitcast.88), channel_id=1, source_target_pairs={{0,32},{32,0},{64,96},{96,64},{128,160},{160,128},{192,224},{224,1... | collective-permute-start | bytes 202760 | tf_op jit(solution)/shard_map/ppermute | solution.py:72
  228.9 9.8 %collective-permute-start.9 = (f32[8448]{0:T(1024)S(1)}, f32[8448]{0:T(1024)S(1)}, u32[]{:S(2)}, u32[]{:S(2)}) collective-permute-start(f32[8448]{0:T(1024)S(1)} %get-tuple-element.20), channel_id=1, source_target_pairs={{0,256},{32,288},{64,320},{96,352},{128,384},{160,416},{192,448},{... | collective-permute-start | bytes 101384 | tf_op jit(solution)/shard_map/ppermute | solution.py:72
Sparse Core Ops, SparseCore 0:
  16.5 112.1 all-gather.1

commit v5 on v3

--- a/solution.py
+++ b/solution.py
@@ -112,6 +112,10 @@
     flat = jnp.pad(flat, (0, stat_rows * col_block - flat.shape[0]))
     extra = jnp.broadcast_to(flat.reshape(stat_rows, 1, col_block), (stat_rows, fsdp_count, col_block))
     outgoing = jnp.concatenate([block_input.reshape(rows, fsdp_count, col_block), extra], axis=0)
+
+    values_grad = value_grad(queries, saved_keys, out_grad)
+    all_values = lax.all_gather(values_grad, "fsdp", axis=0, tiled=True)
+    all_values, outgoing = lax.optimization_barrier((all_values, outgoing))
     arrived = lax.all_to_all(outgoing, "fsdp", split_axis=1, concat_axis=0, tiled=True)
     arrived = arrived.reshape(fsdp_count, rows + stat_rows, col_block)
     col_input = arrived[:, :rows, :].reshape(fsdp_count * rows, col_block)
@@ -121,8 +125,6 @@
     all_inv_std = ((got[:, 3] + got[:, 4]) + got[:, 5]).reshape(-1)
     all_lang = got[:, 6].reshape(-1).astype(jnp.int32)
 
-    values_grad = value_grad(queries, saved_keys, out_grad)
-    all_values = lax.all_gather(values_grad, "fsdp", axis=0, tiled=True)
 
     standard = (col_input.astype(jnp.float32) - all_average[:, None]) * all_inv_std[:, None]
     lang_table = all_lang[None, :] == jnp.arange(lang_count, dtype=jnp.int32)[:, None]

time: 223 us -> 259 us (1.16)
  the two profiles are of different devices: /device:TPU:64 before, /device:TPU:14 now
where the time goes in v5:
time: 259 us; the launch traced here: 258 us
  waiting for transfers between devices  156 us (60%)
  starting transfers between devices  37.3 us (14%)
  local copies, waits for them, and re-layouts  19 us (7%)
  matrix products  17.3 us (7%)
  between operations  15.8 us (6%)
  other arithmetic  12.2 us (5%)
    all_gather x1, waiting for transfers between devices, body(): all_values = lax.all_gather(values_grad, 'fsdp', axis=0, tiled=True)  68.9 us
    all_to_all x1, waiting for transfers between devices, body(): lax.all_to_all(outgoing, 'fsdp', split_axis=1, concat_axis=0, tiled=True)  53.3 us
    ppermute x4, starting transfers between devices, halving_scatter(): grid = keep + lax.ppermute(send, axis, pairs)  19.7 us
    ppermute x5, waiting for transfers between devices, exchange_sum(): return part + lax.ppermute(part, axis, pairs)  18 us
    ppermute x4, waiting for transfers between devices, halving_scatter(): grid = keep + lax.ppermute(send, axis, pairs)  16.2 us
    ppermute x5, starting transfers between devices, exchange_sum(): return part + lax.ppermute(part, axis, pairs)  11.6 us
    all_to_all x1, starting transfers between devices, body(): lax.all_to_all(outgoing, 'fsdp', split_axis=1, concat_axis=0, tiled=True)  5.99 us
    dot_general x1, matrix products, body(): jnp.dot(normed.T, all_values, preferred_element_type=jnp.float32)  5.83 us
  transfers between devices with their start and end apart: 11, of which 11 were waited for; matrix products, arithmetic and copies ran while one was open for 4% of the time, Pallas kernels for 0%

profile of v5, /device:TPU:14, one launch (start us, length us, event | category | flops | bytes accessed | tf_op | source)
XLA Modules:
  0.0 258.0 jit_solution(13516860532821772962)
XLA Ops:
  7.2 1.4 copy.92
  9.6 1.6 copy.89
  11.3 2.3 fusion.45
  13.6 2.8 %fusion.8 = bf16[4,128,128]{1,2,0:T(8,128)(2,1)} fusion(bf16[128,4,8,128]{0,3,2,1:T(8,128)(2,1)S(1)} %bitcast.75, f32[4,8,128,128]{2,3,1,0:T(8,128)} %get-tuple-element.45, f32[4,8,128]{2,1,0:T(8,128)S(1)} %get-tuple-element.44), kind=kOutput, calls=%fused_computation.18 | convolution fusion | flops 135331840 | bytes 3293184 | tf_op jit(solution)/shard_map/kgts,tkgd->skd/dot_general | solution.py:40
  16.5 2.5 copy.78
  22.1 4.5 %pad_maximum_fusion = bf16[132,32,256]{0,2,1:T(8,128)(2,1)} fusion(bf16[4,32,256]{0,2,1:T(8,128)(2,1)S(1)} %broadcast_in_dim.28, bf16[128,32,256]{0,2,1:T(8,128)(2,1)} %bitcast.70), kind=kLoop, calls=%fused_computation.9 | loop fusion | flops 4325376 | bytes 4325376 | tf_op jit(solution)/shard_map/concatenate | solution.py:114
  26.6 68.9 %all-gather.2.cloned.1.call-done = bf16[4096,512]{0,1:T(8,128)(2,1)} async-done(((bf16[128,512]{0,1:T(8,128)(2,1)}), bf16[4096,512]{0,1:T(8,128)(2,1)}) %all-gather.2.cloned.1.call-update) | async-done | bytes 4194320 | tf_op jit(solution)/shard_map/all_gather | solution.py:117
  95.5 5.6 %copy.80 = bf16[132,32,256]{2,0,1:T(8,128)(2,1)} copy(bf16[132,32,256]{0,2,1:T(8,128)(2,1)} %pad_maximum_fusion) | data formatting | bytes 4325376 | tf_op jit(solution)/shard_map/optimization_barrier | solution.py:118
  101.2 6.0 %all-to-all-start = ((bf16[132,32,256]{2,0,1:T(8,128)(2,1)}), bf16[132,32,256]{2,0,1:T(8,128)(2,1)S(1)}, u32[]{:S(2)}, u32[]{:S(2)}) async-start(bf16[132,32,256]{2,0,1:T(8,128)(2,1)} %copy.80), calls=%async_computation | async-start | bytes 4456448 | tf_op jit(solution)/shard_map/all_to_all | solution.py:119
  107.2 53.3 %all-to-all-done = bf16[132,32,256]{2,0,1:T(8,128)(2,1)S(1)} async-done(((bf16[132,32,256]{2,0,1:T(8,128)(2,1)}), bf16[132,32,256]{2,0,1:T(8,128)(2,1)S(1)}, u32[]{:S(2)}, u32[]{:S(2)}) %all-to-all-start) | async-done | bytes 2162720 | tf_op jit(solution)/shard_map/all_to_all | solution.py:119
  160.5 1.6 slice.56
  162.2 4.3 %fusion.1 = f32[4096,256]{1,0:T(8,128)S(1)} fusion(bf16[4096,512]{0,1:T(8,128)(2,1)} %all-gather.2.cloned.1.call-done, bf16[4096,256]{1,0:T(8,128)(2,1)} %bitcast.72, f32[4096]{0:T(1024)S(1)} %bitcast.86, f32[4096]{0:T(1024)S(1)} %bitcast.84, bf16[1,256,512]{2,1,0:T(8,128)(2,1)S(1)} %copy-done.2), kind=kOutput, calls=%fused_computation.2 | convolution fusion | flops 1078984704 | bytes 10780672 | tf_op jit(solution)/shard_map/dot_general | solution.py:138
  166.5 2.1 multiply_reduce_fusion.1
  168.6 5.8 %multiply_reduce_fusion = (f32[]{:T(128)}, f32[256,512]{1,0:T(8,128)S(1)}) fusion(bf16[4096,512]{0,1:T(8,128)(2,1)} %all-gather.2.cloned.1.call-done, bf16[4096,256]{1,0:T(8,128)(2,1)S(1)} %bitcast.73, f32[4096]{0:T(1024)S(1)} %bitcast.87, f32[4096]{0:T(1024)S(1)} %bitcast.85, s32[4096]{0:T(1024)S(1)} %bitcast.83, bf16[1,16,8192]{2,1,0:T(8,128)(2,1)} %param.17, ...), kind=kOutput, calls=%fused_computation.25 | convolution fusion | flops 1112997888 | bytes 6873096 | tf_op jit(solution)/shard_map/dot_general | solution.py:143
  175.8 1.9 collective-permute-start
  180.2 2.4 collective-permute-start.1
  182.7 3.0 %collective-permute-done.1 = f32[2]{0:T(128)S(1)} collective-permute-done((f32[2]{0:T(128)S(1)}, f32[2]{0:T(128)S(1)}, u32[]{:S(2)}, u32[]{:S(2)}) %collective-permute-start.1) | collective-permute-done | bytes 40 | tf_op jit(solution)/shard_map/ppermute | solution.py:47
  185.7 1.4 fusion.57
  187.0 2.0 collective-permute-start.2
  189.1 3.4 %collective-permute-done.2 = f32[2]{0:T(128)S(1)} collective-permute-done((f32[2]{0:T(128)S(1)}, f32[2]{0:T(128)S(1)}, u32[]{:S(2)}, u32[]{:S(2)}) %collective-permute-start.2) | collective-permute-done | bytes 40 | tf_op jit(solution)/shard_map/ppermute | solution.py:47
  192.5 1.9 collective-permute-start.3
  194.4 4.4 %collective-permute-done.3 = f32[2]{0:T(128)S(1)} collective-permute-done((f32[2]{0:T(128)S(1)}, f32[2]{0:T(128)S(1)}, u32[]{:S(2)}, u32[]{:S(2)}) %collective-permute-start.3) | collective-permute-done | bytes 40 | tf_op jit(solution)/shard_map/ppermute | solution.py:47
  198.8 3.3 %collective-permute-start.4 = (f32[2]{0:T(128)S(1)}, f32[2]{0:T(128)S(1)}, u32[]{:S(2)}, u32[]{:S(2)}) collective-permute-start(f32[2]{0:T(128)S(1)} %add.130), channel_id=1, source_target_pairs={{0,16},{1,17},{2,18},{3,19},{4,20},{5,21},{6,22},{7,23},{8,24},{9,... | collective-permute-start | bytes 32 | tf_op jit(solution)/shard_map/ppermute | solution.py:47
  202.2 6.0 %collective-permute-done.4 = f32[2]{0:T(128)S(1)} collective-permute-done((f32[2]{0:T(128)S(1)}, f32[2]{0:T(128)S(1)}, u32[]{:S(2)}, u32[]{:S(2)}) %collective-permute-start.4) | collective-permute-done | bytes 40 | tf_op jit(solution)/shard_map/ppermute | solution.py:47
  213.1 3.6 %collective-permute-start.5 = (f32[2,2,2,8448]{3,2,1,0:T(2,128)S(1)}, f32[2,2,2,8448]{3,2,1,0:T(2,128)S(1)}, u32[]{:S(2)}, u32[]{:S(2)}) collective-permute-start(f32[2,2,2,8448]{3,2,1,0:T(2,128)S(1)} %dynamic-slice_bitcast_fusion), channel_id=1, source_target_pairs={{0,64},{32,96},{64,0},{96,32},{128,192},{160,224},{192,128},{224,1... | collective-permute-start | bytes 811016 | tf_op jit(solution)/shard_map/ppermute | solution.py:72
  216.6 4.8 %collective-permute-done.5 = f32[2,2,2,8448]{3,2,1,0:T(2,128)S(1)} collective-permute-done((f32[2,2,2,8448]{3,2,1,0:T(2,128)S(1)}, f32[2,2,2,8448]{3,2,1,0:T(2,128)S(1)}, u32[]{:S(2)}, u32[]{:S(2)}) %collective-permute-start.5) | collective-permute-done | bytes 270368 | tf_op jit(solution)/shard_map/ppermute | solution.py:72
  221.6 5.6 %collective-permute-start.6 = (f32[2,2,8448]{2,1,0:T(2,128)S(1)}, f32[2,2,8448]{2,1,0:T(2,128)S(1)}, u32[]{:S(2)}, u32[]{:S(2)}) collective-permute-start(f32[2,2,8448]{2,1,0:T(2,128)S(1)} %dynamic-slice_bitcast_fusion.1), channel_id=1, source_target_pairs={{0,128},{32,160},{64,192},{96,224},{128,0},{160,32},{192,64},{224,... | collective-permute-start | bytes 405512 | tf_op jit(solution)/shard_map/ppermute | solution.py:72
  227.3 4.4 %collective-permute-done.6 = f32[2,2,8448]{2,1,0:T(2,128)S(1)} collective-permute-done((f32[2,2,8448]{2,1,0:T(2,128)S(1)}, f32[2,2,8448]{2,1,0:T(2,128)S(1)}, u32[]{:S(2)}, u32[]{:S(2)}) %collective-permute-start.6) | collective-permute-done | bytes 135200 | tf_op jit(solution)/shard_map/ppermute | solution.py:72
  231.9 3.3 %collective-permute-start.7 = (f32[2,8448]{1,0:T(2,128)S(1)}, f32[2,8448]{1,0:T(2,128)S(1)}, u32[]{:S(2)}, u32[]{:S(2)}) collective-permute-start(f32[2,8448]{1,0:T(2,128)S(1)} %bitcast.81), channel_id=1, source_target_pairs={{0,32},{32,0},{64,96},{96,64},{128,160},{160,128},{192,224},{224,1... | collective-permute-start | bytes 202760 | tf_op jit(solution)/shard_map/ppermute | solution.py:72
  235.2 4.4 %collective-permute-done.7 = f32[2,8448]{1,0:T(2,128)S(1)} collective-permute-done((f32[2,8448]{1,0:T(2,128)S(1)}, f32[2,8448]{1,0:T(2,128)S(1)}, u32[]{:S(2)}, u32[]{:S(2)}) %collective-permute-start.7) | collective-permute-done | bytes 67616 | tf_op jit(solution)/shard_map/ppermute | solution.py:72
  239.9 7.2 %collective-permute-start.8 = (f32[8448]{0:T(1024)S(1)}, f32[8448]{0:T(1024)S(1)}, u32[]{:S(2)}, u32[]{:S(2)}) collective-permute-start(f32[8448]{0:T(1024)S(1)} %get-tuple-element.24), channel_id=1, source_target_pairs={{0,256},{32,288},{64,320},{96,352},{128,384},{160,416},{192,448},{... | collective-permute-start | bytes 101384 | tf_op jit(solution)/shard_map/ppermute | solution.py:72
  247.1 2.5 collective-permute-done.8
  (72 shorter events, 13.7 us)
Async XLA Ops:
  7.2 88.4 %all-gather.2.cloned.1.call-start = ((), (), s32[]{:S(2)}) async-start(), calls=%async_computation.1 | async-start | bytes 4325376 | tf_op jit(solution)/shard_map/all_gather | solution.py:117
  13.6 2.9 %copy-start.7 = (s32[128]{0:T(128)S(1)}, s32[128]{0:T(128)}, u32[]{:S(2)}) copy-start(s32[128]{0:T(128)} %param.12) | copy-start | bytes 1540
  13.6 2.9 %copy-start = (bf16[128,8192]{1,0:T(8,128)(2,1)S(1)}, bf16[128,8192]{1,0:T(8,128)(2,1)}, u32[]{:S(2)}) copy-start(bf16[128,8192]{1,0:T(8,128)(2,1)} %param.11) | copy-start | bytes 6291460
  101.2 61.0 %copy-start.2 = (bf16[1,256,512]{2,1,0:T(8,128)(2,1)S(1)}, bf16[1,256,512]{2,1,0:T(8,128)(2,1)}, u32[]{:S(2)}) copy-start(bf16[1,256,512]{2,1,0:T(8,128)(2,1)} %param.16) | copy-start | bytes 786436
  101.2 59.3 %all-to-all-start = ((bf16[132,32,256]{2,0,1:T(8,128)(2,1)}), bf16[132,32,256]{2,0,1:T(8,128)(2,1)S(1)}, u32[]{:S(2)}, u32[]{:S(2)}) async-start(bf16[132,32,256]{2,0,1:T(8,128)(2,1)} %copy.80), calls=%async_computation | async-start | bytes 4456448 | tf_op jit(solution)/shard_map/all_to_all | solution.py:119
  166.5 2.1 copy-start.1
  175.8 3.0 %collective-permute-start = (f32[2]{0:T(128)S(1)}, f32[2]{0:T(128)S(1)}, u32[]{:S(2)}, u32[]{:S(2)}) collective-permute-start(f32[2]{0:T(128)S(1)} %pad_maximum_fusion.1), channel_id=1, source_target_pairs={{0,1},{1,0},{2,3},{3,2},{4,5},{5,4},{6,7},{7,6},{8,9},{9,8},{10,11... | collective-permute-start | bytes 32 | tf_op jit(solution)/shard_map/ppermute | solution.py:47
  180.2 5.5 %collective-permute-start.1 = (f32[2]{0:T(128)S(1)}, f32[2]{0:T(128)S(1)}, u32[]{:S(2)}, u32[]{:S(2)}) collective-permute-start(f32[2]{0:T(128)S(1)} %fusion.56), channel_id=1, source_target_pairs={{0,2},{1,3},{2,0},{3,1},{4,6},{5,7},{6,4},{7,5},{8,10},{9,11},{10,... | collective-permute-start | bytes 32 | tf_op jit(solution)/shard_map/ppermute | solution.py:47
  187.0 5.5 %collective-permute-start.2 = (f32[2]{0:T(128)S(1)}, f32[2]{0:T(128)S(1)}, u32[]{:S(2)}, u32[]{:S(2)}) collective-permute-start(f32[2]{0:T(128)S(1)} %fusion.57), channel_id=1, source_target_pairs={{0,4},{1,5},{2,6},{3,7},{4,0},{5,1},{6,2},{7,3},{8,12},{9,13},{10,... | collective-permute-start | bytes 32 | tf_op jit(solution)/shard_map/ppermute | solution.py:47
  192.5 6.3 %collective-permute-start.3 = (f32[2]{0:T(128)S(1)}, f32[2]{0:T(128)S(1)}, u32[]{:S(2)}, u32[]{:S(2)}) collective-permute-start(f32[2]{0:T(128)S(1)} %add.129), channel_id=1, source_target_pairs={{0,8},{1,9},{2,10},{3,11},{4,12},{5,13},{6,14},{7,15},{8,0},{9,1},... | collective-permute-start | bytes 32 | tf_op jit(solution)/shard_map/ppermute | solution.py:47
  198.8 9.4 %collective-permute-start.4 = (f32[2]{0:T(128)S(1)}, f32[2]{0:T(128)S(1)}, u32[]{:S(2)}, u32[]{:S(2)}) collective-permute-start(f32[2]{0:T(128)S(1)} %add.130), channel_id=1, source_target_pairs={{0,16},{1,17},{2,18},{3,19},{4,20},{5,21},{6,22},{7,23},{8,24},{9,... | collective-permute-start | bytes 32 | tf_op jit(solution)/shard_map/ppermute | solution.py:47
  211.8 38.1 %copy-start.5 = (f32[1,256]{1,0:T(1,128)S(1)}, f32[1,256]{1,0:T(1,128)}, u32[]{:S(2)}) copy-start(f32[1,256]{1,0:T(1,128)} %param.20) | copy-start | bytes 3076
  211.8 38.1 %copy-start.6 = (f32[1,256]{1,0:T(1,128)S(1)}, f32[1,256]{1,0:T(1,128)}, u32[]{:S(2)}) copy-start(f32[1,256]{1,0:T(1,128)} %param.21) | copy-start | bytes 3076
  211.8 38.7 %copy-start.3 = (f32[256,32]{0,1:T(8,128)S(1)}, f32[256,32]{0,1:T(8,128)}, u32[]{:S(2)}) copy-start(f32[256,32]{0,1:T(8,128)} %param.18) | copy-start | bytes 98308
  211.8 38.7 %copy-start.4 = (f32[256,32]{0,1:T(8,128)S(1)}, f32[256,32]{0,1:T(8,128)}, u32[]{:S(2)}) copy-start(f32[256,32]{0,1:T(8,128)} %param.19) | copy-start | bytes 98308
  213.1 8.4 %collective-permute-start.5 = (f32[2,2,2,8448]{3,2,1,0:T(2,128)S(1)}, f32[2,2,2,8448]{3,2,1,0:T(2,128)S(1)}, u32[]{:S(2)}, u32[]{:S(2)}) collective-permute-start(f32[2,2,2,8448]{3,2,1,0:T(2,128)S(1)} %dynamic-slice_bitcast_fusion), channel_id=1, source_target_pairs={{0,64},{32,96},{64,0},{96,32},{128,192},{160,224},{192,128},{224,1... | collective-permute-start | bytes 811016 | tf_op jit(solution)/shard_map/ppermute | solution.py:72
  221.6 10.1 %collective-permute-start.6 = (f32[2,2,8448]{2,1,0:T(2,128)S(1)}, f32[2,2,8448]{2,1,0:T(2,128)S(1)}, u32[]{:S(2)}, u32[]{:S(2)}) collective-permute-start(f32[2,2,8448]{2,1,0:T(2,128)S(1)} %dynamic-slice_bitcast_fusion.1), channel_id=1, source_target_pairs={{0,128},{32,160},{64,192},{96,224},{128,0},{160,32},{192,64},{224,... | collective-permute-start | bytes 405512 | tf_op jit(solution)/shard_map/ppermute | solution.py:72
  231.9 7.7 %collective-permute-start.7 = (f32[2,8448]{1,0:T(2,128)S(1)}, f32[2,8448]{1,0:T(2,128)S(1)}, u32[]{:S(2)}, u32[]{:S(2)}) collective-permute-start(f32[2,8448]{1,0:T(2,128)S(1)} %bitcast.81), channel_id=1, source_target_pairs={{0,32},{32,0},{64,96},{96,64},{128,160},{160,128},{192,224},{224,1... | collective-permute-start | bytes 202760 | tf_op jit(solution)/shard_map/ppermute | solution.py:72
  239.9 9.8 %collective-permute-start.8 = (f32[8448]{0:T(1024)S(1)}, f32[8448]{0:T(1024)S(1)}, u32[]{:S(2)}, u32[]{:S(2)}) collective-permute-start(f32[8448]{0:T(1024)S(1)} %get-tuple-element.24), channel_id=1, source_target_pairs={{0,256},{32,288},{64,320},{96,352},{128,384},{160,416},{192,448},{... | collective-permute-start | bytes 101384 | tf_op jit(solution)/shard_map/ppermute | solution.py:72
Sparse Core Ops, SparseCore 0:
  16.6 78.9 all-gather.1

commit v6 on v3

--- a/solution.py
+++ b/solution.py
@@ -122,7 +122,8 @@
     all_lang = got[:, 6].reshape(-1).astype(jnp.int32)
 
     values_grad = value_grad(queries, saved_keys, out_grad)
-    all_values = lax.all_gather(values_grad, "fsdp", axis=0, tiled=True)
+    all_values = lax.all_gather(values_grad[None], "fsdp", axis=0, tiled=True)
+    all_values = all_values.reshape(fsdp_count * values_grad.shape[0], kv_width)
 
     standard = (col_input.astype(jnp.float32) - all_average[:, None]) * all_inv_std[:, None]
     lang_table = all_lang[None, :] == jnp.arange(lang_count, dtype=jnp.int32)[:, None]

time: 223 us -> 212 us (0.951)
  the two profiles are of different devices: /device:TPU:64 before, /device:TPU:4 now
where the time goes in v6:
time: 212 us; the launch traced here: 211 us
  waiting for transfers between devices  102 us (48%)
  starting transfers between devices  44.6 us (21%)
  local copies, waits for them, and re-layouts  19.8 us (9%)
  matrix products  16.1 us (8%)
  between operations  15.8 us (7%)
  other arithmetic  12.2 us (6%)
    all_to_all x1, waiting for transfers between devices, body(): lax.all_to_all(outgoing, 'fsdp', split_axis=1, concat_axis=0, tiled=True)  71.1 us
    ppermute x4, starting transfers between devices, halving_scatter(): grid = keep + lax.ppermute(send, axis, pairs)  18.8 us
    ppermute x4, waiting for transfers between devices, halving_scatter(): grid = keep + lax.ppermute(send, axis, pairs)  17.5 us
    ppermute x5, starting transfers between devices, exchange_sum(): return part + lax.ppermute(part, axis, pairs)  17.3 us
    ppermute x5, waiting for transfers between devices, exchange_sum(): return part + lax.ppermute(part, axis, pairs)  12.3 us
    all_to_all x1, starting transfers between devices, body(): lax.all_to_all(outgoing, 'fsdp', split_axis=1, concat_axis=0, tiled=True)  8.44 us
    dot_general x1, matrix products, body(): jnp.dot(normed.T, all_values, preferred_element_type=jnp.float32)  5.95 us
    concatenate x1, local copies, waits for them, and re-layouts, body(): jnp.concatenate([block_input.reshape(rows, fsdp_count, col_block), extra]...  5.64 us
  transfers between devices with their start and end apart: 11, of which 11 were waited for; matrix products, arithmetic and copies ran while one was open for 8% of the time, Pallas kernels for 0%

profile of v6, /device:TPU:4, one launch (start us, length us, event | category | flops | bytes accessed | tf_op | source)
XLA Modules:
  0.0 210.7 jit_solution(11883646439309489514)
XLA Ops:
  7.2 1.4 copy.98
  9.6 1.6 copy.94
  11.3 2.3 %fusion.45 = (f32[4,8,128]{2,1,0:T(8,128)S(1)}, f32[4,8,128,128]{2,3,1,0:T(8,128)}) fusion(pred[128,128]{0,1:T(8,128)(4,1)S(1)} %iota_compare_fusion.4, bf16[128,4,8,128]{3,2,1,0:T(8,128)(2,1)S(1)} %bitcast.77, bf16[128,4,128,1]{2,1,0,3:T(4,128)(2,1)S(1)} %bitcast.80), kind=kOutput, calls=%fused_computation.80 | convolution fusion | flops 136315008 | bytes 3309568 | tf_op jit(solution)/shard_map/sub | solution.py:37
  13.6 2.2 %fusion.8 = bf16[4,128,128]{1,2,0:T(8,128)(2,1)S(1)} fusion(bf16[128,4,8,128]{0,3,2,1:T(8,128)(2,1)S(1)} %bitcast.76, f32[4,8,128,128]{2,3,1,0:T(8,128)} %get-tuple-element.41, f32[4,8,128]{2,1,0:T(8,128)S(1)} %get-tuple-element.40), kind=kOutput, calls=%fused_computation.18 | convolution fusion | flops 135331840 | bytes 3293184 | tf_op jit(solution)/shard_map/kgts,tkgd->skd/dot_general | solution.py:40
  16.6 2.5 %copy.78 = bf16[128,8192]{0,1:T(8,128)(2,1)} copy(bf16[128,8192]{1,0:T(8,128)(2,1)S(1)} %copy-done) | data formatting | bytes 4194304 | tf_op args[0]
  22.2 4.5 %pad_maximum_fusion = bf16[132,32,256]{0,2,1:T(8,128)(2,1)} fusion(bf16[4,32,256]{0,2,1:T(8,128)(2,1)S(1)} %broadcast_in_dim.15, bf16[128,32,256]{0,2,1:T(8,128)(2,1)} %bitcast.71), kind=kLoop, calls=%fused_computation.9 | loop fusion | flops 4325376 | bytes 4325376 | tf_op jit(solution)/shard_map/concatenate | solution.py:114
  26.8 5.6 %copy.80 = bf16[132,32,256]{2,0,1:T(8,128)(2,1)} copy(bf16[132,32,256]{0,2,1:T(8,128)(2,1)} %pad_maximum_fusion) | data formatting | bytes 4325376 | tf_op jit(solution)/shard_map/concatenate | solution.py:114
  32.4 8.4 %all-to-all-start = ((bf16[132,32,256]{2,0,1:T(8,128)(2,1)}), bf16[132,32,256]{2,0,1:T(8,128)(2,1)S(1)}, u32[]{:S(2)}, u32[]{:S(2)}) async-start(bf16[132,32,256]{2,0,1:T(8,128)(2,1)} %copy.80), calls=%async_computation | async-start | bytes 4456448 | tf_op jit(solution)/shard_map/all_to_all | solution.py:115
  40.9 71.1 %all-to-all-done = bf16[132,32,256]{2,0,1:T(8,128)(2,1)S(1)} async-done(((bf16[132,32,256]{2,0,1:T(8,128)(2,1)}), bf16[132,32,256]{2,0,1:T(8,128)(2,1)S(1)}, u32[]{:S(2)}, u32[]{:S(2)}) %all-to-all-start) | async-done | bytes 2162720 | tf_op jit(solution)/shard_map/all_to_all | solution.py:115
  112.0 1.6 slice.56
  113.7 1.4 all-gather.2.cloned.1.call-done
  115.1 3.6 %fusion.1 = f32[4096,256]{1,0:T(8,128)S(1)} fusion(bf16[4096,512]{1,0:T(8,128)(2,1)} %bitcast.89, bf16[4096,256]{1,0:T(8,128)(2,1)} %bitcast.73, f32[4096]{0:T(1024)S(1)} %bitcast.87, f32[4096]{0:T(1024)S(1)} %bitcast.85, bf16[1,256,512]{2,1,0:T(8,128)(2,1)S(1)} %copy-done.2), kind=kOutput, calls=%fused_computation.2 | convolution fusion | flops 1078984704 | bytes 10780672 | tf_op jit(solution)/shard_map/dot_general | solution.py:137
  118.7 2.1 multiply_reduce_fusion.1
  120.8 6.0 %multiply_reduce_fusion = (f32[]{:T(128)}, f32[256,512]{1,0:T(8,128)S(1)}) fusion(bf16[4096,512]{1,0:T(8,128)(2,1)} %bitcast.90, bf16[4096,256]{1,0:T(8,128)(2,1)S(1)} %bitcast.74, f32[4096]{0:T(1024)S(1)} %bitcast.88, f32[4096]{0:T(1024)S(1)} %bitcast.86, s32[4096]{0:T(1024)S(1)} %bitcast.84, bf16[1,16,8192]{2,1,0:T(8,128)(2,1)} %param.17, s32[]{:T(128)S(6)} %select_n.35), kind=kOutput, calls=%fused_computation.25 | convolution fusion | flops 1112997888 | bytes 6873096 | tf_op jit(solution)/shard_map/dot_general | solution.py:142
  128.1 2.1 %collective-permute-start = (f32[2]{0:T(128)S(1)}, f32[2]{0:T(128)S(1)}, u32[]{:S(2)}, u32[]{:S(2)}) collective-permute-start(f32[2]{0:T(128)S(1)} %pad_maximum_fusion.1), channel_id=1, source_target_pairs={{0,1},{1,0},{2,3},{3,2},{4,5},{5,4},{6,7},{7,6},{8,9},{9,8},{10,11... | collective-permute-start | bytes 32 | tf_op jit(solution)/shard_map/ppermute | solution.py:47
  132.5 2.3 %collective-permute-start.1 = (f32[2]{0:T(128)S(1)}, f32[2]{0:T(128)S(1)}, u32[]{:S(2)}, u32[]{:S(2)}) collective-permute-start(f32[2]{0:T(128)S(1)} %fusion.56), channel_id=1, source_target_pairs={{0,2},{1,3},{2,0},{3,1},{4,6},{5,7},{6,4},{7,5},{8,10},{9,11},{10,... | collective-permute-start | bytes 32 | tf_op jit(solution)/shard_map/ppermute | solution.py:47
  134.8 3.2 %collective-permute-done.1 = f32[2]{0:T(128)S(1)} collective-permute-done((f32[2]{0:T(128)S(1)}, f32[2]{0:T(128)S(1)}, u32[]{:S(2)}, u32[]{:S(2)}) %collective-permute-start.1) | collective-permute-done | bytes 40 | tf_op jit(solution)/shard_map/ppermute | solution.py:47
  138.0 1.4 fusion.57
  139.3 3.1 %collective-permute-start.2 = (f32[2]{0:T(128)S(1)}, f32[2]{0:T(128)S(1)}, u32[]{:S(2)}, u32[]{:S(2)}) collective-permute-start(f32[2]{0:T(128)S(1)} %fusion.57), channel_id=1, source_target_pairs={{0,4},{1,5},{2,6},{3,7},{4,0},{5,1},{6,2},{7,3},{8,12},{9,13},{10,... | collective-permute-start | bytes 32 | tf_op jit(solution)/shard_map/ppermute | solution.py:47
  142.5 2.3 %collective-permute-done.2 = f32[2]{0:T(128)S(1)} collective-permute-done((f32[2]{0:T(128)S(1)}, f32[2]{0:T(128)S(1)}, u32[]{:S(2)}, u32[]{:S(2)}) %collective-permute-start.2) | collective-permute-done | bytes 40 | tf_op jit(solution)/shard_map/ppermute | solution.py:47
  144.8 3.8 %collective-permute-start.3 = (f32[2]{0:T(128)S(1)}, f32[2]{0:T(128)S(1)}, u32[]{:S(2)}, u32[]{:S(2)}) collective-permute-start(f32[2]{0:T(128)S(1)} %add.129), channel_id=1, source_target_pairs={{0,8},{1,9},{2,10},{3,11},{4,12},{5,13},{6,14},{7,15},{8,0},{9,1},... | collective-permute-start | bytes 32 | tf_op jit(solution)/shard_map/ppermute | solution.py:47
  148.6 2.5 %collective-permute-done.3 = f32[2]{0:T(128)S(1)} collective-permute-done((f32[2]{0:T(128)S(1)}, f32[2]{0:T(128)S(1)}, u32[]{:S(2)}, u32[]{:S(2)}) %collective-permute-start.3) | collective-permute-done | bytes 40 | tf_op jit(solution)/shard_map/ppermute | solution.py:47
  151.1 6.0 %collective-permute-start.4 = (f32[2]{0:T(128)S(1)}, f32[2]{0:T(128)S(1)}, u32[]{:S(2)}, u32[]{:S(2)}) collective-permute-start(f32[2]{0:T(128)S(1)} %add.130), channel_id=1, source_target_pairs={{0,16},{1,17},{2,18},{3,19},{4,20},{5,21},{6,22},{7,23},{8,24},{9,... | collective-permute-start | bytes 32 | tf_op jit(solution)/shard_map/ppermute | solution.py:47
  157.1 3.4 %collective-permute-done.4 = f32[2]{0:T(128)S(1)} collective-permute-done((f32[2]{0:T(128)S(1)}, f32[2]{0:T(128)S(1)}, u32[]{:S(2)}, u32[]{:S(2)}) %collective-permute-start.4) | collective-permute-done | bytes 40 | tf_op jit(solution)/shard_map/ppermute | solution.py:47
  165.4 3.0 %collective-permute-start.5 = (f32[2,2,2,8448]{3,2,1,0:T(2,128)S(1)}, f32[2,2,2,8448]{3,2,1,0:T(2,128)S(1)}, u32[]{:S(2)}, u32[]{:S(2)}) collective-permute-start(f32[2,2,2,8448]{3,2,1,0:T(2,128)S(1)} %dynamic-slice_bitcast_fusion), channel_id=1, source_target_pairs={{0,64},{32,96},{64,0},{96,32},{128,192},{160,224},{192,128},{224,1... | collective-permute-start | bytes 811016 | tf_op jit(solution)/shard_map/ppermute | solution.py:72
  168.4 5.3 %collective-permute-done.5 = f32[2,2,2,8448]{3,2,1,0:T(2,128)S(1)} collective-permute-done((f32[2,2,2,8448]{3,2,1,0:T(2,128)S(1)}, f32[2,2,2,8448]{3,2,1,0:T(2,128)S(1)}, u32[]{:S(2)}, u32[]{:S(2)}) %collective-permute-start.5) | collective-permute-done | bytes 270368 | tf_op jit(solution)/shard_map/ppermute | solution.py:72
  173.9 6.0 %collective-permute-start.6 = (f32[2,2,8448]{2,1,0:T(2,128)S(1)}, f32[2,2,8448]{2,1,0:T(2,128)S(1)}, u32[]{:S(2)}, u32[]{:S(2)}) collective-permute-start(f32[2,2,8448]{2,1,0:T(2,128)S(1)} %dynamic-slice_bitcast_fusion.1), channel_id=1, source_target_pairs={{0,128},{32,160},{64,192},{96,224},{128,0},{160,32},{192,64},{224,... | collective-permute-start | bytes 405512 | tf_op jit(solution)/shard_map/ppermute | solution.py:72
  179.9 4.4 %collective-permute-done.6 = f32[2,2,8448]{2,1,0:T(2,128)S(1)} collective-permute-done((f32[2,2,8448]{2,1,0:T(2,128)S(1)}, f32[2,2,8448]{2,1,0:T(2,128)S(1)}, u32[]{:S(2)}, u32[]{:S(2)}) %collective-permute-start.6) | collective-permute-done | bytes 135200 | tf_op jit(solution)/shard_map/ppermute | solution.py:72
  184.6 2.1 %collective-permute-start.7 = (f32[2,8448]{1,0:T(2,128)S(1)}, f32[2,8448]{1,0:T(2,128)S(1)}, u32[]{:S(2)}, u32[]{:S(2)}) collective-permute-start(f32[2,8448]{1,0:T(2,128)S(1)} %bitcast.82), channel_id=1, source_target_pairs={{0,32},{32,0},{64,96},{96,64},{128,160},{160,128},{192,224},{224,1... | collective-permute-start | bytes 202760 | tf_op jit(solution)/shard_map/ppermute | solution.py:72
  186.7 5.5 %collective-permute-done.7 = f32[2,8448]{1,0:T(2,128)S(1)} collective-permute-done((f32[2,8448]{1,0:T(2,128)S(1)}, f32[2,8448]{1,0:T(2,128)S(1)}, u32[]{:S(2)}, u32[]{:S(2)}) %collective-permute-start.7) | collective-permute-done | bytes 67616 | tf_op jit(solution)/shard_map/ppermute | solution.py:72
  192.5 7.6 %collective-permute-start.8 = (f32[8448]{0:T(1024)S(1)}, f32[8448]{0:T(1024)S(1)}, u32[]{:S(2)}, u32[]{:S(2)}) collective-permute-start(f32[8448]{0:T(1024)S(1)} %get-tuple-element.20), channel_id=1, source_target_pairs={{0,256},{32,288},{64,320},{96,352},{128,384},{160,416},{192,448},{... | collective-permute-start | bytes 101384 | tf_op jit(solution)/shard_map/ppermute | solution.py:72
  200.1 2.2 %collective-permute-done.8 = f32[8448]{0:T(1024)S(1)} collective-permute-done((f32[8448]{0:T(1024)S(1)}, f32[8448]{0:T(1024)S(1)}, u32[]{:S(2)}, u32[]{:S(2)}) %collective-permute-start.8) | collective-permute-done | bytes 33824 | tf_op jit(solution)/shard_map/ppermute | solution.py:72
  (73 shorter events, 14.3 us)
Async XLA Ops:
  7.2 108.0 %all-gather.2.cloned.1.call-start = ((), (), s32[]{:S(2)}) async-start(), calls=%async_computation.1 | async-start | bytes 4325376 | tf_op jit(solution)/shard_map/all_gather | solution.py:125
  13.6 3.0 %copy-start.7 = (s32[128]{0:T(128)S(1)}, s32[128]{0:T(128)}, u32[]{:S(2)}) copy-start(s32[128]{0:T(128)} %param.12) | copy-start | bytes 1540
  13.6 3.0 %copy-start = (bf16[128,8192]{1,0:T(8,128)(2,1)S(1)}, bf16[128,8192]{1,0:T(8,128)(2,1)}, u32[]{:S(2)}) copy-start(bf16[128,8192]{1,0:T(8,128)(2,1)} %param.11) | copy-start | bytes 6291460
  32.4 82.7 %copy-start.2 = (bf16[1,256,512]{2,1,0:T(8,128)(2,1)S(1)}, bf16[1,256,512]{2,1,0:T(8,128)(2,1)}, u32[]{:S(2)}) copy-start(bf16[1,256,512]{2,1,0:T(8,128)(2,1)} %param.16) | copy-start | bytes 786436
  32.4 79.6 %all-to-all-start = ((bf16[132,32,256]{2,0,1:T(8,128)(2,1)}), bf16[132,32,256]{2,0,1:T(8,128)(2,1)S(1)}, u32[]{:S(2)}, u32[]{:S(2)}) async-start(bf16[132,32,256]{2,0,1:T(8,128)(2,1)} %copy.80), calls=%async_computation | async-start | bytes 4456448 | tf_op jit(solution)/shard_map/all_to_all | solution.py:115
  118.7 2.1 copy-start.1
  128.1 3.0 %collective-permute-start = (f32[2]{0:T(128)S(1)}, f32[2]{0:T(128)S(1)}, u32[]{:S(2)}, u32[]{:S(2)}) collective-permute-start(f32[2]{0:T(128)S(1)} %pad_maximum_fusion.1), channel_id=1, source_target_pairs={{0,1},{1,0},{2,3},{3,2},{4,5},{5,4},{6,7},{7,6},{8,9},{9,8},{10,11... | collective-permute-start | bytes 32 | tf_op jit(solution)/shard_map/ppermute | solution.py:47
  132.5 5.5 %collective-permute-start.1 = (f32[2]{0:T(128)S(1)}, f32[2]{0:T(128)S(1)}, u32[]{:S(2)}, u32[]{:S(2)}) collective-permute-start(f32[2]{0:T(128)S(1)} %fusion.56), channel_id=1, source_target_pairs={{0,2},{1,3},{2,0},{3,1},{4,6},{5,7},{6,4},{7,5},{8,10},{9,11},{10,... | collective-permute-start | bytes 32 | tf_op jit(solution)/shard_map/ppermute | solution.py:47
  139.3 5.5 %collective-permute-start.2 = (f32[2]{0:T(128)S(1)}, f32[2]{0:T(128)S(1)}, u32[]{:S(2)}, u32[]{:S(2)}) collective-permute-start(f32[2]{0:T(128)S(1)} %fusion.57), channel_id=1, source_target_pairs={{0,4},{1,5},{2,6},{3,7},{4,0},{5,1},{6,2},{7,3},{8,12},{9,13},{10,... | collective-permute-start | bytes 32 | tf_op jit(solution)/shard_map/ppermute | solution.py:47
  144.8 6.3 %collective-permute-start.3 = (f32[2]{0:T(128)S(1)}, f32[2]{0:T(128)S(1)}, u32[]{:S(2)}, u32[]{:S(2)}) collective-permute-start(f32[2]{0:T(128)S(1)} %add.129), channel_id=1, source_target_pairs={{0,8},{1,9},{2,10},{3,11},{4,12},{5,13},{6,14},{7,15},{8,0},{9,1},... | collective-permute-start | bytes 32 | tf_op jit(solution)/shard_map/ppermute | solution.py:47
  151.1 9.4 %collective-permute-start.4 = (f32[2]{0:T(128)S(1)}, f32[2]{0:T(128)S(1)}, u32[]{:S(2)}, u32[]{:S(2)}) collective-permute-start(f32[2]{0:T(128)S(1)} %add.130), channel_id=1, source_target_pairs={{0,16},{1,17},{2,18},{3,19},{4,20},{5,21},{6,22},{7,23},{8,24},{9,... | collective-permute-start | bytes 32 | tf_op jit(solution)/shard_map/ppermute | solution.py:47
  164.1 38.6 %copy-start.5 = (f32[1,256]{1,0:T(1,128)S(1)}, f32[1,256]{1,0:T(1,128)}, u32[]{:S(2)}) copy-start(f32[1,256]{1,0:T(1,128)} %param.20) | copy-start | bytes 3076
  164.1 38.6 %copy-start.6 = (f32[1,256]{1,0:T(1,128)S(1)}, f32[1,256]{1,0:T(1,128)}, u32[]{:S(2)}) copy-start(f32[1,256]{1,0:T(1,128)} %param.21) | copy-start | bytes 3076
  164.1 39.1 %copy-start.3 = (f32[256,32]{0,1:T(8,128)S(1)}, f32[256,32]{0,1:T(8,128)}, u32[]{:S(2)}) copy-start(f32[256,32]{0,1:T(8,128)} %param.18) | copy-start | bytes 98308
  164.1 39.1 %copy-start.4 = (f32[256,32]{0,1:T(8,128)S(1)}, f32[256,32]{0,1:T(8,128)}, u32[]{:S(2)}) copy-start(f32[256,32]{0,1:T(8,128)} %param.19) | copy-start | bytes 98308
  165.4 8.4 %collective-permute-start.5 = (f32[2,2,2,8448]{3,2,1,0:T(2,128)S(1)}, f32[2,2,2,8448]{3,2,1,0:T(2,128)S(1)}, u32[]{:S(2)}, u32[]{:S(2)}) collective-permute-start(f32[2,2,2,8448]{3,2,1,0:T(2,128)S(1)} %dynamic-slice_bitcast_fusion), channel_id=1, source_target_pairs={{0,64},{32,96},{64,0},{96,32},{128,192},{160,224},{192,128},{224,1... | collective-permute-start | bytes 811016 | tf_op jit(solution)/shard_map/ppermute | solution.py:72
  173.9 10.4 %collective-permute-start.6 = (f32[2,2,8448]{2,1,0:T(2,128)S(1)}, f32[2,2,8448]{2,1,0:T(2,128)S(1)}, u32[]{:S(2)}, u32[]{:S(2)}) collective-permute-start(f32[2,2,8448]{2,1,0:T(2,128)S(1)} %dynamic-slice_bitcast_fusion.1), channel_id=1, source_target_pairs={{0,128},{32,160},{64,192},{96,224},{128,0},{160,32},{192,64},{224,... | collective-permute-start | bytes 405512 | tf_op jit(solution)/shard_map/ppermute | solution.py:72
  184.6 7.7 %collective-permute-start.7 = (f32[2,8448]{1,0:T(2,128)S(1)}, f32[2,8448]{1,0:T(2,128)S(1)}, u32[]{:S(2)}, u32[]{:S(2)}) collective-permute-start(f32[2,8448]{1,0:T(2,128)S(1)} %bitcast.82), channel_id=1, source_target_pairs={{0,32},{32,0},{64,96},{96,64},{128,160},{160,128},{192,224},{224,1... | collective-permute-start | bytes 202760 | tf_op jit(solution)/shard_map/ppermute | solution.py:72
  192.5 9.9 %collective-permute-start.8 = (f32[8448]{0:T(1024)S(1)}, f32[8448]{0:T(1024)S(1)}, u32[]{:S(2)}, u32[]{:S(2)}) collective-permute-start(f32[8448]{0:T(1024)S(1)} %get-tuple-element.20), channel_id=1, source_target_pairs={{0,256},{32,288},{64,320},{96,352},{128,384},{160,416},{192,448},{... | collective-permute-start | bytes 101384 | tf_op jit(solution)/shard_map/ppermute | solution.py:72
Sparse Core Ops, SparseCore 0:
  16.7 98.3 all-gather.1

commit v7 on v5

--- a/solution.py
+++ b/solution.py
@@ -107,24 +107,20 @@
     rows = block_input.shape[0]
     average, inv_std = row_stats(block_input)
     parts = split_three(average) + split_three(inv_std) + [lang_ids.astype(jnp.bfloat16)]
-    stat_rows = -(-len(parts) * rows // col_block)
+    stat_rows = -(-len(parts) * rows // kv_width)
     flat = jnp.concatenate(parts)
-    flat = jnp.pad(flat, (0, stat_rows * col_block - flat.shape[0]))
-    extra = jnp.broadcast_to(flat.reshape(stat_rows, 1, col_block), (stat_rows, fsdp_count, col_block))
-    outgoing = jnp.concatenate([block_input.reshape(rows, fsdp_count, col_block), extra], axis=0)
+    flat = jnp.pad(flat, (0, stat_rows * kv_width - flat.shape[0]))
+    col_input = lax.all_to_all(block_input, "fsdp", split_axis=1, concat_axis=0, tiled=True)
 
     values_grad = value_grad(queries, saved_keys, out_grad)
-    all_values = lax.all_gather(values_grad, "fsdp", axis=0, tiled=True)
-    all_values, outgoing = lax.optimization_barrier((all_values, outgoing))
-    arrived = lax.all_to_all(outgoing, "fsdp", split_axis=1, concat_axis=0, tiled=True)
-    arrived = arrived.reshape(fsdp_count, rows + stat_rows, col_block)
-    col_input = arrived[:, :rows, :].reshape(fsdp_count * rows, col_block)
-    got = arrived[:, rows:, :].reshape(fsdp_count, stat_rows * col_block)[:, : len(parts) * rows]
+    outgoing = jnp.concatenate([values_grad, flat.reshape(stat_rows, kv_width)], axis=0)
+    arrived = lax.all_gather(outgoing[None], "fsdp", axis=0, tiled=True)
+    all_values = arrived[:, :rows, :].reshape(fsdp_count * rows, kv_width)
+    got = arrived[:, rows:, :].reshape(fsdp_count, stat_rows * kv_width)[:, : len(parts) * rows]
     got = got.reshape(fsdp_count, len(parts), rows).astype(jnp.float32)
     all_average = ((got[:, 0] + got[:, 1]) + got[:, 2]).reshape(-1)
     all_inv_std = ((got[:, 3] + got[:, 4]) + got[:, 5]).reshape(-1)
     all_lang = got[:, 6].reshape(-1).astype(jnp.int32)
-
 
     standard = (col_input.astype(jnp.float32) - all_average[:, None]) * all_inv_std[:, None]
     lang_table = all_lang[None, :] == jnp.arange(lang_count, dtype=jnp.int32)[:, None]

time: 259 us -> 220 us (0.85)
  the two profiles are of different devices: /device:TPU:14 before, /device:TPU:2 now
where the time goes in v7:
time: 220 us; the launch traced here: 219 us
  waiting for transfers between devices  104 us (47%)
  starting transfers between devices  46.5 us (21%)
  other arithmetic  19.2 us (9%)
  local copies, waits for them, and re-layouts  17.7 us (8%)
  between operations  15.9 us (7%)
  matrix products  15.5 us (7%)
    all_to_all x1, waiting for transfers between devices, body(): lax.all_to_all(block_input, 'fsdp', split_axis=1, concat_axis=0, tiled=True)  67.1 us
    ppermute x4, starting transfers between devices, halving_scatter(): grid = keep + lax.ppermute(send, axis, pairs)  21.9 us
    ppermute x5, starting transfers between devices, exchange_sum(): return part + lax.ppermute(part, axis, pairs)  15 us
    ppermute x5, waiting for transfers between devices, exchange_sum(): return part + lax.ppermute(part, axis, pairs)  14.6 us
    ppermute x4, waiting for transfers between devices, halving_scatter(): grid = keep + lax.ppermute(send, axis, pairs)  14.5 us
    all_to_all x1, starting transfers between devices, body(): lax.all_to_all(block_input, 'fsdp', split_axis=1, concat_axis=0, tiled=True)  9.56 us
    all_gather x1, waiting for transfers between devices, body(): arrived = lax.all_gather(outgoing[None], 'fsdp', axis=0, tiled=True)  7.75 us
    dot_general x1, matrix products, body(): jnp.dot(normed.T, all_values, preferred_element_type=jnp.float32)  6.42 us
  transfers between devices with their start and end apart: 11, of which 11 were waited for; matrix products, arithmetic and copies ran while one was open for 5% of the time, Pallas kernels for 0%

profile of v7, /device:TPU:2, one launch (start us, length us, event | category | flops | bytes accessed | tf_op | source)
XLA Modules:
  0.0 218.8 jit_solution(16835034663486000384)
XLA Ops:
  8.1 1.9 convert_reduce_fusion
  10.0 2.3 %fusion.4 = f32[128]{0:T(128)S(1)} fusion(bf16[128,8192]{1,0:T(8,128)(2,1)} %param.11, f32[128]{0:T(128)S(1)} %get-tuple-element.32), kind=kLoop, calls=%fused_computation.8 | loop fusion | flops 4194176 | bytes 2098176 | tf_op jit(solution)/shard_map/reduce_sum | solution.py:21
  15.6 3.5 %fusion.45 = (f32[4,8,128]{2,1,0:T(8,128)S(1)}, f32[4,8,128,128]{2,3,1,0:T(8,128)}) fusion(pred[128,128]{0,1:T(8,128)(4,1)S(1)} %iota_compare_fusion.4, bf16[128,4,8,128]{3,2,1,0:T(8,128)(2,1)} %bitcast.78, bf16[128,4,128,1]{2,1,0,3:T(4,128)(2,1)S(1)} %bitcast.83), kind=kOutput, calls=%fused_computation.81 | convolution fusion | flops 136315008 | bytes 3309568 | tf_op jit(solution)/shard_map/sub | solution.py:37
  19.1 2.2 %fusion.8 = bf16[4,128,128]{1,2,0:T(8,128)(2,1)S(1)} fusion(bf16[128,4,8,128]{0,3,2,1:T(8,128)(2,1)S(1)} %bitcast.77, f32[4,8,128,128]{2,3,1,0:T(8,128)} %get-tuple-element.37, f32[4,8,128]{2,1,0:T(8,128)S(1)} %get-tuple-element.36), kind=kOutput, calls=%fused_computation.18 | convolution fusion | flops 135331840 | bytes 3293184 | tf_op jit(solution)/shard_map/kgts,tkgd->skd/dot_general | solution.py:40
  22.2 2.5 %copy.60 = bf16[128,8192]{0,1:T(8,128)(2,1)} copy(bf16[128,8192]{1,0:T(8,128)(2,1)S(1)} %copy-done.2) | data formatting | bytes 4194304 | tf_op args[0]
  24.6 9.6 %all-to-all-start = ((bf16[128,32,256]{0,2,1:T(8,128)(2,1)}), bf16[128,32,256]{0,2,1:T(8,128)(2,1)S(1)}, u32[]{:S(2)}, u32[]{:S(2)}) async-start(bf16[128,32,256]{0,2,1:T(8,128)(2,1)} %bitcast.72), calls=%async_computation | async-start | bytes 4194304 | tf_op jit(solution)/shard_map/all_to_all | solution.py:113
  34.2 67.1 %all-to-all-done = bf16[128,32,256]{0,2,1:T(8,128)(2,1)S(1)} async-done(((bf16[128,32,256]{0,2,1:T(8,128)(2,1)}), bf16[128,32,256]{0,2,1:T(8,128)(2,1)S(1)}, u32[]{:S(2)}, u32[]{:S(2)}) %all-to-all-start) | async-done | bytes 2097184 | tf_op jit(solution)/shard_map/all_to_all | solution.py:113
  101.3 2.5 %convert_bitcast_fusion = f32[32,128,256]{1,2,0:T(8,128)} fusion(bf16[128,32,256]{0,2,1:T(8,128)(2,1)S(1)} %all-to-all-done), kind=kLoop, calls=%fused_computation.11 | loop fusion | flops 1048576 | bytes 6291456 | tf_op jit(solution)/shard_map/convert_element_type | solution.py:125
  103.8 5.7 %copy.61 = f32[32,128,256]{2,1,0:T(8,128)} copy(f32[32,128,256]{1,2,0:T(8,128)} %convert_bitcast_fusion) | data formatting | bytes 8388608 | tf_op jit(solution)/shard_map/convert_element_type | solution.py:125
  109.5 7.8 %all-gather.4.cloned.1.call-done = bf16[32,130,512]{2,1,0:T(8,128)(2,1)} async-done(((bf16[1,130,512]{2,1,0:T(8,128)(2,1)}), bf16[32,130,512]{2,1,0:T(8,128)(2,1)}) %all-gather.4.cloned.1.call-update) | async-done | bytes 4259856 | tf_op jit(solution)/shard_map/all_gather | solution.py:117
  118.4 4.3 %fusion.5 = f32[4096,256]{1,0:T(8,128)S(1)} fusion(f32[32,128,256]{2,1,0:T(8,128)} %copy.61, f32[4096]{0:T(1024)S(1)} %bitcast.87, f32[4096]{0:T(1024)S(1)} %bitcast.86), kind=kLoop, calls=%fused_computation.10 | loop fusion | flops 2097152 | bytes 8421376 | tf_op jit(solution)/shard_map/mul | solution.py:125
  123.4 1.4 copy-done
  126.1 2.1 multiply_reduce_fusion.1
  128.2 6.4 %multiply_reduce_fusion = (f32[]{:T(128)}, f32[256,512]{1,0:T(8,128)S(1)}) fusion(bf16[4096,512]{1,0:T(8,128)(2,1)} %bitcast.71, f32[4096,256]{1,0:T(8,128)} %copy-done, s32[4096]{0:T(1024)S(1)} %bitcast.82, bf16[1,16,8192]{2,1,0:T(8,128)(2,1)} %param.17, s32[]{:T(128)S(6)} %select_n.36), kind=kOutput, calls=%fused_computation.25 | convolution fusion | flops 1109852160 | bytes 8937480 | tf_op jit(solution)/shard_map/dot_general | solution.py:139
  135.9 2.1 collective-permute-start
  140.4 1.9 collective-permute-start.1
  142.3 3.5 %collective-permute-done.1 = f32[2]{0:T(128)S(1)} collective-permute-done((f32[2]{0:T(128)S(1)}, f32[2]{0:T(128)S(1)}, u32[]{:S(2)}, u32[]{:S(2)}) %collective-permute-start.1) | collective-permute-done | bytes 40 | tf_op jit(solution)/shard_map/ppermute | solution.py:47
  145.8 1.4 fusion.57
  147.2 2.6 %collective-permute-start.2 = (f32[2]{0:T(128)S(1)}, f32[2]{0:T(128)S(1)}, u32[]{:S(2)}, u32[]{:S(2)}) collective-permute-start(f32[2]{0:T(128)S(1)} %fusion.57), channel_id=1, source_target_pairs={{0,4},{1,5},{2,6},{3,7},{4,0},{5,1},{6,2},{7,3},{8,12},{9,13},{10,... | collective-permute-start | bytes 32 | tf_op jit(solution)/shard_map/ppermute | solution.py:47
  149.8 2.8 %collective-permute-done.2 = f32[2]{0:T(128)S(1)} collective-permute-done((f32[2]{0:T(128)S(1)}, f32[2]{0:T(128)S(1)}, u32[]{:S(2)}, u32[]{:S(2)}) %collective-permute-start.2) | collective-permute-done | bytes 40 | tf_op jit(solution)/shard_map/ppermute | solution.py:47
  152.6 3.6 %collective-permute-start.3 = (f32[2]{0:T(128)S(1)}, f32[2]{0:T(128)S(1)}, u32[]{:S(2)}, u32[]{:S(2)}) collective-permute-start(f32[2]{0:T(128)S(1)} %add.129), channel_id=1, source_target_pairs={{0,8},{1,9},{2,10},{3,11},{4,12},{5,13},{6,14},{7,15},{8,0},{9,1},... | collective-permute-start | bytes 32 | tf_op jit(solution)/shard_map/ppermute | solution.py:47
  156.3 2.7 %collective-permute-done.3 = f32[2]{0:T(128)S(1)} collective-permute-done((f32[2]{0:T(128)S(1)}, f32[2]{0:T(128)S(1)}, u32[]{:S(2)}, u32[]{:S(2)}) %collective-permute-start.3) | collective-permute-done | bytes 40 | tf_op jit(solution)/shard_map/ppermute | solution.py:47
  159.0 4.7 %collective-permute-start.4 = (f32[2]{0:T(128)S(1)}, f32[2]{0:T(128)S(1)}, u32[]{:S(2)}, u32[]{:S(2)}) collective-permute-start(f32[2]{0:T(128)S(1)} %add.130), channel_id=1, source_target_pairs={{0,16},{1,17},{2,18},{3,19},{4,20},{5,21},{6,22},{7,23},{8,24},{9,... | collective-permute-start | bytes 32 | tf_op jit(solution)/shard_map/ppermute | solution.py:47
  163.7 4.6 %collective-permute-done.4 = f32[2]{0:T(128)S(1)} collective-permute-done((f32[2]{0:T(128)S(1)}, f32[2]{0:T(128)S(1)}, u32[]{:S(2)}, u32[]{:S(2)}) %collective-permute-start.4) | collective-permute-done | bytes 40 | tf_op jit(solution)/shard_map/ppermute | solution.py:47
  173.2 3.4 %collective-permute-start.5 = (f32[2,2,2,8448]{3,2,1,0:T(2,128)S(1)}, f32[2,2,2,8448]{3,2,1,0:T(2,128)S(1)}, u32[]{:S(2)}, u32[]{:S(2)}) collective-permute-start(f32[2,2,2,8448]{3,2,1,0:T(2,128)S(1)} %dynamic-slice_bitcast_fusion), channel_id=1, source_target_pairs={{0,64},{32,96},{64,0},{96,32},{128,192},{160,224},{192,128},{224,1... | collective-permute-start | bytes 811016 | tf_op jit(solution)/shard_map/ppermute | solution.py:72
  176.6 5.0 %collective-permute-done.5 = f32[2,2,2,8448]{3,2,1,0:T(2,128)S(1)} collective-permute-done((f32[2,2,2,8448]{3,2,1,0:T(2,128)S(1)}, f32[2,2,2,8448]{3,2,1,0:T(2,128)S(1)}, u32[]{:S(2)}, u32[]{:S(2)}) %collective-permute-start.5) | collective-permute-done | bytes 270368 | tf_op jit(solution)/shard_map/ppermute | solution.py:72
  181.7 6.8 %collective-permute-start.6 = (f32[2,2,8448]{2,1,0:T(2,128)S(1)}, f32[2,2,8448]{2,1,0:T(2,128)S(1)}, u32[]{:S(2)}, u32[]{:S(2)}) collective-permute-start(f32[2,2,8448]{2,1,0:T(2,128)S(1)} %dynamic-slice_bitcast_fusion.1), channel_id=1, source_target_pairs={{0,128},{32,160},{64,192},{96,224},{128,0},{160,32},{192,64},{224,... | collective-permute-start | bytes 405512 | tf_op jit(solution)/shard_map/ppermute | solution.py:72
  188.5 3.9 %collective-permute-done.6 = f32[2,2,8448]{2,1,0:T(2,128)S(1)} collective-permute-done((f32[2,2,8448]{2,1,0:T(2,128)S(1)}, f32[2,2,8448]{2,1,0:T(2,128)S(1)}, u32[]{:S(2)}, u32[]{:S(2)}) %collective-permute-start.6) | collective-permute-done | bytes 135200 | tf_op jit(solution)/shard_map/ppermute | solution.py:72
  192.6 4.1 %collective-permute-start.7 = (f32[2,8448]{1,0:T(2,128)S(1)}, f32[2,8448]{1,0:T(2,128)S(1)}, u32[]{:S(2)}, u32[]{:S(2)}) collective-permute-start(f32[2,8448]{1,0:T(2,128)S(1)} %bitcast.85), channel_id=1, source_target_pairs={{0,32},{32,0},{64,96},{96,64},{128,160},{160,128},{192,224},{224,1... | collective-permute-start | bytes 202760 | tf_op jit(solution)/shard_map/ppermute | solution.py:72
  196.7 3.6 %collective-permute-done.7 = f32[2,8448]{1,0:T(2,128)S(1)} collective-permute-done((f32[2,8448]{1,0:T(2,128)S(1)}, f32[2,8448]{1,0:T(2,128)S(1)}, u32[]{:S(2)}, u32[]{:S(2)}) %collective-permute-start.7) | collective-permute-done | bytes 67616 | tf_op jit(solution)/shard_map/ppermute | solution.py:72
  200.6 7.8 %collective-permute-start.8 = (f32[8448]{0:T(1024)S(1)}, f32[8448]{0:T(1024)S(1)}, u32[]{:S(2)}, u32[]{:S(2)}) collective-permute-start(f32[8448]{0:T(1024)S(1)} %get-tuple-element.16), channel_id=1, source_target_pairs={{0,256},{32,288},{64,320},{96,352},{128,384},{160,416},{192,448},{... | collective-permute-start | bytes 101384 | tf_op jit(solution)/shard_map/ppermute | solution.py:72
  208.3 2.1 collective-permute-done.8
  (84 shorter events, 17.1 us)
Async XLA Ops:
  7.2 6.6 %copy-start.6 = (bf16[128,512]{1,0:T(8,128)(2,1)S(1)}, bf16[128,512]{1,0:T(8,128)(2,1)}, u32[]{:S(2)}) copy-start(bf16[128,512]{1,0:T(8,128)(2,1)} %param.14) | copy-start | bytes 393220
  7.2 6.6 %copy-start.4 = (bf16[128,4096]{1,0:T(8,128)(2,1)S(1)}, bf16[128,4096]{1,0:T(8,128)(2,1)}, u32[]{:S(2)}) copy-start(bf16[128,4096]{1,0:T(8,128)(2,1)} %param.13) | copy-start | bytes 3145732
  7.2 7.8 %copy-start.5 = (bf16[128,4096]{1,0:T(8,128)(2,1)S(1)}, bf16[128,4096]{1,0:T(8,128)(2,1)}, u32[]{:S(2)}) copy-start(bf16[128,4096]{1,0:T(8,128)(2,1)} %param.15) | copy-start | bytes 3145732
  7.2 110.1 %all-gather.4.cloned.1.call-start = ((), (), s32[]{:S(2)}) async-start(), calls=%async_computation.1 | async-start | bytes 4595712 | tf_op jit(solution)/shard_map/all_gather | solution.py:117
  19.1 3.0 %copy-start.2 = (bf16[128,8192]{1,0:T(8,128)(2,1)S(1)}, bf16[128,8192]{1,0:T(8,128)(2,1)}, u32[]{:S(2)}) copy-start(bf16[128,8192]{1,0:T(8,128)(2,1)} %param.11) | copy-start | bytes 6291460
  24.6 76.7 %all-to-all-start = ((bf16[128,32,256]{0,2,1:T(8,128)(2,1)}), bf16[128,32,256]{0,2,1:T(8,128)(2,1)S(1)}, u32[]{:S(2)}, u32[]{:S(2)}) async-start(bf16[128,32,256]{0,2,1:T(8,128)(2,1)} %bitcast.72), calls=%async_computation | async-start | bytes 4194304 | tf_op jit(solution)/shard_map/all_to_all | solution.py:113
  118.3 4.5 %slice-start = ((s8[4456448]{0:T(1024)(128)(4,1)}), s8[4194304]{0:T(1024)(128)(4,1)S(1)}, s32[]{:S(2)}) async-start(s8[4456448]{0:T(1024)(128)(4,1)} %bitcast.73), calls=%async_computation.2 | async-start | bytes 8388608
  118.4 4.4 %slice-start.1 = ((s8[4456448]{0:T(1024)(128)(4,1)}), s8[262144]{0:T(1024)(128)(4,1)S(1)}, s32[]{:S(2)}) async-start(s8[4456448]{0:T(1024)(128)(4,1)} %bitcast.73), calls=%async_computation.3 | async-start | bytes 524288
  122.8 2.0 copy-start
  122.8 2.0 copy-start.3
  123.4 2.7 %copy-start.1 = (bf16[32,128,512]{2,1,0:T(8,128)(2,1)}, bf16[32,128,512]{2,1,0:T(8,128)(2,1)S(1)}, u32[]{:S(2)}) copy-start(bf16[32,128,512]{2,1,0:T(8,128)(2,1)S(1)} %slice.65) | copy-start | bytes 12582916
  135.9 3.0 %collective-permute-start = (f32[2]{0:T(128)S(1)}, f32[2]{0:T(128)S(1)}, u32[]{:S(2)}, u32[]{:S(2)}) collective-permute-start(f32[2]{0:T(128)S(1)} %pad_maximum_fusion), channel_id=1, source_target_pairs={{0,1},{1,0},{2,3},{3,2},{4,5},{5,4},{6,7},{7,6},{8,9},{9,8},{10,11... | collective-permute-start | bytes 32 | tf_op jit(solution)/shard_map/ppermute | solution.py:47
  140.4 5.5 %collective-permute-start.1 = (f32[2]{0:T(128)S(1)}, f32[2]{0:T(128)S(1)}, u32[]{:S(2)}, u32[]{:S(2)}) collective-permute-start(f32[2]{0:T(128)S(1)} %fusion.56), channel_id=1, source_target_pairs={{0,2},{1,3},{2,0},{3,1},{4,6},{5,7},{6,4},{7,5},{8,10},{9,11},{10,... | collective-permute-start | bytes 32 | tf_op jit(solution)/shard_map/ppermute | solution.py:47
  147.2 5.5 %collective-permute-start.2 = (f32[2]{0:T(128)S(1)}, f32[2]{0:T(128)S(1)}, u32[]{:S(2)}, u32[]{:S(2)}) collective-permute-start(f32[2]{0:T(128)S(1)} %fusion.57), channel_id=1, source_target_pairs={{0,4},{1,5},{2,6},{3,7},{4,0},{5,1},{6,2},{7,3},{8,12},{9,13},{10,... | collective-permute-start | bytes 32 | tf_op jit(solution)/shard_map/ppermute | solution.py:47
  152.6 6.3 %collective-permute-start.3 = (f32[2]{0:T(128)S(1)}, f32[2]{0:T(128)S(1)}, u32[]{:S(2)}, u32[]{:S(2)}) collective-permute-start(f32[2]{0:T(128)S(1)} %add.129), channel_id=1, source_target_pairs={{0,8},{1,9},{2,10},{3,11},{4,12},{5,13},{6,14},{7,15},{8,0},{9,1},... | collective-permute-start | bytes 32 | tf_op jit(solution)/shard_map/ppermute | solution.py:47
  159.0 9.4 %collective-permute-start.4 = (f32[2]{0:T(128)S(1)}, f32[2]{0:T(128)S(1)}, u32[]{:S(2)}, u32[]{:S(2)}) collective-permute-start(f32[2]{0:T(128)S(1)} %add.130), channel_id=1, source_target_pairs={{0,16},{1,17},{2,18},{3,19},{4,20},{5,21},{6,22},{7,23},{8,24},{9,... | collective-permute-start | bytes 32 | tf_op jit(solution)/shard_map/ppermute | solution.py:47
  171.9 38.7 %copy-start.9 = (f32[1,256]{1,0:T(1,128)S(1)}, f32[1,256]{1,0:T(1,128)}, u32[]{:S(2)}) copy-start(f32[1,256]{1,0:T(1,128)} %param.20) | copy-start | bytes 3076
  172.0 38.7 %copy-start.10 = (f32[1,256]{1,0:T(1,128)S(1)}, f32[1,256]{1,0:T(1,128)}, u32[]{:S(2)}) copy-start(f32[1,256]{1,0:T(1,128)} %param.21) | copy-start | bytes 3076
  172.0 39.3 %copy-start.7 = (f32[256,32]{0,1:T(8,128)S(1)}, f32[256,32]{0,1:T(8,128)}, u32[]{:S(2)}) copy-start(f32[256,32]{0,1:T(8,128)} %param.18) | copy-start | bytes 98308
  172.0 39.3 %copy-start.8 = (f32[256,32]{0,1:T(8,128)S(1)}, f32[256,32]{0,1:T(8,128)}, u32[]{:S(2)}) copy-start(f32[256,32]{0,1:T(8,128)} %param.19) | copy-start | bytes 98308
  173.2 8.4 %collective-permute-start.5 = (f32[2,2,2,8448]{3,2,1,0:T(2,128)S(1)}, f32[2,2,2,8448]{3,2,1,0:T(2,128)S(1)}, u32[]{:S(2)}, u32[]{:S(2)}) collective-permute-start(f32[2,2,2,8448]{3,2,1,0:T(2,128)S(1)} %dynamic-slice_bitcast_fusion), channel_id=1, source_target_pairs={{0,64},{32,96},{64,0},{96,32},{128,192},{160,224},{192,128},{224,1... | collective-permute-start | bytes 811016 | tf_op jit(solution)/shard_map/ppermute | solution.py:72
  181.7 10.6 %collective-permute-start.6 = (f32[2,2,8448]{2,1,0:T(2,128)S(1)}, f32[2,2,8448]{2,1,0:T(2,128)S(1)}, u32[]{:S(2)}, u32[]{:S(2)}) collective-permute-start(f32[2,2,8448]{2,1,0:T(2,128)S(1)} %dynamic-slice_bitcast_fusion.1), channel_id=1, source_target_pairs={{0,128},{32,160},{64,192},{96,224},{128,0},{160,32},{192,64},{224,... | collective-permute-start | bytes 405512 | tf_op jit(solution)/shard_map/ppermute | solution.py:72
  192.6 7.7 %collective-permute-start.7 = (f32[2,8448]{1,0:T(2,128)S(1)}, f32[2,8448]{1,0:T(2,128)S(1)}, u32[]{:S(2)}, u32[]{:S(2)}) collective-permute-start(f32[2,8448]{1,0:T(2,128)S(1)} %bitcast.85), channel_id=1, source_target_pairs={{0,32},{32,0},{64,96},{96,64},{128,160},{160,128},{192,224},{224,1... | collective-permute-start | bytes 202760 | tf_op jit(solution)/shard_map/ppermute | solution.py:72
  200.6 9.8 %collective-permute-start.8 = (f32[8448]{0:T(1024)S(1)}, f32[8448]{0:T(1024)S(1)}, u32[]{:S(2)}, u32[]{:S(2)}) collective-permute-start(f32[8448]{0:T(1024)S(1)} %get-tuple-element.16), channel_id=1, source_target_pairs={{0,256},{32,288},{64,320},{96,352},{128,384},{160,416},{192,448},{... | collective-permute-start | bytes 101384 | tf_op jit(solution)/shard_map/ppermute | solution.py:72
Sparse Core Ops, SparseCore 0:
  22.3 94.9 all-gather.3

commit v8 on v6

--- a/solution.py
+++ b/solution.py
@@ -140,9 +140,11 @@
         lang_table.astype(jnp.float32), standard * input_grad, precision=lax.Precision.HIGHEST
     )
     wv_grad = jnp.dot(normed.T, all_values, preferred_element_type=jnp.float32) * weight_scale
-    squares = doubling_sum(
-        jnp.stack([jnp.sum(wv_grad * wv_grad), jnp.sum(gain_grad * gain_grad)]), "fsdp"
+    partial = jnp.stack([jnp.sum(wv_grad * wv_grad), jnp.sum(gain_grad * gain_grad)])
+    partials = lax.all_to_all(
+        jnp.broadcast_to(partial, (fsdp_count, 2)), "fsdp", split_axis=0, concat_axis=0, tiled=True
     )
+    squares = jnp.sum(partials, axis=0)
     wv_clip = jnp.minimum(1.0, CLIP_SHARE * (width * kv_width) ** 0.5 / jnp.sqrt(squares[0]))
     gain_clip = jnp.minimum(1.0, CLIP_SHARE * (lang_count * width) ** 0.5 / jnp.sqrt(squares[1]))
     new_wv = weight_rows.astype(jnp.float32) - wv_clip * wv_grad
@@ -154,7 +156,9 @@
     wv_part = wv_part.reshape(island_count, col_block * wv_share)
     gain_part = new_gain.reshape(island_count, gain_share * col_block)
     packed = jnp.concatenate([wv_part, gain_part], axis=1)
-    total = halving_scatter(packed, "island", (2, 1, 3, 0))[None, :]
+    total = jnp.sum(
+        lax.all_to_all(packed, "island", split_axis=0, concat_axis=0, tiled=True), axis=0, keepdims=True
+    )
     total_wv = total[0, : col_block * wv_share].reshape(col_block, wv_share)
     total_gain = total[0, col_block * wv_share :].reshape(gain_share, col_block)
 

time: 212 us -> 185 us (0.87)
  the two profiles are of different devices: /device:TPU:4 before, /device:TPU:1 now
where the time goes in v8:
time: 185 us; the launch traced here: 184 us
  waiting for transfers between devices  70.4 us (38%)
  blocking collectives  41.9 us (23%)
  local copies, waits for them, and re-layouts  19.7 us (11%)
  matrix products  16.1 us (9%)
  between operations  15.7 us (8%)
  starting transfers between devices  10.7 us (6%)
  other arithmetic  9.6 us (5%)
    all_to_all x1, waiting for transfers between devices, body(): lax.all_to_all(outgoing, 'fsdp', split_axis=1, concat_axis=0, tiled=True)  69.7 us
    all_to_all x1, blocking collectives, body(): lax.all_to_all(packed, 'island', split_axis=0, concat_axis=0, tiled=True)  27.1 us
    all_to_all x1, blocking collectives, body(): lax.all_to_all(jnp.broadcast_to(partial, (fsdp_count, 2)), 'fsdp', split_...  14.8 us
    all_to_all x1, starting transfers between devices, body(): lax.all_to_all(outgoing, 'fsdp', split_axis=1, concat_axis=0, tiled=True)  10.7 us
    dot_general x1, matrix products, body(): jnp.dot(normed.T, all_values, preferred_element_type=jnp.float32)  5.95 us
    concatenate x1, local copies, waits for them, and re-layouts, body(): jnp.concatenate([block_input.reshape(rows, fsdp_count, col_block), extra]...  5.63 us
    unnamed x25, local copies, waits for them, and re-layouts  5.22 us
    concatenate x1, other arithmetic, body(): jnp.concatenate([block_input.reshape(rows, fsdp_count, col_block), extra]...  4.53 us
  transfers between devices with their start and end apart: 2, of which 2 were waited for; matrix products, arithmetic and copies ran while one was open for 10% of the time, Pallas kernels for 0%

profile of v8, /device:TPU:1, one launch (start us, length us, event | category | flops | bytes accessed | tf_op | source)
XLA Modules:
  0.0 184.1 jit_solution(2179436695641191873)
XLA Ops:
  7.2 1.4 copy.135
  8.7 0.9 reshape.123
  9.6 1.6 copy.130
  11.3 2.3 %fusion.45 = (f32[4,8,128]{2,1,0:T(8,128)S(1)}, f32[4,8,128,128]{2,3,1,0:T(8,128)}) fusion(pred[128,128]{0,1:T(8,128)(4,1)S(1)} %iota_compare_fusion.4, bf16[128,4,8,128]{3,2,1,0:T(8,128)(2,1)S(1)} %bitcast.66, bf16[128,4,128,1]{2,1,0,3:T(4,128)(2,1)S(1)} %bitcast.69), kind=kOutput, calls=%fused_computation.69 | convolution fusion | flops 136315008 | bytes 3309568 | tf_op jit(solution)/shard_map/sub | solution.py:37
  13.6 2.2 %fusion.8 = bf16[4,128,128]{1,2,0:T(8,128)(2,1)S(1)} fusion(bf16[128,4,8,128]{0,3,2,1:T(8,128)(2,1)S(1)} %bitcast.65, f32[4,8,128,128]{2,3,1,0:T(8,128)} %get-tuple-element.45, f32[4,8,128]{2,1,0:T(8,128)S(1)} %get-tuple-element.44), kind=kOutput, calls=%fused_computation.18 | convolution fusion | flops 135331840 | bytes 3293184 | tf_op jit(solution)/shard_map/kgts,tkgd->skd/dot_general | solution.py:40
  15.8 0.8 copy.119
  16.6 2.5 %copy.112 = bf16[128,8192]{0,1:T(8,128)(2,1)} copy(bf16[128,8192]{1,0:T(8,128)(2,1)S(1)} %copy-done) | data formatting | bytes 4194304 | tf_op args[0]
  19.1 0.4 convert_reduce_fusion
  19.5 0.2 dynamic-update-slice
  20.1 0.7 fusion.4
  20.8 0.2 dynamic-update-slice.3
  21.8 0.5 broadcast_in_dim.30
  22.2 4.5 %pad_maximum_fusion = bf16[132,32,256]{0,2,1:T(8,128)(2,1)} fusion(bf16[4,32,256]{0,2,1:T(8,128)(2,1)S(1)} %broadcast_in_dim.30, bf16[128,32,256]{0,2,1:T(8,128)(2,1)} %bitcast.60), kind=kLoop, calls=%fused_computation.9 | loop fusion | flops 4325376 | bytes 4325376 | tf_op jit(solution)/shard_map/concatenate | solution.py:114
  26.8 5.6 %copy.114 = bf16[132,32,256]{2,0,1:T(8,128)(2,1)} copy(bf16[132,32,256]{0,2,1:T(8,128)(2,1)} %pad_maximum_fusion) | data formatting | bytes 4325376 | tf_op jit(solution)/shard_map/concatenate | solution.py:114
  32.4 10.7 %all-to-all-start = ((bf16[132,32,256]{2,0,1:T(8,128)(2,1)}), bf16[132,32,256]{2,0,1:T(8,128)(2,1)S(1)}, u32[]{:S(2)}, u32[]{:S(2)}) async-start(bf16[132,32,256]{2,0,1:T(8,128)(2,1)} %copy.114), calls=%async_computation | async-start | bytes 4456448 | tf_op jit(solution)/shard_map/all_to_all | solution.py:115
  43.1 69.7 %all-to-all-done = bf16[132,32,256]{2,0,1:T(8,128)(2,1)S(1)} async-done(((bf16[132,32,256]{2,0,1:T(8,128)(2,1)}), bf16[132,32,256]{2,0,1:T(8,128)(2,1)S(1)}, u32[]{:S(2)}, u32[]{:S(2)}) %all-to-all-start) | async-done | bytes 2162720 | tf_op jit(solution)/shard_map/all_to_all | solution.py:115
  112.8 1.6 slice.56
  114.6 0.7 all-gather.2.cloned.1.call-done
  115.3 3.6 %fusion.1 = f32[4096,256]{1,0:T(8,128)S(1)} fusion(bf16[4096,512]{1,0:T(8,128)(2,1)} %bitcast.77, bf16[4096,256]{1,0:T(8,128)(2,1)} %bitcast.62, f32[4096]{0:T(1024)S(1)} %bitcast.75, f32[4096]{0:T(1024)S(1)} %bitcast.73, bf16[1,256,512]{2,1,0:T(8,128)(2,1)S(1)} %copy-done.2), kind=kOutput, calls=%fused_computation.2 | convolution fusion | flops 1078984704 | bytes 10780672 | tf_op jit(solution)/shard_map/dot_general | solution.py:137
  118.8 2.1 %multiply_reduce_fusion.1 = (f32[]{:T(128)}, f32[16,256]{1,0:T(8,128)S(1)}) fusion(f32[4096,256]{1,0:T(8,128)S(1)} %fusion.1, s32[4096]{0:T(1024)S(1)} %bitcast.71), kind=kOutput, calls=%fused_computation.45 | convolution fusion | flops 201400320 | bytes 4227076 | tf_op jit(solution)/shard_map/dot_general | solution.py:139
  120.9 5.9 %multiply_reduce_fusion = (f32[]{:T(128)}, f32[256,512]{1,0:T(8,128)S(1)}) fusion(bf16[4096,512]{1,0:T(8,128)(2,1)} %bitcast.78, bf16[4096,256]{1,0:T(8,128)(2,1)S(1)} %bitcast.63, f32[4096]{0:T(1024)S(1)} %bitcast.76, f32[4096]{0:T(1024)S(1)} %bitcast.74, s32[4096]{0:T(1024)S(1)} %bitcast.72, bf16[1,16,8192]{2,1,0:T(8,128)(2,1)} %param.17, s32[]{:T(128)S(6)} %select_n.7), kind=kOutput, calls=%fused_computation.26 | convolution fusion | flops 1112997888 | bytes 6873096 | tf_op jit(solution)/shard_map/dot_general | solution.py:142
  126.9 1.4 pad_maximum_fusion.1
  128.2 14.8 %all_to_all.30 = f32[32,1,2]{2,1,0:T(1,128)S(1)} all-to-all(f32[32,1,2]{2,1,0:T(1,128)S(1)} %broadcast_in_dim.33), channel_id=1, replica_groups=mesh['island'=16,'fsdp'=32] {'fsdp'}, dimensions={0} | all-to-all | bytes 512 | tf_op jit(solution)/shard_map/all_to_all | solution.py:144
  143.1 0.6 fusion.44
  144.7 0.6 copy.122
  145.3 1.0 reshape.128
  146.9 0.7 multiply_subtract_fusion.2
  147.7 0.6 copy.123
  148.3 27.1 %all_to_all.31 = f32[16,1,8448]{2,1,0:T(1,128)S(1)} all-to-all(f32[16,1,8448]{2,1,0:T(1,128)S(1)} %copy.123), channel_id=1, replica_groups=mesh['island'=16,'fsdp'=32] {'island'}, dimensions={0} | all-to-all | bytes 1081344 | tf_op jit(solution)/shard_map/all_to_all | solution.py:160
  175.4 0.3 reduce_sum.69
  176.0 0.6 multiply_subtract_fusion.3
  176.6 0.6 multiply_subtract_fusion.1
  (45 shorter events, 2.0 us)
Async XLA Ops:
  7.2 108.1 %all-gather.2.cloned.1.call-start = ((), (), s32[]{:S(2)}) async-start(), calls=%async_computation.3 | async-start | bytes 4325376 | tf_op jit(solution)/shard_map/all_gather | solution.py:125
  13.6 3.0 %copy-start.7 = (s32[128]{0:T(128)S(1)}, s32[128]{0:T(128)}, u32[]{:S(2)}) copy-start(s32[128]{0:T(128)} %param.12) | copy-start | bytes 1540
  13.6 3.0 %copy-start = (bf16[128,8192]{1,0:T(8,128)(2,1)S(1)}, bf16[128,8192]{1,0:T(8,128)(2,1)}, u32[]{:S(2)}) copy-start(bf16[128,8192]{1,0:T(8,128)(2,1)} %param.11) | copy-start | bytes 6291460
  32.4 82.9 %copy-start.2 = (bf16[1,256,512]{2,1,0:T(8,128)(2,1)S(1)}, bf16[1,256,512]{2,1,0:T(8,128)(2,1)}, u32[]{:S(2)}) copy-start(bf16[1,256,512]{2,1,0:T(8,128)(2,1)} %param.16) | copy-start | bytes 786436
  32.4 80.4 %all-to-all-start = ((bf16[132,32,256]{2,0,1:T(8,128)(2,1)}), bf16[132,32,256]{2,0,1:T(8,128)(2,1)S(1)}, u32[]{:S(2)}, u32[]{:S(2)}) async-start(bf16[132,32,256]{2,0,1:T(8,128)(2,1)} %copy.114), calls=%async_computation | async-start | bytes 4456448 | tf_op jit(solution)/shard_map/all_to_all | solution.py:115
  118.8 2.1 %copy-start.1 = (bf16[32,128,256]{2,1,0:T(8,128)(2,1)S(1)}, bf16[32,128,256]{2,1,0:T(8,128)(2,1)}, u32[]{:S(2)}) copy-start(bf16[32,128,256]{2,1,0:T(8,128)(2,1)} %slice.56) | copy-start | bytes 6291460
  144.6 31.4 %copy-start.5 = (f32[1,256]{1,0:T(1,128)S(1)}, f32[1,256]{1,0:T(1,128)}, u32[]{:S(2)}) copy-start(f32[1,256]{1,0:T(1,128)} %param.20) | copy-start | bytes 3076
  144.6 31.4 %copy-start.6 = (f32[1,256]{1,0:T(1,128)S(1)}, f32[1,256]{1,0:T(1,128)}, u32[]{:S(2)}) copy-start(f32[1,256]{1,0:T(1,128)} %param.21) | copy-start | bytes 3076
  144.7 31.9 %copy-start.3 = (f32[256,32]{0,1:T(8,128)S(1)}, f32[256,32]{0,1:T(8,128)}, u32[]{:S(2)}) copy-start(f32[256,32]{0,1:T(8,128)} %param.18) | copy-start | bytes 98308
  144.7 31.9 %copy-start.4 = (f32[256,32]{0,1:T(8,128)S(1)}, f32[256,32]{0,1:T(8,128)}, u32[]{:S(2)}) copy-start(f32[256,32]{0,1:T(8,128)} %param.19) | copy-start | bytes 98308
Sparse Core Ops, SparseCore 0:
  16.7 98.5 all-gather.1

commit v9 on v8

--- a/solution.py
+++ b/solution.py
@@ -110,10 +110,10 @@
     stat_rows = -(-len(parts) * rows // col_block)
     flat = jnp.concatenate(parts)
     flat = jnp.pad(flat, (0, stat_rows * col_block - flat.shape[0]))
-    extra = jnp.broadcast_to(flat.reshape(stat_rows, 1, col_block), (stat_rows, fsdp_count, col_block))
-    outgoing = jnp.concatenate([block_input.reshape(rows, fsdp_count, col_block), extra], axis=0)
-    arrived = lax.all_to_all(outgoing, "fsdp", split_axis=1, concat_axis=0, tiled=True)
-    arrived = arrived.reshape(fsdp_count, rows + stat_rows, col_block)
+    extra = jnp.broadcast_to(flat.reshape(1, stat_rows, col_block), (fsdp_count, stat_rows, col_block))
+    columns = block_input.reshape(rows, fsdp_count, col_block).transpose(1, 0, 2)
+    outgoing = jnp.concatenate([columns, extra], axis=1)
+    arrived = lax.all_to_all(outgoing, "fsdp", split_axis=0, concat_axis=0, tiled=True)
     col_input = arrived[:, :rows, :].reshape(fsdp_count * rows, col_block)
     got = arrived[:, rows:, :].reshape(fsdp_count, stat_rows * col_block)[:, : len(parts) * rows]
     got = got.reshape(fsdp_count, len(parts), rows).astype(jnp.float32)

time: 185 us -> 185 us (level)
  no operation moved by 1% of the time
where the time goes in v9:
time: 185 us; the launch traced here: 184 us
  waiting for transfers between devices  70.4 us (38%)
  blocking collectives  41.9 us (23%)
  local copies, waits for them, and re-layouts  19.7 us (11%)
  matrix products  16.1 us (9%)
  between operations  15.7 us (8%)
  starting transfers between devices  10.7 us (6%)
  other arithmetic  9.6 us (5%)
    all_to_all x1, waiting for transfers between devices, body(): lax.all_to_all(outgoing, 'fsdp', split_axis=0, concat_axis=0, tiled=True)  69.7 us
    all_to_all x1, blocking collectives, body(): lax.all_to_all(packed, 'island', split_axis=0, concat_axis=0, tiled=True)  27.1 us
    all_to_all x1, blocking collectives, body(): lax.all_to_all(jnp.broadcast_to(partial, (fsdp_count, 2)), 'fsdp', split_...  14.8 us
    all_to_all x1, starting transfers between devices, body(): lax.all_to_all(outgoing, 'fsdp', split_axis=0, concat_axis=0, tiled=True)  10.7 us
    dot_general x1, matrix products, body(): jnp.dot(normed.T, all_values, preferred_element_type=jnp.float32)  5.95 us
    concatenate x1, local copies, waits for them, and re-layouts, body(): outgoing = jnp.concatenate([columns, extra], axis=1)  5.63 us
    unnamed x25, local copies, waits for them, and re-layouts  5.22 us
    concatenate x1, other arithmetic, body(): outgoing = jnp.concatenate([columns, extra], axis=1)  4.53 us
  transfers between devices with their start and end apart: 2, of which 2 were waited for; matrix products, arithmetic and copies ran while one was open for 10% of the time, Pallas kernels for 0%

profile of v9, /device:TPU:1, one launch (start us, length us, event | category | flops | bytes accessed | tf_op | source)
XLA Modules:
  0.0 184.1 jit_solution(18121941632748668655)
XLA Ops:
  7.2 1.4 copy.135
  8.7 0.9 reshape.118
  9.6 1.6 copy.130
  11.3 2.3 %fusion.45 = (f32[4,8,128]{2,1,0:T(8,128)S(1)}, f32[4,8,128,128]{2,3,1,0:T(8,128)}) fusion(pred[128,128]{0,1:T(8,128)(4,1)S(1)} %iota_compare_fusion.4, bf16[128,4,8,128]{3,2,1,0:T(8,128)(2,1)S(1)} %bitcast.61, bf16[128,4,128,1]{2,1,0,3:T(4,128)(2,1)S(1)} %bitcast.64), kind=kOutput, calls=%fused_computation.69 | convolution fusion | flops 136315008 | bytes 3309568 | tf_op jit(solution)/shard_map/sub | solution.py:37
  13.6 2.2 %fusion.8 = bf16[4,128,128]{1,2,0:T(8,128)(2,1)S(1)} fusion(bf16[128,4,8,128]{0,3,2,1:T(8,128)(2,1)S(1)} %bitcast.60, f32[4,8,128,128]{2,3,1,0:T(8,128)} %get-tuple-element.45, f32[4,8,128]{2,1,0:T(8,128)S(1)} %get-tuple-element.44), kind=kOutput, calls=%fused_computation.18 | convolution fusion | flops 135331840 | bytes 3293184 | tf_op jit(solution)/shard_map/kgts,tkgd->skd/dot_general | solution.py:40
  15.8 0.8 copy.119
  16.6 2.5 %copy.112 = bf16[128,8192]{0,1:T(8,128)(2,1)} copy(bf16[128,8192]{1,0:T(8,128)(2,1)S(1)} %copy-done) | data formatting | bytes 4194304 | tf_op args[0]
  19.1 0.4 convert_reduce_fusion
  19.5 0.2 dynamic-update-slice
  20.1 0.7 fusion.4
  20.8 0.2 dynamic-update-slice.3
  21.8 0.5 broadcast_in_dim.30
  22.2 4.5 %pad_maximum_fusion = bf16[32,132,256]{1,2,0:T(8,128)(2,1)} fusion(bf16[32,4,256]{1,2,0:T(8,128)(2,1)S(1)} %broadcast_in_dim.30, bf16[32,128,256]{1,2,0:T(8,128)(2,1)} %bitcast.55), kind=kLoop, calls=%fused_computation.9 | loop fusion | flops 4325376 | bytes 4325376 | tf_op jit(solution)/shard_map/concatenate | solution.py:115
  26.8 5.6 %copy.114 = bf16[32,132,256]{2,1,0:T(8,128)(2,1)} copy(bf16[32,132,256]{1,2,0:T(8,128)(2,1)} %pad_maximum_fusion) | data formatting | bytes 4325376 | tf_op jit(solution)/shard_map/concatenate | solution.py:115
  32.4 10.7 %all-to-all-start = ((bf16[32,132,256]{2,1,0:T(8,128)(2,1)}), bf16[32,132,256]{2,1,0:T(8,128)(2,1)S(1)}, u32[]{:S(2)}, u32[]{:S(2)}) async-start(bf16[32,132,256]{2,1,0:T(8,128)(2,1)} %copy.114), calls=%async_computation | async-start | bytes 4456448 | tf_op jit(solution)/shard_map/all_to_all | solution.py:116
  43.1 69.7 %all-to-all-done = bf16[32,132,256]{2,1,0:T(8,128)(2,1)S(1)} async-done(((bf16[32,132,256]{2,1,0:T(8,128)(2,1)}), bf16[32,132,256]{2,1,0:T(8,128)(2,1)S(1)}, u32[]{:S(2)}, u32[]{:S(2)}) %all-to-all-start) | async-done | bytes 2162720 | tf_op jit(solution)/shard_map/all_to_all | solution.py:116
  112.9 1.6 slice.56
  114.6 0.7 all-gather.2.cloned.1.call-done
  115.3 3.6 %fusion.1 = f32[4096,256]{1,0:T(8,128)S(1)} fusion(bf16[4096,512]{1,0:T(8,128)(2,1)} %bitcast.72, bf16[4096,256]{1,0:T(8,128)(2,1)} %bitcast.57, f32[4096]{0:T(1024)S(1)} %bitcast.70, f32[4096]{0:T(1024)S(1)} %bitcast.68, bf16[1,256,512]{2,1,0:T(8,128)(2,1)S(1)} %copy-done.2), kind=kOutput, calls=%fused_computation.2 | convolution fusion | flops 1078984704 | bytes 10780672 | tf_op jit(solution)/shard_map/dot_general | solution.py:137
  118.8 2.1 %multiply_reduce_fusion.1 = (f32[]{:T(128)}, f32[16,256]{1,0:T(8,128)S(1)}) fusion(f32[4096,256]{1,0:T(8,128)S(1)} %fusion.1, s32[4096]{0:T(1024)S(1)} %bitcast.66), kind=kOutput, calls=%fused_computation.45 | convolution fusion | flops 201400320 | bytes 4227076 | tf_op jit(solution)/shard_map/dot_general | solution.py:139
  120.9 5.9 %multiply_reduce_fusion = (f32[]{:T(128)}, f32[256,512]{1,0:T(8,128)S(1)}) fusion(bf16[4096,512]{1,0:T(8,128)(2,1)} %bitcast.73, bf16[4096,256]{1,0:T(8,128)(2,1)S(1)} %bitcast.58, f32[4096]{0:T(1024)S(1)} %bitcast.71, f32[4096]{0:T(1024)S(1)} %bitcast.69, s32[4096]{0:T(1024)S(1)} %bitcast.67, bf16[1,16,8192]{2,1,0:T(8,128)(2,1)} %param.17, s32[]{:T(128)S(6)} %select_n.7), kind=kOutput, calls=%fused_computation.26 | convolution fusion | flops 1112997888 | bytes 6873096 | tf_op jit(solution)/shard_map/dot_general | solution.py:142
  126.9 1.4 pad_maximum_fusion.1
  128.2 14.8 %all_to_all.20 = f32[32,1,2]{2,1,0:T(1,128)S(1)} all-to-all(f32[32,1,2]{2,1,0:T(1,128)S(1)} %broadcast_in_dim.33), channel_id=1, replica_groups=mesh['island'=16,'fsdp'=32] {'fsdp'}, dimensions={0} | all-to-all | bytes 512 | tf_op jit(solution)/shard_map/all_to_all | solution.py:144
  143.1 0.6 fusion.44
  144.7 0.6 copy.122
  145.3 1.0 reshape.123
  146.9 0.7 multiply_subtract_fusion.2
  147.7 0.6 copy.123
  148.3 27.1 %all_to_all.21 = f32[16,1,8448]{2,1,0:T(1,128)S(1)} all-to-all(f32[16,1,8448]{2,1,0:T(1,128)S(1)} %copy.123), channel_id=1, replica_groups=mesh['island'=16,'fsdp'=32] {'island'}, dimensions={0} | all-to-all | bytes 1081344 | tf_op jit(solution)/shard_map/all_to_all | solution.py:160
  175.4 0.3 reduce_sum.69
  176.0 0.6 multiply_subtract_fusion.3
  176.6 0.6 multiply_subtract_fusion.1
  (45 shorter events, 2.0 us)
Async XLA Ops:
  7.2 108.1 %all-gather.2.cloned.1.call-start = ((), (), s32[]{:S(2)}) async-start(), calls=%async_computation.3 | async-start | bytes 4325376 | tf_op jit(solution)/shard_map/all_gather | solution.py:125
  13.6 3.0 %copy-start.7 = (s32[128]{0:T(128)S(1)}, s32[128]{0:T(128)}, u32[]{:S(2)}) copy-start(s32[128]{0:T(128)} %param.12) | copy-start | bytes 1540
  13.6 3.0 %copy-start = (bf16[128,8192]{1,0:T(8,128)(2,1)S(1)}, bf16[128,8192]{1,0:T(8,128)(2,1)}, u32[]{:S(2)}) copy-start(bf16[128,8192]{1,0:T(8,128)(2,1)} %param.11) | copy-start | bytes 6291460
  32.4 82.9 %copy-start.2 = (bf16[1,256,512]{2,1,0:T(8,128)(2,1)S(1)}, bf16[1,256,512]{2,1,0:T(8,128)(2,1)}, u32[]{:S(2)}) copy-start(bf16[1,256,512]{2,1,0:T(8,128)(2,1)} %param.16) | copy-start | bytes 786436
  32.4 80.4 %all-to-all-start = ((bf16[32,132,256]{2,1,0:T(8,128)(2,1)}), bf16[32,132,256]{2,1,0:T(8,128)(2,1)S(1)}, u32[]{:S(2)}, u32[]{:S(2)}) async-start(bf16[32,132,256]{2,1,0:T(8,128)(2,1)} %copy.114), calls=%async_computation | async-start | bytes 4456448 | tf_op jit(solution)/shard_map/all_to_all | solution.py:116
  118.8 2.1 %copy-start.1 = (bf16[32,128,256]{2,1,0:T(8,128)(2,1)S(1)}, bf16[32,128,256]{2,1,0:T(8,128)(2,1)}, u32[]{:S(2)}) copy-start(bf16[32,128,256]{2,1,0:T(8,128)(2,1)} %slice.56) | copy-start | bytes 6291460
  144.6 31.4 %copy-start.5 = (f32[1,256]{1,0:T(1,128)S(1)}, f32[1,256]{1,0:T(1,128)}, u32[]{:S(2)}) copy-start(f32[1,256]{1,0:T(1,128)} %param.20) | copy-start | bytes 3076
  144.6 31.4 %copy-start.6 = (f32[1,256]{1,0:T(1,128)S(1)}, f32[1,256]{1,0:T(1,128)}, u32[]{:S(2)}) copy-start(f32[1,256]{1,0:T(1,128)} %param.21) | copy-start | bytes 3076
  144.7 31.9 %copy-start.3 = (f32[256,32]{0,1:T(8,128)S(1)}, f32[256,32]{0,1:T(8,128)}, u32[]{:S(2)}) copy-start(f32[256,32]{0,1:T(8,128)} %param.18) | copy-start | bytes 98308
  144.7 31.9 %copy-start.4 = (f32[256,32]{0,1:T(8,128)S(1)}, f32[256,32]{0,1:T(8,128)}, u32[]{:S(2)}) copy-start(f32[256,32]{0,1:T(8,128)} %param.19) | copy-start | bytes 98308
Sparse Core Ops, SparseCore 0:
  16.7 98.5 all-gather.1

commit v10 on v8

--- a/solution.py
+++ b/solution.py
@@ -137,7 +137,7 @@
         jnp.dot(all_values, weight_rows.T, preferred_element_type=jnp.float32) * weight_scale
     )
     gain_grad = jnp.dot(
-        lang_table.astype(jnp.float32), standard * input_grad, precision=lax.Precision.HIGHEST
+        lang_table.astype(jnp.float32), standard * input_grad, precision=lax.Precision.HIGH
     )
     wv_grad = jnp.dot(normed.T, all_values, preferred_element_type=jnp.float32) * weight_scale
     partial = jnp.stack([jnp.sum(wv_grad * wv_grad), jnp.sum(gain_grad * gain_grad)])

time: 185 us -> 184 us (level)
  no operation moved by 1% of the time
where the time goes in v10:
time: 184 us
  waiting for transfers between devices  70.4 us (38%)
  blocking collectives  41.9 us (23%)
  local copies, waits for them, and re-layouts  20 us (11%)
  between operations  15.7 us (9%)
  matrix products  15.3 us (8%)
  starting transfers between devices  10.7 us (6%)
  other arithmetic  9.6 us (5%)
    all_to_all x1, waiting for transfers between devices, body(): lax.all_to_all(outgoing, 'fsdp', split_axis=1, concat_axis=0, tiled=True)  69.9 us
    all_to_all x1, blocking collectives, body(): lax.all_to_all(packed, 'island', split_axis=0, concat_axis=0, tiled=True)  26.5 us
    all_to_all x1, blocking collectives, body(): lax.all_to_all(jnp.broadcast_to(partial, (fsdp_count, 2)), 'fsdp', split_...  15.4 us
    all_to_all x1, starting transfers between devices, body(): lax.all_to_all(outgoing, 'fsdp', split_axis=1, concat_axis=0, tiled=True)  10.7 us
    dot_general x1, matrix products, body(): jnp.dot(normed.T, all_values, preferred_element_type=jnp.float32)  5.95 us
    concatenate x1, local copies, waits for them, and re-layouts, body(): jnp.concatenate([block_input.reshape(rows, fsdp_count, col_block), extra]...  5.63 us
    unnamed x25, local copies, waits for them, and re-layouts  5.54 us
    concatenate x1, other arithmetic, body(): jnp.concatenate([block_input.reshape(rows, fsdp_count, col_block), extra]...  4.53 us
  transfers between devices with their start and end apart: 2, of which 2 were waited for; matrix products, arithmetic and copies ran while one was open for 10% of the time, Pallas kernels for 0%

profile of v10, /device:TPU:1, one launch (start us, length us, event | category | flops | bytes accessed | tf_op | source)
XLA Modules:
  0.0 183.6 jit_solution(2264684344549656586)
XLA Ops:
  7.2 1.4 copy.135
  8.7 0.9 reshape.123
  9.6 1.6 copy.130
  11.3 2.3 %fusion.45 = (f32[4,8,128]{2,1,0:T(8,128)S(1)}, f32[4,8,128,128]{2,3,1,0:T(8,128)}) fusion(pred[128,128]{0,1:T(8,128)(4,1)S(1)} %iota_compare_fusion.4, bf16[128,4,8,128]{3,2,1,0:T(8,128)(2,1)S(1)} %bitcast.66, bf16[128,4,128,1]{2,1,0,3:T(4,128)(2,1)S(1)} %bitcast.69), kind=kOutput, calls=%fused_computation.69 | convolution fusion | flops 136315008 | bytes 3309568 | tf_op jit(solution)/shard_map/sub | solution.py:37
  13.6 2.2 %fusion.8 = bf16[4,128,128]{1,2,0:T(8,128)(2,1)S(1)} fusion(bf16[128,4,8,128]{0,3,2,1:T(8,128)(2,1)S(1)} %bitcast.65, f32[4,8,128,128]{2,3,1,0:T(8,128)} %get-tuple-element.45, f32[4,8,128]{2,1,0:T(8,128)S(1)} %get-tuple-element.44), kind=kOutput, calls=%fused_computation.18 | convolution fusion | flops 135331840 | bytes 3293184 | tf_op jit(solution)/shard_map/kgts,tkgd->skd/dot_general | solution.py:40
  15.8 0.8 copy.119
  16.6 2.5 %copy.112 = bf16[128,8192]{0,1:T(8,128)(2,1)} copy(bf16[128,8192]{1,0:T(8,128)(2,1)S(1)} %copy-done) | data formatting | bytes 4194304 | tf_op args[0]
  19.1 0.4 convert_reduce_fusion
  19.5 0.2 dynamic-update-slice
  20.1 0.7 fusion.4
  21.8 0.5 broadcast_in_dim.30
  22.2 4.5 %pad_maximum_fusion = bf16[132,32,256]{0,2,1:T(8,128)(2,1)} fusion(bf16[4,32,256]{0,2,1:T(8,128)(2,1)S(1)} %broadcast_in_dim.30, bf16[128,32,256]{0,2,1:T(8,128)(2,1)} %bitcast.60), kind=kLoop, calls=%fused_computation.9 | loop fusion | flops 4325376 | bytes 4325376 | tf_op jit(solution)/shard_map/concatenate | solution.py:114
  26.8 5.6 %copy.114 = bf16[132,32,256]{2,0,1:T(8,128)(2,1)} copy(bf16[132,32,256]{0,2,1:T(8,128)(2,1)} %pad_maximum_fusion) | data formatting | bytes 4325376 | tf_op jit(solution)/shard_map/concatenate | solution.py:114
  32.4 10.7 %all-to-all-start = ((bf16[132,32,256]{2,0,1:T(8,128)(2,1)}), bf16[132,32,256]{2,0,1:T(8,128)(2,1)S(1)}, u32[]{:S(2)}, u32[]{:S(2)}) async-start(bf16[132,32,256]{2,0,1:T(8,128)(2,1)} %copy.114), calls=%async_computation | async-start | bytes 4456448 | tf_op jit(solution)/shard_map/all_to_all | solution.py:115
  43.1 69.9 %all-to-all-done = bf16[132,32,256]{2,0,1:T(8,128)(2,1)S(1)} async-done(((bf16[132,32,256]{2,0,1:T(8,128)(2,1)}), bf16[132,32,256]{2,0,1:T(8,128)(2,1)S(1)}, u32[]{:S(2)}, u32[]{:S(2)}) %all-to-all-start) | async-done | bytes 2162720 | tf_op jit(solution)/shard_map/all_to_all | solution.py:115
  113.0 1.6 slice.56
  114.7 0.5 all-gather.2.cloned.1.call-done
  115.2 3.6 %fusion.1 = f32[4096,256]{1,0:T(8,128)S(1)} fusion(bf16[4096,512]{1,0:T(8,128)(2,1)} %bitcast.77, bf16[4096,256]{1,0:T(8,128)(2,1)} %bitcast.62, f32[4096]{0:T(1024)S(1)} %bitcast.75, f32[4096]{0:T(1024)S(1)} %bitcast.73, bf16[1,256,512]{2,1,0:T(8,128)(2,1)S(1)} %copy-done.2), kind=kOutput, calls=%fused_computation.2 | convolution fusion | flops 1078984704 | bytes 10780672 | tf_op jit(solution)/shard_map/dot_general | solution.py:137
  118.8 1.3 multiply_reduce_fusion.1
  120.1 0.3 copy-done.1
  120.4 5.9 %multiply_reduce_fusion = (f32[]{:T(128)}, f32[256,512]{1,0:T(8,128)S(1)}) fusion(bf16[4096,512]{1,0:T(8,128)(2,1)} %bitcast.78, bf16[4096,256]{1,0:T(8,128)(2,1)S(1)} %bitcast.63, f32[4096]{0:T(1024)S(1)} %bitcast.76, f32[4096]{0:T(1024)S(1)} %bitcast.74, s32[4096]{0:T(1024)S(1)} %bitcast.72, bf16[1,16,8192]{2,1,0:T(8,128)(2,1)} %param.17, s32[]{:T(128)S(6)} %select_n.7), kind=kOutput, calls=%fused_computation.26 | convolution fusion | flops 1112997888 | bytes 6873096 | tf_op jit(solution)/shard_map/dot_general | solution.py:142
  126.3 1.4 pad_maximum_fusion.1
  127.7 15.4 %all_to_all.30 = f32[32,1,2]{2,1,0:T(1,128)S(1)} all-to-all(f32[32,1,2]{2,1,0:T(1,128)S(1)} %broadcast_in_dim.33), channel_id=1, replica_groups=mesh['island'=16,'fsdp'=32] {'fsdp'}, dimensions={0} | all-to-all | bytes 512 | tf_op jit(solution)/shard_map/all_to_all | solution.py:144
  143.1 0.6 fusion.44
  144.7 0.6 copy.122
  145.4 1.0 reshape.128
  147.0 0.7 multiply_subtract_fusion.2
  147.8 0.6 copy.123
  148.3 26.5 %all_to_all.31 = f32[16,1,8448]{2,1,0:T(1,128)S(1)} all-to-all(f32[16,1,8448]{2,1,0:T(1,128)S(1)} %copy.123), channel_id=1, replica_groups=mesh['island'=16,'fsdp'=32] {'island'}, dimensions={0} | all-to-all | bytes 1081344 | tf_op jit(solution)/shard_map/all_to_all | solution.py:160
  174.8 0.3 reduce_sum.69
  175.5 0.6 multiply_subtract_fusion.3
  176.1 0.6 multiply_subtract_fusion.1
  (45 shorter events, 2.3 us)
Async XLA Ops:
  7.2 108.0 %all-gather.2.cloned.1.call-start = ((), (), s32[]{:S(2)}) async-start(), calls=%async_computation.3 | async-start | bytes 4325376 | tf_op jit(solution)/shard_map/all_gather | solution.py:125
  13.6 3.0 %copy-start.7 = (s32[128]{0:T(128)S(1)}, s32[128]{0:T(128)}, u32[]{:S(2)}) copy-start(s32[128]{0:T(128)} %param.12) | copy-start | bytes 1540
  13.6 3.0 %copy-start = (bf16[128,8192]{1,0:T(8,128)(2,1)S(1)}, bf16[128,8192]{1,0:T(8,128)(2,1)}, u32[]{:S(2)}) copy-start(bf16[128,8192]{1,0:T(8,128)(2,1)} %param.11) | copy-start | bytes 6291460
  32.4 82.8 %copy-start.2 = (bf16[1,256,512]{2,1,0:T(8,128)(2,1)S(1)}, bf16[1,256,512]{2,1,0:T(8,128)(2,1)}, u32[]{:S(2)}) copy-start(bf16[1,256,512]{2,1,0:T(8,128)(2,1)} %param.16) | copy-start | bytes 786436
  32.4 80.5 %all-to-all-start = ((bf16[132,32,256]{2,0,1:T(8,128)(2,1)}), bf16[132,32,256]{2,0,1:T(8,128)(2,1)S(1)}, u32[]{:S(2)}, u32[]{:S(2)}) async-start(bf16[132,32,256]{2,0,1:T(8,128)(2,1)} %copy.114), calls=%async_computation | async-start | bytes 4456448 | tf_op jit(solution)/shard_map/all_to_all | solution.py:115
  118.8 1.6 copy-start.1
  144.7 30.8 %copy-start.5 = (f32[1,256]{1,0:T(1,128)S(1)}, f32[1,256]{1,0:T(1,128)}, u32[]{:S(2)}) copy-start(f32[1,256]{1,0:T(1,128)} %param.20) | copy-start | bytes 3076
  144.7 30.8 %copy-start.6 = (f32[1,256]{1,0:T(1,128)S(1)}, f32[1,256]{1,0:T(1,128)}, u32[]{:S(2)}) copy-start(f32[1,256]{1,0:T(1,128)} %param.21) | copy-start | bytes 3076
  144.7 31.4 %copy-start.3 = (f32[256,32]{0,1:T(8,128)S(1)}, f32[256,32]{0,1:T(8,128)}, u32[]{:S(2)}) copy-start(f32[256,32]{0,1:T(8,128)} %param.18) | copy-start | bytes 98308
  144.7 31.3 %copy-start.4 = (f32[256,32]{0,1:T(8,128)S(1)}, f32[256,32]{0,1:T(8,128)}, u32[]{:S(2)}) copy-start(f32[256,32]{0,1:T(8,128)} %param.19) | copy-start | bytes 98308
Sparse Core Ops, SparseCore 0:
  16.7 98.4 all-gather.1
